TPU v7x, 128 devices: a whole 4x4x4 slice. The times are simulated.
128 devices in a mesh: dp: 4 (over z), ep: 32 (over y, x, core).
Axes of the slice: x: 4, y: 4, z: 4, core: 2. Of those that a mesh axis runs over, the one named last changes fastest.
Arguments:
- queries: bfloat16 [2048, 2, 8192], P(('dp', 'ep')), may hold values from -150 to 150
- keys_new: bfloat16 [2048, 2, 512], P(('dp', 'ep')), may hold values from -5 to 5
- values_new: bfloat16 [2048, 2, 512], P(('dp', 'ep')), may hold values from -5 to 5
- importance: float32 [2048, 2, 4], P(('dp', 'ep')), may hold values from 0.25 to 4
- merge_flags: int32 [2048, 2, 4], P(('dp', 'ep')), may hold values 0 or 1
- key_cache: bfloat16 [2048, 512, 512], P(('dp', 'ep')), may hold values from -5.1 to 5.1
- value_cache: bfloat16 [2048, 512, 512], P(('dp', 'ep')), may hold values from -5 to 5
- last_weight: float32 [2048, 4], P(('dp', 'ep')), may hold values from 0.5 to 8
- lengths: int32 [2048], P(('dp', 'ep')), may hold values from 2 to 510, as said below
- residual: bfloat16 [2048, 2, 2048], P(('dp', 'ep')), may hold values from -6 to 6
- o_weight: bfloat16 [8192, 2048], P('ep'), may hold values from -0.0625 to 0.0625
- norm_gain: float32 [2048], replicated, may hold values from 0.5 to 1.5
- expert_gate_up: bfloat16 [128, 2048, 1536], P(('dp', 'ep')), may hold values from -0.125 to 0.125
- expert_down: bfloat16 [128, 768, 2048], P(('dp', 'ep')), may hold values from -0.21875 to 0.21875
- routes: int32 [2048, 2, 8], P(('dp', 'ep')), may hold values from 0 to 127, all different within a row; in each aligned block of 32 rows (0 to 31, 32 to 63, ..., all dimensions but the last counted through in order) at most 4 rows name the same one
- route_weights: float32 [2048, 2, 8], P(('dp', 'ep')), may hold values from 0.05 to 0.5
Outputs:
- attended: bfloat16 [2048, 2, 8192], P(('dp', 'ep'))
- layer_out: bfloat16 [2048, 2, 2048], P(('dp', 'ep'))
Inputs may be any that keep to these rules, and one draw needn't show every extreme that they name: `lengths`: the largest length is 510 in every draw. `routes`: each token names 8 different experts; among the rows of one device (32 tokens) no expert is named more than 4 times, a bound that some block reaches.
All inputs are finite; a program needn't handle non-finite values. No bound on the sum of `merge_flags` on one device may be relied on, other than what follows from the above.
Results may differ from a plain program's by a relative error of at most 0.018.
Values may be sent and summed in bfloat16 or wider, within the bound.
No kernel may reach another device: no remote copies, remote signals or barrier semaphores. Data moves between devices by JAX's collectives and lax.ppermute only.
A program may use at most 128 MiB of HBM per device.

v0:
```python
import math

import jax
import jax.numpy as jnp
from jax import lax
from jax.sharding import PartitionSpec as P

EPS = 1e-06


def build_tail(
    key_cache,
    value_cache,
    lengths,
    keys_new,
    values_new,
    importance,
    merge_flags,
    last_weight,
    heads_kv,
):
    requests, steps, features = keys_new.shape
    head_dim = features // heads_kv
    last_slot = lengths - 1

    def take_slot(cache_rows, position):
        return lax.dynamic_slice_in_dim(cache_rows, position, 1, 0)

    first_keys = jax.vmap(take_slot)(key_cache, last_slot)
    first_values = jax.vmap(take_slot)(value_cache, last_slot)
    blank = jnp.zeros((requests, steps, features), jnp.bfloat16)
    tail_keys = jnp.concatenate([first_keys, blank], axis=1).reshape(
        requests, steps + 1, heads_kv, head_dim
    )
    tail_values = jnp.concatenate([first_values, blank], axis=1).reshape(
        requests, steps + 1, heads_kv, head_dim
    )
    filled = jnp.ones((requests, heads_kv), jnp.int32)
    weight = last_weight
    positions = jnp.arange(steps + 1, dtype=jnp.int32)
    live_counts = []
    key_states = []
    value_states = []
    for step in range(steps):
        merging = merge_flags[:, step] == 1
        portion = importance[:, step]
        target = jnp.where(merging, filled - 1, filled)
        picked = positions[None, :, None] == target[:, None, :]

        def settle(tail, fresh):
            fresh = fresh.reshape(requests, heads_kv, head_dim).astype(jnp.float32)
            former = jnp.sum(jnp.where(picked[..., None], tail.astype(jnp.float32), 0.0), axis=1)
            blended = (weight[..., None] * former + portion[..., None] * fresh) / (
                weight + portion
            )[..., None]
            new_row = jnp.where(merging[..., None], blended, fresh).astype(jnp.bfloat16)
            return jnp.where(picked[..., None], new_row[:, None], tail)

        tail_keys = settle(tail_keys, keys_new[:, step])
        tail_values = settle(tail_values, values_new[:, step])
        weight = jnp.where(merging, weight + portion, portion)
        filled = jnp.where(merging, filled, filled + 1)
        live_counts.append(filled)
        key_states.append(tail_keys)
        value_states.append(tail_values)
    return (
        jnp.stack(key_states, axis=1),
        jnp.stack(value_states, axis=1),
        jnp.stack(live_counts, axis=2),
    )


def first_pass(keys, queries, slot_order, limits, block, scale):
    requests, slots = (keys.shape[0], keys.shape[1])
    heads_kv, rows = (queries.shape[1], queries.shape[2])
    usable = jnp.sum((slot_order[None, :] < limits[:, None]).astype(jnp.int32), axis=1)
    blocks = (jnp.max(usable) + block - 1) // block
    initial = jnp.full((requests, heads_kv, rows, slots), -jnp.inf, jnp.float32)

    def first_advance(index, buffer):
        start = index * block
        key_block = lax.dynamic_slice_in_dim(keys, start, block, 1)
        scores = (
            jnp.einsum("ngqd,nkgd->ngqk", queries, key_block, preferred_element_type=jnp.float32)
            * scale
        )
        order_block = lax.dynamic_slice_in_dim(slot_order, start, block, 0)
        valid = order_block[None, :] < limits[:, None]
        scores = jnp.where(valid[:, None, None, :], scores, -jnp.inf)
        return lax.dynamic_update_slice_in_dim(buffer, scores, start, 3)

    return (lax.fori_loop(0, blocks, first_advance, initial), blocks)


def second_pass(values, buffer, highest, blocks, block):
    requests, heads_kv, rows = (buffer.shape[0], buffer.shape[1], buffer.shape[2])
    head_dim = values.shape[3]

    def second_advance(index, carry):
        summed, totals = carry
        start = index * block
        scores = lax.dynamic_slice_in_dim(buffer, start, block, 3)
        raw = jnp.exp(scores - highest[..., None])
        totals = totals + jnp.sum(raw, axis=3)
        value_block = lax.dynamic_slice_in_dim(values, start, block, 1)
        summed = summed + jnp.einsum(
            "ngqk,nkgd->ngqd",
            raw.astype(jnp.bfloat16),
            value_block,
            preferred_element_type=jnp.float32,
        )
        return (summed, totals)

    initial = (
        jnp.zeros((requests, heads_kv, rows, head_dim), jnp.float32),
        jnp.zeros((requests, heads_kv, rows), jnp.float32),
    )
    return lax.fori_loop(0, blocks, second_advance, initial)


def run_experts(arriving, expert_gate_up, expert_down):
    hidden_units = expert_down.shape[1]
    both = jnp.einsum(
        "sjcd,jdf->sjcf", arriving, expert_gate_up, preferred_element_type=jnp.float32
    )
    active = (jax.nn.silu(both[..., :hidden_units]) * both[..., hidden_units:]).astype(jnp.bfloat16)
    return jnp.einsum(
        "sjcf,jfd->sjcd", active, expert_down, preferred_element_type=jnp.float32
    ).astype(jnp.bfloat16)


def shards(
    queries,
    keys_new,
    values_new,
    importance,
    merge_flags,
    key_cache,
    value_cache,
    last_weight,
    lengths,
    residual,
    o_weight,
    norm_gain,
    expert_gate_up,
    expert_down,
    routes,
    route_weights,
):
    heads_kv = last_weight.shape[1]
    requests, steps, query_width = queries.shape
    features = keys_new.shape[2]
    head_dim = features // heads_kv
    heads_query = query_width // head_dim
    group = heads_query // heads_kv
    slots_all = key_cache.shape[1]
    scale = 1.0 / math.sqrt(head_dim)
    tail_keys, tail_values, live = build_tail(
        key_cache,
        value_cache,
        lengths,
        keys_new,
        values_new,
        importance,
        merge_flags,
        last_weight,
        heads_kv,
    )
    grouped = (
        queries.reshape(requests, steps, heads_kv, group, head_dim)
        .transpose(0, 2, 1, 3, 4)
        .reshape(requests, heads_kv, steps * group, head_dim)
    )
    per_step = grouped.reshape(requests, heads_kv, steps, group, head_dim)
    tail_scores = (
        jnp.einsum("ngtqd,ntsgd->ngtqs", per_step, tail_keys, preferred_element_type=jnp.float32)
        * scale
    )
    tail_scores = tail_scores.reshape(requests, heads_kv, steps * group, steps + 1)
    live_rows = jnp.repeat(live, group, axis=2)
    tail_valid = jnp.arange(steps + 1, dtype=jnp.int32)[None, None, None, :] < live_rows[..., None]
    tail_scores = jnp.where(tail_valid, tail_scores, -jnp.inf)
    tail_highest = jnp.max(tail_scores, axis=3)
    limits = lengths - 1
    keys_grid = key_cache.reshape(requests, slots_all, heads_kv, head_dim)
    values_grid = value_cache.reshape(requests, slots_all, heads_kv, head_dim)
    block = math.gcd(slots_all, 256)
    slot_order = jnp.arange(slots_all, dtype=jnp.int32)
    buffer, blocks = first_pass(keys_grid, grouped, slot_order, limits, block, scale)
    highest = jnp.maximum(jnp.max(buffer, axis=3), tail_highest)
    summed, totals = second_pass(values_grid, buffer, highest, blocks, block)
    tail_raw = jnp.exp(tail_scores - highest[..., None])
    totals = totals + jnp.sum(tail_raw, axis=3)
    tail_weights = tail_raw.astype(jnp.bfloat16).reshape(
        requests, heads_kv, steps, group, steps + 1
    )
    tail_sums = jnp.einsum(
        "ngtqs,ntsgd->ngtqd", tail_weights, tail_values, preferred_element_type=jnp.float32
    )
    summed = summed + tail_sums.reshape(requests, heads_kv, steps * group, head_dim)
    attended = (summed / totals[..., None]).astype(jnp.bfloat16)
    attended = (
        attended.reshape(requests, heads_kv, steps, group, head_dim)
        .transpose(0, 2, 1, 3, 4)
        .reshape(requests, steps, query_width)
    )
    members = lax.axis_size("ep")
    rows = requests * steps
    spread = lax.all_to_all(
        attended.reshape(rows, members, query_width // members),
        "ep",
        split_axis=1,
        concat_axis=0,
        tiled=True,
    )
    spread = spread.reshape(members * rows, query_width // members)
    projected = lax.psum_scatter(
        jnp.dot(spread, o_weight, preferred_element_type=jnp.float32),
        "ep",
        scatter_dimension=0,
        tiled=True,
    )
    width = o_weight.shape[1]
    mixed = residual.reshape(rows, width).astype(jnp.float32) + projected
    normed = (
        mixed * lax.rsqrt(jnp.mean(mixed * mixed, axis=1, keepdims=True) + EPS) * norm_gain
    ).astype(jnp.bfloat16)
    experts_local = expert_gate_up.shape[0]
    dp_size = lax.axis_size("dp")
    experts_all = experts_local * dp_size * members
    top_k = routes.shape[2]
    capacity = max(2, 2 * rows * top_k // experts_all)
    chosen = routes.reshape(rows * top_k)
    sequence = jnp.arange(rows * top_k, dtype=jnp.int32)
    earlier = sequence[:, None] > sequence[None, :]
    rank = jnp.sum(((chosen[:, None] == chosen[None, :]) & earlier).astype(jnp.int32), axis=1)
    target = chosen * capacity + rank
    placing = (
        jnp.arange(experts_all * capacity, dtype=jnp.int32)[:, None] == target[None, :]
    ).reshape(experts_all * capacity, rows, top_k)
    placing = jnp.any(placing, axis=2).astype(jnp.bfloat16)
    outgoing = jnp.dot(placing, normed, preferred_element_type=jnp.float32).astype(jnp.bfloat16)
    arrived = lax.all_to_all(
        outgoing.reshape(experts_all, capacity, width),
        ("dp", "ep"),
        split_axis=0,
        concat_axis=0,
        tiled=True,
    )
    depth = arrived.shape[1]
    sources = arrived.shape[0] // experts_local
    answer = run_experts(
        arrived.reshape(sources, experts_local, depth, width), expert_gate_up, expert_down
    )
    returned = lax.all_to_all(
        answer.reshape(sources * experts_local, depth, width),
        ("dp", "ep"),
        split_axis=0,
        concat_axis=0,
        tiled=True,
    )
    results = returned.reshape(experts_all * capacity, width)[target].reshape(rows, top_k, width)
    blended = jnp.sum(route_weights.reshape(rows, top_k, 1) * results.astype(jnp.float32), axis=1)
    layer_out = (mixed + blended).astype(jnp.bfloat16).reshape(requests, steps, width)
    return (attended, layer_out)


def solution(mesh):
    return jax.shard_map(
        shards,
        mesh=mesh,
        in_specs=(
            P(("dp", "ep"), None, None),
            P(("dp", "ep"), None, None),
            P(("dp", "ep"), None, None),
            P(("dp", "ep"), None, None),
            P(("dp", "ep"), None, None),
            P(("dp", "ep"), None, None),
            P(("dp", "ep"), None, None),
            P(("dp", "ep"), None),
            P(("dp", "ep")),
            P(("dp", "ep"), None, None),
            P("ep", None),
            P(),
            P(("dp", "ep"), None, None),
            P(("dp", "ep"), None, None),
            P(("dp", "ep"), None, None),
            P(("dp", "ep"), None, None),
        ),
        out_specs=(P(("dp", "ep"), None, None), P(("dp", "ep"), None, None)),
        check_vma=False,
    )
```

profile of v0, /device:TPU:1, one launch (start us, length us, event | category | flops | bytes accessed | tf_op | source)
XLA Modules:
  0.0 341.7 jit_solution(7338408195934166069)
XLA Ops:
  7.2 1.4 select_bitcast_fusion
  8.6 1.2 add_select_fusion
  9.9 1.3 slice_bitcast_fusion
  11.2 1.3 fusion.66
  12.5 0.8 copy.130
  16.0 12.3 %copy.124 = bf16[16,512,512]{1,2,0:T(8,128)(2,1)} copy(bf16[16,512,512]{2,1,0:T(8,128)(2,1)} %param.25) | data formatting | bytes 16777216 | tf_op args[5]
  28.4 1.5 gather_fusion.1
  29.8 1.5 gather_fusion.2
  31.3 12.3 %copy.142 = bf16[16,512,512]{1,2,0:T(8,128)(2,1)} copy(bf16[16,512,512]{2,1,0:T(8,128)(2,1)} %param.26) | data formatting | bytes 16777216 | tf_op args[6]
  47.4 0.7 slice_convert_fusion
  48.1 0.8 div.81
  48.9 0.8 broadcast_in_dim.176
  49.6 0.8 mul.189
  50.5 0.8 select_reduce_fusion
  51.9 1.3 copy.138
  53.3 1.3 copy.141
  54.6 1.2 copy.137
  55.8 1.3 copy.140
  59.2 2.2 reshape.374
  61.5 1.9 copy.125
  63.4 2.5 broadcast_in_dim.174
  65.8 9.2 %while.22 = (s32[]{:T(128)}, f32[16,4,32,512]{3,2,1,0:T(8,128)}, s32[]{:T(128)}, s32[512]{0:T(512)S(1)}, s32[16]{0:T(128)S(1)}, /*index=5*/bf16[16,512,4,128]{1,...) while((s32[]{:T(128)}, f32[16,4,32,512]{3,2,1,0:T(8,128)}, ...), condition=%wide.region_3.4_spmd, body=%wide.region_2.3_spmd.sunk | while | flops 135270400 | bytes 6828255 | solution.py:92
  66.0 4.5 %bitcast_dynamic-update-slice_fusion.2 = f32[16,4,32,512]{3,2,1,0:T(8,128)} fusion(f32[16,4,32,512]{3,2,1,0:T(8,128)} %get-tuple-element.305, s32[]{:T(128)S(6)} %select_n.274, bf16[16,4,32,128]{3,2,1,0:T(8,128)(2,1)} %get-tuple-element.321, bf16[16,512,4,128]{1,3,2,0:T(8,128)(2,1)} %get-tuple-element.320, ...), kind=kOutput, calls=%fused_computation.5.clone.1 | convolution fusion | flops 135266304 | bytes 6820864 | tf_op jit(solution)/shard_map/while/body/ngqd,nkgd->ngqk/dot_general | solution.py:84
  70.6 4.4 %bitcast_dynamic-update-slice_fusion.2 = f32[16,4,32,512]{3,2,1,0:T(8,128)} fusion(f32[16,4,32,512]{3,2,1,0:T(8,128)} %get-tuple-element.305, s32[]{:T(128)S(6)} %select_n.274, bf16[16,4,32,128]{3,2,1,0:T(8,128)(2,1)} %get-tuple-element.321, bf16[16,512,4,128]{1,3,2,0:T(8,128)(2,1)} %get-tuple-element.320, ...), kind=kOutput, calls=%fused_computation.5.clone.1 | convolution fusion | flops 135266304 | bytes 6820864 | tf_op jit(solution)/shard_map/while/body/ngqd,nkgd->ngqk/dot_general | solution.py:84
  75.1 2.6 reduce_max.32
  77.6 0.7 reduce_max.35
  78.4 0.9 fusion.58
  79.3 0.9 fusion.59
  80.2 0.9 broadcast_select_fusion
  81.0 1.5 fusion.71
  83.2 0.7 reduce_max.34
  83.9 0.9 max.10
  84.8 0.9 fusion.37
  85.7 1.5 reduce_sum.114
  87.2 0.8 max.9
  88.0 1.2 broadcast_in_dim.172
  89.2 13.3 %while.23 = (s32[]{:T(128)}, f32[16,4,32,128]{3,2,1,0:T(8,128)}, f32[16,4,32]{2,1,0:T(4,128)S(1)}, s32[]{:T(128)}, f32[16,4,32,512]{3,2,1,0:T(8,128)}, /*index=5...) while((s32[]{:T(128)}, f32[16,4,32,128]{3,2,1,0:T(8,128)}, ...), condition=%wide.region_10.11_spmd, body=%wide.region_8.10_spmd.sunk | while | flops 136577024 | bytes 27313340 | solution.py:118
  89.2 5.9 %fusion.87 = f32[16,4,32,128]{3,2,1,0:T(8,128)} fusion(f32[16,4,32,128]{3,2,1,0:T(8,128)} %get-tuple-element.338, bf16[16,512,4,128]{1,3,2,0:T(8,128)(2,1)} %get-tuple-element.354, s32[]{:T(128)S(6)} %select_n.275, f32[16,4,32,512]{3,2,1,0:T(8,128)} %get-tuple-element.352, f32[16,4,32]{2,1,0:T(4,128)S(1)} %get-tuple-element.353), kind=kOutput, calls=%fused_computation.13.clone.1 | convolution fusion | flops 135528448 | bytes 8397824 | tf_op jit(solution)/shard_map/while/body/ngqk,nkgd->ngqd/dot_general | solution.py:106
  95.9 5.9 %fusion.87 = f32[16,4,32,128]{3,2,1,0:T(8,128)} fusion(f32[16,4,32,128]{3,2,1,0:T(8,128)} %get-tuple-element.338, bf16[16,512,4,128]{1,3,2,0:T(8,128)(2,1)} %get-tuple-element.354, s32[]{:T(128)S(6)} %select_n.275, f32[16,4,32,512]{3,2,1,0:T(8,128)} %get-tuple-element.352, f32[16,4,32]{2,1,0:T(4,128)S(1)} %get-tuple-element.353), kind=kOutput, calls=%fused_computation.13.clone.1 | convolution fusion | flops 135528448 | bytes 8397824 | tf_op jit(solution)/shard_map/while/body/ngqk,nkgd->ngqd/dot_general | solution.py:106
  102.5 0.8 add.170
  103.3 1.3 fusion.39
  104.5 1.6 fusion.31
  106.1 0.9 copy.189
  107.0 2.0 reshape_reshape.3
  109.0 1.3 copy.147
  110.4 19.9 %all_to_all.25 = bf16[32,32,256]{2,0,1:T(8,128)(2,1)S(1)} all-to-all(bf16[32,32,256]{2,0,1:T(8,128)(2,1)S(1)} %copy.147), channel_id=1, replica_groups=mesh['dp'=4,'ep'=32] {'ep'}, dimensions={1} | all-to-all | bytes 1048576 | tf_op jit(solution)/shard_map/all_to_all | solution.py:209
  130.3 5.7 %fusion.72 = f32[1024,2048]{1,0:T(8,128)} fusion(bf16[1024,256]{1,0:T(8,128)(2,1)S(1)} %bitcast.163, bf16[256,2048]{1,0:T(8,128)(2,1)} %param.30), kind=kOutput, calls=%fused_computation.124 | convolution fusion | flops 1073741824 | bytes 9961472 | tf_op jit(solution)/shard_map/dot_general | solution.py:218
  136.0 0.9 copy-done.3
  136.9 0.7 reshape.395
  138.5 87.1 %reduce-scatter.2.cloned.1.call-done = f32[32,2048]{1,0:T(8,128)} async-done(((f32[1024,2048]{1,0:T(8,128)}), f32[32,2048]{1,0:T(8,128)}) %reduce-scatter.2.cloned.1.call-update) | async-done | bytes 262160 | tf_op jit(solution)/shard_map/reduce_scatter | solution.py:217
  225.6 1.2 multiply_reduce_fusion
  226.8 2.1 convolution_convert_fusion
  228.9 4.1 %reshape.383 = bf16[128,4,2048]{2,1,0:T(4,128)(2,1)} reshape(bf16[512,2048]{1,0:T(8,128)(2,1)} %convolution_convert_fusion) | data formatting | bytes 4194304 | tf_op jit(solution)/shard_map/reshape | solution.py:244
  233.0 39.9 %all_to_all.26 = bf16[128,4,2048]{2,1,0:T(4,128)(2,1)S(1)} all-to-all(bf16[128,4,2048]{2,1,0:T(4,128)(2,1)} %reshape.383), channel_id=1, replica_groups=mesh['dp'=4,'ep'=32] {'dp','ep'}, dimensions={0} | all-to-all | bytes 4194304 | tf_op jit(solution)/shard_map/all_to_all | solution.py:243
  272.9 9.1 %fusion.17 = f32[128,1,4,1536]{3,0,2,1:T(8,128)S(1)} fusion(bf16[1,2048,1536]{2,1,0:T(8,128)(2,1)} %param.32, bf16[128,4,2048]{2,1,0:T(4,128)(2,1)S(1)} %all_to_all.26), kind=kOutput, calls=%fused_computation.18 | convolution fusion | flops 3221225472 | bytes 11534336 | tf_op jit(solution)/shard_map/sjcd,jdf->sjcf/dot_general | solution.py:123
  282.1 1.8 fusion.22
  283.9 2.9 copy.152
  286.8 5.6 %all-to-all-start.2 = ((bf16[128,4,2048]{2,1,0:T(4,128)(2,1)}), bf16[128,4,2048]{2,1,0:T(4,128)(2,1)}, u32[]{:S(2)}, u32[]{:S(2)}) async-start(bf16[128,4,2048]{2,1,0:T(4,128)(2,1)} %copy.152), calls=%async_computation.3 | async-start | bytes 4194304 | tf_op jit(solution)/shard_map/all_to_all | solution.py:255
  292.5 2.0 reshape.381
  294.5 28.2 %all-to-all-done.2 = bf16[128,4,2048]{2,1,0:T(4,128)(2,1)} async-done(((bf16[128,4,2048]{2,1,0:T(4,128)(2,1)}), bf16[128,4,2048]{2,1,0:T(4,128)(2,1)}, u32[]{:S(2)}, u32[]{:S(2)}) %all-to-all-start.2) | async-done | bytes 2097184 | tf_op jit(solution)/shard_map/all_to_all | solution.py:255
  322.7 4.0 %reshape.387 = bf16[512,2048]{1,0:T(8,128)(2,1)} reshape(bf16[128,4,2048]{2,1,0:T(4,128)(2,1)} %all-to-all-done.2) | data formatting | bytes 4194304 | tf_op jit(solution)/shard_map/reshape | solution.py:262
  326.7 5.2 %gather_fusion = bf16[256,2048]{1,0:T(8,128)(2,1)} fusion(bf16[512,2048]{1,0:T(8,128)(2,1)} %reshape.387, s32[1024]{0:T(1024)S(1)} %pad_clamp_fusion), kind=kCustom, calls=%fused_computation | custom fusion | bytes 2098176 | tf_op jit(solution)/shard_map/gather | solution.py:262
  331.9 2.2 fusion.25
  334.1 0.8 reshape.388
  (95 shorter events, 12.1 us)
Async XLA Ops:
  7.2 274.9 %copy-start = (bf16[1,768,2048]{2,1,0:T(8,128)(2,1)S(1)}, bf16[1,768,2048]{2,1,0:T(8,128)(2,1)}, u32[]{:S(2)}) copy-start(bf16[1,768,2048]{2,1,0:T(8,128)(2,1)} %param.33) | copy-start | bytes 9437188
  7.2 218.4 %reduce-scatter.2.cloned.1.call-start = ((), (), s32[]{:S(2)}) async-start(), calls=%async_computation.4 | async-start | bytes 8650752 | tf_op jit(solution)/shard_map/reduce_scatter | solution.py:217
  9.9 33.7 %copy-start.16 = (pred[16,1,4]{0,2,1:T(4,128)(4,1)}, pred[16,1,4]{0,2,1:T(4,128)(4,1)S(1)}, u32[]{:S(2)}) copy-start(pred[16,1,4]{0,2,1:T(4,128)(4,1)S(1)} %get-tuple-element.177) | copy-start | bytes 196
  13.2 37.2 %copy-start.10 = (f32[16,4]{1,0:T(8,128)}, f32[16,4]{1,0:T(8,128)S(1)}, u32[]{:S(2)}) copy-start(f32[16,4]{1,0:T(8,128)S(1)} %copy.130) | copy-start | bytes 772
  14.6 13.8 %copy-start.12 = (s32[16]{0:T(128)}, s32[16]{0:T(128)S(1)}, u32[]{:S(2)}) copy-start(s32[16]{0:T(128)S(1)} %broadcast_add_fusion) | copy-start | bytes 196
  31.3 16.1 %copy-start.6 = (bf16[16,2,512]{2,1,0:T(2,128)(2,1)S(1)}, bf16[16,2,512]{2,1,0:T(2,128)(2,1)}, u32[]{:S(2)}) copy-start(bf16[16,2,512]{2,1,0:T(2,128)(2,1)} %param.22) | copy-start | bytes 98308
  31.3 16.1 %copy-start.7 = (bf16[16,2,512]{2,1,0:T(2,128)(2,1)S(1)}, bf16[16,2,512]{2,1,0:T(2,128)(2,1)}, u32[]{:S(2)}) copy-start(bf16[16,2,512]{2,1,0:T(2,128)(2,1)} %param.21) | copy-start | bytes 98308
  59.2 6.6 %copy-start.13 = (s32[16]{0:T(128)S(1)}, s32[16]{0:T(128)}, u32[]{:S(2)}) copy-start(s32[16]{0:T(128)} %copy-done.12) | copy-start | bytes 196
  75.0 3.3 copy-start.5
  75.0 4.2 %copy-start.4 = (f32[16,4,128]{2,1,0:T(4,128)S(1)}, f32[16,4,128]{2,1,0:T(4,128)}, u32[]{:S(2)}) copy-start(f32[16,4,128]{2,1,0:T(4,128)} %reduce_sum.112) | copy-start | bytes 98308
  75.0 4.2 %copy-start.8 = (f32[16,1,512]{2,1,0:T(1,128)S(1)}, f32[16,1,512]{2,1,0:T(1,128)}, u32[]{:S(2)}) copy-start(f32[16,1,512]{2,1,0:T(1,128)} %get-tuple-element.185) | copy-start | bytes 98308
  75.1 4.2 %copy-start.9 = (f32[16,1,512]{2,1,0:T(1,128)S(1)}, f32[16,1,512]{2,1,0:T(1,128)}, u32[]{:S(2)}) copy-start(f32[16,1,512]{2,1,0:T(1,128)} %get-tuple-element.201) | copy-start | bytes 98308
  82.5 0.6 copy-start.2
  89.2 5.9 %copy-start.1 = (f32[16,4,32,512]{3,2,1,0:T(8,128)S(1)}, f32[16,4,32,512]{3,2,1,0:T(8,128)}, u32[]{:S(2)}) copy-start(f32[16,4,32,512]{3,2,1,0:T(8,128)} %get-tuple-element.352) | copy-start | bytes 12582916 | tf_op jit(solution)/shard_map/while
  95.8 5.9 %copy-start.1 = (f32[16,4,32,512]{3,2,1,0:T(8,128)S(1)}, f32[16,4,32,512]{3,2,1,0:T(8,128)}, u32[]{:S(2)}) copy-start(f32[16,4,32,512]{3,2,1,0:T(8,128)} %get-tuple-element.352) | copy-start | bytes 12582916 | tf_op jit(solution)/shard_map/while
  136.0 0.9 copy-start.3
  136.0 1.6 copy-start.11
  136.0 90.8 %copy-start.14 = (f32[2048]{0:T(1024)S(1)}, f32[2048]{0:T(1024)}, u32[]{:S(2)}) copy-start(f32[2048]{0:T(1024)} %param.31) | copy-start | bytes 24580
  286.8 7.6 %copy-start.15 = (f32[16,2,8]{0,2,1:T(8,128)S(1)}, f32[16,2,8]{0,2,1:T(8,128)}, u32[]{:S(2)}) copy-start(f32[16,2,8]{0,2,1:T(8,128)} %param.35) | copy-start | bytes 3076
  286.8 35.9 %all-to-all-start.2 = ((bf16[128,4,2048]{2,1,0:T(4,128)(2,1)}), bf16[128,4,2048]{2,1,0:T(4,128)(2,1)}, u32[]{:S(2)}, u32[]{:S(2)}) async-start(bf16[128,4,2048]{2,1,0:T(4,128)(2,1)} %copy.152), calls=%async_computation.3 | async-start | bytes 4194304 | tf_op jit(solution)/shard_map/all_to_all | solution.py:255
Sparse Core Ops, SparseCore 0:
  136.2 89.3 reduce-scatter.1
where the time goes:
time: 344 us; the launch traced here: 342 us
  waiting for transfers between devices  115 us (33%)
  local copies, waits for them, and re-layouts  79.6 us (23%)
  blocking collectives  59.8 us (17%)
  matrix products  42.2 us (12%)
  other arithmetic  24 us (7%)
  between operations  15 us (4%)
  starting transfers between devices  5.59 us (2%)
    reduce_scatter x1, waiting for transfers between devices, shards(): lax.psum_scatter(jnp.dot(spread, o_weight, preferred_element_type=jnp.flo...  87.1 us
    all_to_all x1, blocking collectives, shards(): lax.all_to_all(outgoing.reshape(experts_all, capacity, width), ('dp', 'ep...  39.9 us
    all_to_all x1, waiting for transfers between devices, shards(): lax.all_to_all(answer.reshape(sources * experts_local, depth, width), ('d...  28.2 us
    unnamed x37, local copies, waits for them, and re-layouts  27.1 us
    all_to_all x1, blocking collectives, shards(): lax.all_to_all(attended.reshape(rows, members, query_width // members), '...  19.9 us
    dot_general x2, matrix products, second_advance(): jnp.einsum('ngqk,nkgd->ngqd', raw.astype(jnp.bfloat16), value_block, pref...  11.8 us
    dot_general x1, matrix products, run_experts(): jnp.einsum('sjcd,jdf->sjcf', arriving, expert_gate_up, preferred_element_...  9.14 us
    dot_general x2, matrix products, first_advance(): jnp.einsum('ngqd,nkgd->ngqk', queries, key_block, preferred_element_type=...  8.92 us
  transfers between devices with their start and end apart: 2, of which 2 were waited for; matrix products, arithmetic and copies ran while one was open for 1% of the time, Pallas kernels for 0%

commit v1 on v0

--- a/solution.py
+++ b/solution.py
@@ -204,23 +204,25 @@
         .transpose(0, 2, 1, 3, 4)
         .reshape(requests, steps, query_width)
     )
-    members = lax.axis_size("ep")
     rows = requests * steps
+    width = o_weight.shape[1]
+    gathered = lax.all_gather(o_weight, ("x", "c"), axis=0, tiled=True)
+    lines = lax.axis_size("y")
     spread = lax.all_to_all(
-        attended.reshape(rows, members, query_width // members),
-        "ep",
+        attended.reshape(rows, lines, query_width // lines),
+        "y",
         split_axis=1,
         concat_axis=0,
         tiled=True,
     )
-    spread = spread.reshape(members * rows, query_width // members)
+    spread = spread.reshape(lines * rows, query_width // lines)
     projected = lax.psum_scatter(
-        jnp.dot(spread, o_weight, preferred_element_type=jnp.float32),
-        "ep",
+        jnp.dot(spread, gathered, preferred_element_type=jnp.float32),
+        "y",
         scatter_dimension=0,
         tiled=True,
     )
-    width = o_weight.shape[1]
+    members = lax.axis_size("y") * lax.axis_size("x") * lax.axis_size("c")
     mixed = residual.reshape(rows, width).astype(jnp.float32) + projected
     normed = (
         mixed * lax.rsqrt(jnp.mean(mixed * mixed, axis=1, keepdims=True) + EPS) * norm_gain
@@ -242,7 +244,7 @@
     outgoing = jnp.dot(placing, normed, preferred_element_type=jnp.float32).astype(jnp.bfloat16)
     arrived = lax.all_to_all(
         outgoing.reshape(experts_all, capacity, width),
-        ("dp", "ep"),
+        ("dp", "y", "x", "c"),
         split_axis=0,
         concat_axis=0,
         tiled=True,
@@ -254,7 +256,7 @@
     )
     returned = lax.all_to_all(
         answer.reshape(sources * experts_local, depth, width),
-        ("dp", "ep"),
+        ("dp", "y", "x", "c"),
         split_axis=0,
         concat_axis=0,
         tiled=True,
@@ -266,27 +268,31 @@
 
 
 def solution(mesh):
+    lines = mesh.devices.shape[1] // 8
+    mesh = jax.sharding.Mesh(
+        mesh.devices.reshape(mesh.devices.shape[0], lines, 4, 2), ("dp", "y", "x", "c")
+    )
     return jax.shard_map(
         shards,
         mesh=mesh,
         in_specs=(
-            P(("dp", "ep"), None, None),
-            P(("dp", "ep"), None, None),
-            P(("dp", "ep"), None, None),
-            P(("dp", "ep"), None, None),
-            P(("dp", "ep"), None, None),
-            P(("dp", "ep"), None, None),
-            P(("dp", "ep"), None, None),
-            P(("dp", "ep"), None),
-            P(("dp", "ep")),
-            P(("dp", "ep"), None, None),
-            P("ep", None),
+            P(("dp", "y", "x", "c"), None, None),
+            P(("dp", "y", "x", "c"), None, None),
+            P(("dp", "y", "x", "c"), None, None),
+            P(("dp", "y", "x", "c"), None, None),
+            P(("dp", "y", "x", "c"), None, None),
+            P(("dp", "y", "x", "c"), None, None),
+            P(("dp", "y", "x", "c"), None, None),
+            P(("dp", "y", "x", "c"), None),
+            P(("dp", "y", "x", "c")),
+            P(("dp", "y", "x", "c"), None, None),
+            P(("y", "x", "c"), None),
             P(),
-            P(("dp", "ep"), None, None),
-            P(("dp", "ep"), None, None),
-            P(("dp", "ep"), None, None),
-            P(("dp", "ep"), None, None),
+            P(("dp", "y", "x", "c"), None, None),
+            P(("dp", "y", "x", "c"), None, None),
+            P(("dp", "y", "x", "c"), None, None),
+            P(("dp", "y", "x", "c"), None, None),
         ),
-        out_specs=(P(("dp", "ep"), None, None), P(("dp", "ep"), None, None)),
+        out_specs=(P(("dp", "y", "x", "c"), None, None), P(("dp", "y", "x", "c"), None, None)),
         check_vma=False,
     )

time: 344 us -> 271 us (0.79)
  waiting for transfers between devices: 115 us -> 49.2 us
  matrix products: 42.2 us -> 31.9 us
  blocking collectives: 59.8 us -> 64.8 us
    reduce_scatter x1, waiting for transfers between devices: 87.1 us -> 22.3 us  [shards(): lax.psum_scatter(jnp.dot(spread, gathered, preferred_element_type=jnp.flo...]
    dot_general x2 -> x1, matrix products: 11.8 us -> 5.79 us  [second_advance(): jnp.einsum('ngqk,nkgd->ngqd', raw.astype(jnp.bfloat16), value_block, pref...]
    all_to_all x2, blocking collectives: 59.8 us -> 64.8 us  [the longest x1 39.9 us: shards(): lax.all_to_all(outgoing.reshape(experts_all, capacity, width), ('dp', 'y'...]
    dot_general x2 -> x1, matrix products: 8.92 us -> 4.41 us  [first_advance(): jnp.einsum('ngqd,nkgd->ngqk', queries, key_block, preferred_element_type=...]
    unnamed x37 -> x57, local copies, waits for them, and re-layouts: 27.1 us -> 28.7 us
  transfers between devices with their start and end apart: 2 -> 3, of which waited for: 2 -> 2; matrix products, arithmetic and copies ran while one was open for 1% -> 34% of each run, Pallas kernels for 0% -> 0%
where the time goes in v1:
time: 271 us; the launch traced here: 269 us
  local copies, waits for them, and re-layouts  81.4 us (30%)
  blocking collectives  64.8 us (24%)
  waiting for transfers between devices  49.2 us (18%)
  matrix products  31.9 us (12%)
  other arithmetic  20.7 us (8%)
  between operations  15.2 us (6%)
  starting transfers between devices  5.63 us (2%)
    all_to_all x1, blocking collectives, shards(): lax.all_to_all(outgoing.reshape(experts_all, capacity, width), ('dp', 'y'...  39.9 us
    unnamed x57, local copies, waits for them, and re-layouts  28.7 us
    all_to_all x1, waiting for transfers between devices, shards(): lax.all_to_all(answer.reshape(sources * experts_local, depth, width), ('d...  26.2 us
    all_to_all x1, blocking collectives, shards(): lax.all_to_all(attended.reshape(rows, lines, query_width // lines), 'y',...  24.9 us
    reduce_scatter x1, waiting for transfers between devices, shards(): lax.psum_scatter(jnp.dot(spread, gathered, preferred_element_type=jnp.flo...  22.3 us
    dot_general x1, matrix products, run_experts(): jnp.einsum('sjcd,jdf->sjcf', arriving, expert_gate_up, preferred_element_...  9.14 us
    dot_general x1, matrix products, shards(): jnp.dot(spread, gathered, preferred_element_type=jnp.float32)  5.9 us
    dot_general x1, matrix products, second_advance(): jnp.einsum('ngqk,nkgd->ngqd', raw.astype(jnp.bfloat16), value_block, pref...  5.79 us
  transfers between devices with their start and end apart: 3, of which 2 were waited for; matrix products, arithmetic and copies ran while one was open for 34% of the time, Pallas kernels for 0%

profile of v1, /device:TPU:1, one launch (start us, length us, event | category | flops | bytes accessed | tf_op | source)
XLA Modules:
  0.0 268.8 jit_solution(13624798248452465379)
XLA Ops:
  7.2 0.7 all-gather.2.cloned.1.call-update
  8.0 0.8 broadcast_add_fusion
  10.7 12.3 %copy.95 = bf16[16,512,512]{1,2,0:T(8,128)(2,1)} copy(bf16[16,512,512]{2,1,0:T(8,128)(2,1)} %param.25) | data formatting | bytes 16777216 | tf_op args[5]
  23.1 1.5 gather_fusion.1
  24.6 1.5 gather_fusion.2
  26.2 12.4 %copy.113 = bf16[16,512,512]{1,2,0:T(8,128)(2,1)} copy(bf16[16,512,512]{2,1,0:T(8,128)(2,1)} %param.26) | data formatting | bytes 16777216 | tf_op args[6]
  43.5 0.7 copy.100
  44.8 0.7 copy.103
  46.0 1.6 slice_convert_fusion
  47.5 0.8 div.81
  48.3 0.8 broadcast_in_dim.176
  49.1 0.8 mul.189
  49.8 0.8 mul.186
  51.3 0.7 copy.109
  52.1 1.4 copy.112
  53.4 1.3 copy.108
  54.8 1.3 copy.111
  57.4 0.7 pad_add_fusion
  58.1 0.7 copy.98
  58.8 2.2 reshape.374
  61.0 1.9 copy.96
  62.9 2.5 broadcast_in_dim.174
  65.4 4.6 %while.22 = (s32[]{:T(128)}, f32[16,4,32,512]{3,2,1,0:T(8,128)}, s32[]{:T(128)}, s32[512]{0:T(512)S(1)}, s32[16]{0:T(128)S(1)}, /*index=5*/bf16[16,512,4,128]{1,...) while((s32[]{:T(128)}, f32[16,4,32,512]{3,2,1,0:T(8,128)}, ...), condition=%wide.region_3.4_spmd, body=%wide.region_2.3_spmd.sunk | while | flops 135270400 | bytes 6828255 | solution.py:92
  65.6 4.4 %bitcast_dynamic-update-slice_fusion.2 = f32[16,4,32,512]{3,2,1,0:T(8,128)} fusion(f32[16,4,32,512]{3,2,1,0:T(8,128)} %get-tuple-element.291, s32[]{:T(128)S(6)} %select_n.274, bf16[16,4,32,128]{3,2,1,0:T(8,128)(2,1)} %get-tuple-element.307, bf16[16,512,4,128]{1,3,2,0:T(8,128)(2,1)} %get-tuple-element.306, ...), kind=kOutput, calls=%fused_computation.5.clone.1 | convolution fusion | flops 135266304 | bytes 6820864 | tf_op jit(solution)/shard_map/while/body/ngqd,nkgd->ngqk/dot_general | solution.py:84
  70.1 2.6 reduce_max.32
  72.7 0.7 reduce_max.35
  73.4 0.8 fusion.58
  74.3 0.9 fusion.59
  75.2 0.9 broadcast_select_fusion
  76.1 1.5 fusion.71
  78.2 0.7 reduce_max.34
  78.9 0.9 max.10
  79.9 0.9 fusion.37
  80.7 1.5 reduce_sum.114
  82.3 0.8 max.9
  83.1 1.1 broadcast_in_dim.172
  84.2 6.5 %while.23 = (s32[]{:T(128)}, f32[16,4,32,128]{3,2,1,0:T(8,128)}, f32[16,4,32]{2,1,0:T(4,128)S(1)}, s32[]{:T(128)}, f32[16,4,32,512]{3,2,1,0:T(8,128)}, /*index=5...) while((s32[]{:T(128)}, f32[16,4,32,128]{3,2,1,0:T(8,128)}, ...), condition=%wide.region_10.11_spmd, body=%wide.region_8.10_spmd.sunk | while | flops 136577024 | bytes 27313340 | solution.py:118
  84.2 5.8 %fusion.87 = f32[16,4,32,128]{3,2,1,0:T(8,128)} fusion(f32[16,4,32,128]{3,2,1,0:T(8,128)} %get-tuple-element.324, bf16[16,512,4,128]{1,3,2,0:T(8,128)(2,1)} %get-tuple-element.340, s32[]{:T(128)S(6)} %select_n.275, f32[16,4,32,512]{3,2,1,0:T(8,128)} %get-tuple-element.338, f32[16,4,32]{2,1,0:T(4,128)S(1)} %get-tuple-element.339), kind=kOutput, calls=%fused_computation.13.clone.1 | convolution fusion | flops 135528448 | bytes 8397824 | tf_op jit(solution)/shard_map/while/body/ngqk,nkgd->ngqd/dot_general | solution.py:106
  90.0 0.7 fusion.88
  90.7 0.8 add.170
  91.5 1.3 fusion.39
  92.7 1.6 fusion.31
  94.3 0.8 copy-done.2
  95.1 0.9 copy.161
  96.0 2.1 reshape_reshape.3
  98.1 24.9 %all_to_all.25 = bf16[32,4,2048]{2,0,1:T(8,128)(2,1)} all-to-all(bf16[32,4,2048]{2,0,1:T(8,128)(2,1)} %reshape_reshape.3), channel_id=1, replica_groups=mesh['dp'=4,'y'=4,'x'=4,'c'=2] {'y'}, dimensions={1} | all-to-all | bytes 1048576 | tf_op jit(solution)/shard_map/all_to_all | solution.py:211
  123.0 5.9 %fusion.72 = f32[128,2048]{1,0:T(8,128)} fusion(bf16[128,2048]{1,0:T(8,128)(2,1)} %bitcast.167, bf16[2048,2048]{1,0:T(8,128)(2,1)} %all-gather.2.cloned.1.call-done), kind=kOutput, calls=%fused_computation.124 | convolution fusion | flops 1073741824 | bytes 9961472 | tf_op jit(solution)/shard_map/dot_general | solution.py:220
  128.9 0.7 reshape.395
  130.5 22.3 %reduce-scatter.2.cloned.1.call-done = f32[32,2048]{1,0:T(8,128)} async-done(((f32[128,2048]{1,0:T(8,128)}), f32[32,2048]{1,0:T(8,128)}) %reduce-scatter.2.cloned.1.call-update) | async-done | bytes 262160 | tf_op jit(solution)/shard_map/reduce_scatter | solution.py:219
  152.8 1.2 multiply_reduce_fusion
  153.9 2.1 convolution_convert_fusion
  156.1 4.1 %reshape.383 = bf16[128,4,2048]{2,1,0:T(4,128)(2,1)} reshape(bf16[512,2048]{1,0:T(8,128)(2,1)} %convolution_convert_fusion) | data formatting | bytes 4194304 | tf_op jit(solution)/shard_map/reshape | solution.py:246
  160.2 39.9 %all_to_all.26 = bf16[128,4,2048]{2,1,0:T(4,128)(2,1)S(1)} all-to-all(bf16[128,4,2048]{2,1,0:T(4,128)(2,1)} %reshape.383), channel_id=1, replica_groups=mesh['dp'=4,'y'=4,'x'=4,'c'=2] {'dp','y','x','c'}, dimensions={0} | all-to-all | bytes 4194304 | tf_op jit(solution)/shard_map/all_to_all | solution.py:245
  200.1 9.1 %fusion.17 = f32[128,1,4,1536]{3,0,2,1:T(8,128)S(1)} fusion(bf16[1,2048,1536]{2,1,0:T(8,128)(2,1)} %param.32, bf16[128,4,2048]{2,1,0:T(4,128)(2,1)S(1)} %all_to_all.26), kind=kOutput, calls=%fused_computation.18 | convolution fusion | flops 3221225472 | bytes 11534336 | tf_op jit(solution)/shard_map/sjcd,jdf->sjcf/dot_general | solution.py:123
  209.2 1.8 fusion.22
  211.0 2.9 %copy.123 = bf16[128,4,2048]{2,1,0:T(4,128)(2,1)} copy(bf16[128,4,2048]{2,0,1:T(8,128)(2,1)S(1)} %fusion.22) | data formatting | bytes 4194304 | tf_op jit(solution)/shard_map/convert_element_type | solution.py:129
  214.0 5.6 %all-to-all-start.2 = ((bf16[128,4,2048]{2,1,0:T(4,128)(2,1)}), bf16[128,4,2048]{2,1,0:T(4,128)(2,1)}, u32[]{:S(2)}, u32[]{:S(2)}) async-start(bf16[128,4,2048]{2,1,0:T(4,128)(2,1)} %copy.123), calls=%async_computation.3 | async-start | bytes 4194304 | tf_op jit(solution)/shard_map/all_to_all | solution.py:257
  219.7 1.9 copy.118
  221.6 2.0 reshape.381
  223.6 26.2 %all-to-all-done.2 = bf16[128,4,2048]{2,1,0:T(4,128)(2,1)} async-done(((bf16[128,4,2048]{2,1,0:T(4,128)(2,1)}), bf16[128,4,2048]{2,1,0:T(4,128)(2,1)}, u32[]{:S(2)}, u32[]{:S(2)}) %all-to-all-start.2) | async-done | bytes 2097184 | tf_op jit(solution)/shard_map/all_to_all | solution.py:257
  249.8 3.9 %reshape.387 = bf16[512,2048]{1,0:T(8,128)(2,1)} reshape(bf16[128,4,2048]{2,1,0:T(4,128)(2,1)} %all-to-all-done.2) | data formatting | bytes 4194304 | tf_op jit(solution)/shard_map/reshape | solution.py:264
  253.8 5.2 %gather_fusion = bf16[256,2048]{1,0:T(8,128)(2,1)} fusion(bf16[512,2048]{1,0:T(8,128)(2,1)} %reshape.387, s32[1024]{0:T(1024)S(1)} %pad_clamp_fusion), kind=kCustom, calls=%fused_computation | custom fusion | bytes 2098176 | tf_op jit(solution)/shard_map/gather | solution.py:264
  259.0 2.2 fusion.25
  261.2 0.8 reshape.388
  (110 shorter events, 11.2 us)
Async XLA Ops:
  7.2 202.0 %copy-start = (bf16[1,768,2048]{2,1,0:T(8,128)(2,1)S(1)}, bf16[1,768,2048]{2,1,0:T(8,128)(2,1)}, u32[]{:S(2)}) copy-start(bf16[1,768,2048]{2,1,0:T(8,128)(2,1)} %param.33) | copy-start | bytes 9437188
  7.2 115.8 %all-gather.2.cloned.1.call-start = ((), (), s32[]{:S(2)}) async-start(), calls=%async_computation.4 | async-start | bytes 9437184 | tf_op jit(solution)/shard_map/all_gather | solution.py:209
  7.9 144.8 %reduce-scatter.2.cloned.1.call-start = ((), (), s32[]{:S(2)}) async-start(), calls=%async_computation.5 | async-start | bytes 1310720 | tf_op jit(solution)/shard_map/reduce_scatter | solution.py:219
  8.8 0.5 copy-start.19
  10.7 12.4 %copy-start.26 = (s32[16]{0:T(128)S(1)}, s32[16]{0:T(128)}, u32[]{:S(2)}) copy-start(s32[16]{0:T(128)} %param.28) | copy-start | bytes 196
  26.1 12.4 %copy-start.25 = (s32[16,2,4]{0,2,1:T(4,128)S(1)}, s32[16,2,4]{0,2,1:T(4,128)}, u32[]{:S(2)}) copy-start(s32[16,2,4]{0,2,1:T(4,128)} %param.24) | copy-start | bytes 1540
  26.1 15.4 %copy-start.23 = (f32[16,4]{0,1:T(4,128)S(1)}, f32[16,4]{0,1:T(4,128)}, u32[]{:S(2)}) copy-start(f32[16,4]{0,1:T(4,128)} %param.27) | copy-start | bytes 772
  26.2 16.1 %copy-start.18 = (f32[16,2,4]{0,2,1:T(4,128)S(1)}, f32[16,2,4]{0,2,1:T(4,128)}, u32[]{:S(2)}) copy-start(f32[16,2,4]{0,2,1:T(4,128)} %param.23) | copy-start | bytes 1540
  26.2 19.8 %copy-start.8 = (bf16[16,2,512]{2,1,0:T(2,128)(2,1)S(1)}, bf16[16,2,512]{2,1,0:T(2,128)(2,1)}, u32[]{:S(2)}) copy-start(bf16[16,2,512]{2,1,0:T(2,128)(2,1)} %param.22) | copy-start | bytes 98308
  39.7 0.6 copy-start.24
  40.6 0.6 copy-start.12
  40.6 5.3 %copy-start.10 = (pred[16,3,4]{1,2,0:T(4,128)(4,1)}, pred[16,3,4]{1,2,0:T(4,128)(4,1)S(1)}, u32[]{:S(2)}) copy-start(pred[16,3,4]{1,2,0:T(4,128)(4,1)S(1)} %get-tuple-element.189) | copy-start | bytes 580
  58.8 6.6 %copy-start.20 = (s32[16]{0:T(128)S(1)}, s32[16]{0:T(128)}, u32[]{:S(2)}) copy-start(s32[16]{0:T(128)} %copy-done.19) | copy-start | bytes 196
  70.0 3.4 %copy-start.6 = (f32[16,4,128]{2,1,0:T(4,128)S(1)}, f32[16,4,128]{2,1,0:T(4,128)}, u32[]{:S(2)}) copy-start(f32[16,4,128]{2,1,0:T(4,128)} %reshape.389) | copy-start | bytes 98308
  70.0 3.4 %copy-start.7 = (f32[16,4,128]{2,1,0:T(4,128)S(1)}, f32[16,4,128]{2,1,0:T(4,128)}, u32[]{:S(2)}) copy-start(f32[16,4,128]{2,1,0:T(4,128)} %reshape.392) | copy-start | bytes 98308
  70.0 3.4 %copy-start.14 = (f32[16,4]{1,0:T(8,128)S(1)}, f32[16,4]{1,0:T(8,128)}, u32[]{:S(2)}) copy-start(f32[16,4]{1,0:T(8,128)} %copy.101) | copy-start | bytes 772
  70.0 3.4 %copy-start.15 = (f32[16,4]{1,0:T(8,128)S(1)}, f32[16,4]{1,0:T(8,128)}, u32[]{:S(2)}) copy-start(f32[16,4]{1,0:T(8,128)} %copy.105) | copy-start | bytes 772
  70.0 3.4 %copy-start.16 = (f32[16,4]{1,0:T(8,128)S(1)}, f32[16,4]{1,0:T(8,128)}, u32[]{:S(2)}) copy-start(f32[16,4]{1,0:T(8,128)} %copy.103) | copy-start | bytes 772
  70.0 4.2 %copy-start.5 = (f32[16,4,128]{2,1,0:T(4,128)S(1)}, f32[16,4,128]{2,1,0:T(4,128)}, u32[]{:S(2)}) copy-start(f32[16,4,128]{2,1,0:T(4,128)} %reduce_sum.112) | copy-start | bytes 98308
  70.0 4.2 %copy-start.9 = (f32[16,1,512]{2,1,0:T(1,128)S(1)}, f32[16,1,512]{2,1,0:T(1,128)}, u32[]{:S(2)}) copy-start(f32[16,1,512]{2,1,0:T(1,128)} %get-tuple-element.171) | copy-start | bytes 98308
  70.0 5.2 %copy-start.11 = (pred[16,3,4]{1,2,0:T(4,128)(4,1)S(1)}, pred[16,3,4]{1,2,0:T(4,128)(4,1)}, u32[]{:S(2)}) copy-start(pred[16,3,4]{1,2,0:T(4,128)(4,1)} %copy-done.10) | copy-start | bytes 580
  70.0 5.2 %copy-start.13 = (pred[16,3,4]{1,2,0:T(4,128)(4,1)S(1)}, pred[16,3,4]{1,2,0:T(4,128)(4,1)}, u32[]{:S(2)}) copy-start(pred[16,3,4]{1,2,0:T(4,128)(4,1)} %copy-done.12) | copy-start | bytes 580
  77.6 0.6 copy-start.3
  84.2 5.8 %copy-start.1 = (f32[16,4,32,512]{3,2,1,0:T(8,128)S(1)}, f32[16,4,32,512]{3,2,1,0:T(8,128)}, u32[]{:S(2)}) copy-start(f32[16,4,32,512]{3,2,1,0:T(8,128)} %get-tuple-element.338) | copy-start | bytes 12582916 | tf_op jit(solution)/shard_map/while
  94.3 0.8 copy-start.2
  123.0 5.9 %copy-start.4 = (bf16[16,2,2048]{2,1,0:T(2,128)(2,1)S(1)}, bf16[16,2,2048]{2,1,0:T(2,128)(2,1)}, u32[]{:S(2)}) copy-start(bf16[16,2,2048]{2,1,0:T(2,128)(2,1)} %param.29) | copy-start | bytes 393220
  123.0 6.7 %copy-start.17 = (s32[16,2,8]{0,2,1:T(8,128)S(1)}, s32[16,2,8]{0,2,1:T(8,128)}, u32[]{:S(2)}) copy-start(s32[16,2,8]{0,2,1:T(8,128)} %param.34) | copy-start | bytes 3076
  123.0 30.9 %copy-start.21 = (f32[2048]{0:T(1024)S(1)}, f32[2048]{0:T(1024)}, u32[]{:S(2)}) copy-start(f32[2048]{0:T(1024)} %param.31) | copy-start | bytes 24580
  214.0 5.7 %copy-start.22 = (f32[16,2,8]{0,2,1:T(8,128)S(1)}, f32[16,2,8]{0,2,1:T(8,128)}, u32[]{:S(2)}) copy-start(f32[16,2,8]{0,2,1:T(8,128)} %param.35) | copy-start | bytes 3076
  214.0 35.9 %all-to-all-start.2 = ((bf16[128,4,2048]{2,1,0:T(4,128)(2,1)}), bf16[128,4,2048]{2,1,0:T(4,128)(2,1)}, u32[]{:S(2)}, u32[]{:S(2)}) async-start(bf16[128,4,2048]{2,1,0:T(4,128)(2,1)} %copy.123), calls=%async_computation.3 | async-start | bytes 4194304 | tf_op jit(solution)/shard_map/all_to_all | solution.py:257
Sparse Core Ops, SparseCore 0:
  9.7 53.3 all-gather.1
  129.0 23.6 reduce-scatter.1

commit v2 on v1

--- a/solution.py
+++ b/solution.py
@@ -3,6 +3,8 @@
 import jax
 import jax.numpy as jnp
 from jax import lax
+from jax.experimental import pallas as pl
+from jax.experimental.pallas import tpu as pltpu
 from jax.sharding import PartitionSpec as P
 
 EPS = 1e-06
@@ -70,53 +72,50 @@
     )
 
 
-def first_pass(keys, queries, slot_order, limits, block, scale):
-    requests, slots = (keys.shape[0], keys.shape[1])
-    heads_kv, rows = (queries.shape[1], queries.shape[2])
-    usable = jnp.sum((slot_order[None, :] < limits[:, None]).astype(jnp.int32), axis=1)
-    blocks = (jnp.max(usable) + block - 1) // block
-    initial = jnp.full((requests, heads_kv, rows, slots), -jnp.inf, jnp.float32)
-
-    def first_advance(index, buffer):
-        start = index * block
-        key_block = lax.dynamic_slice_in_dim(keys, start, block, 1)
-        scores = (
-            jnp.einsum("ngqd,nkgd->ngqk", queries, key_block, preferred_element_type=jnp.float32)
-            * scale
-        )
-        order_block = lax.dynamic_slice_in_dim(slot_order, start, block, 0)
-        valid = order_block[None, :] < limits[:, None]
-        scores = jnp.where(valid[:, None, None, :], scores, -jnp.inf)
-        return lax.dynamic_update_slice_in_dim(buffer, scores, start, 3)
-
-    return (lax.fori_loop(0, blocks, first_advance, initial), blocks)
-
-
-def second_pass(values, buffer, highest, blocks, block):
-    requests, heads_kv, rows = (buffer.shape[0], buffer.shape[1], buffer.shape[2])
-    head_dim = values.shape[3]
-
-    def second_advance(index, carry):
-        summed, totals = carry
-        start = index * block
-        scores = lax.dynamic_slice_in_dim(buffer, start, block, 3)
-        raw = jnp.exp(scores - highest[..., None])
-        totals = totals + jnp.sum(raw, axis=3)
-        value_block = lax.dynamic_slice_in_dim(values, start, block, 1)
-        summed = summed + jnp.einsum(
-            "ngqk,nkgd->ngqd",
-            raw.astype(jnp.bfloat16),
-            value_block,
-            preferred_element_type=jnp.float32,
-        )
-        return (summed, totals)
-
-    initial = (
-        jnp.zeros((requests, heads_kv, rows, head_dim), jnp.float32),
-        jnp.zeros((requests, heads_kv, rows), jnp.float32),
-    )
-    return lax.fori_loop(0, blocks, second_advance, initial)
-
+def cache_attention(grouped, key_cache, value_cache, limits, tail_highest, scale):
+    requests, heads_kv, rows, head_dim = grouped.shape
+    slots, width = key_cache.shape[1], key_cache.shape[2]
+
+    def kernel(limit_ref, q_ref, k_ref, v_ref, th_ref, acc_ref, tot_ref, top_ref):
+        limit = limit_ref[pl.program_id(0)]
+        valid = lax.broadcasted_iota(jnp.int32, (rows, slots), 1) < limit
+        for g in range(heads_kv):
+            lanes = slice(g * head_dim, (g + 1) * head_dim)
+            scores = (
+                lax.dot_general(
+                    q_ref[0, g],
+                    k_ref[0, :, lanes],
+                    (((1,), (1,)), ((), ())),
+                    preferred_element_type=jnp.float32,
+                )
+                * scale
+            )
+            scores = jnp.where(valid, scores, -jnp.inf)
+            top = jnp.maximum(jnp.max(scores, axis=1, keepdims=True), th_ref[0, g])
+            raw = jnp.exp(scores - top)
+            tot_ref[0, g] = jnp.sum(raw, axis=1, keepdims=True)
+            top_ref[0, g] = top
+            acc_ref[0, g] = jnp.dot(
+                raw.astype(jnp.bfloat16), v_ref[0, :, lanes], preferred_element_type=jnp.float32
+            )
+
+    per_row = pl.BlockSpec((1, heads_kv, rows, head_dim), lambda r, lim: (r, 0, 0, 0))
+    per_head = pl.BlockSpec((1, heads_kv, rows, 1), lambda r, lim: (r, 0, 0, 0))
+    per_cache = pl.BlockSpec((1, slots, width), lambda r, lim: (r, 0, 0))
+    return pl.pallas_call(
+        kernel,
+        out_shape=(
+            jax.ShapeDtypeStruct((requests, heads_kv, rows, head_dim), jnp.float32),
+            jax.ShapeDtypeStruct((requests, heads_kv, rows, 1), jnp.float32),
+            jax.ShapeDtypeStruct((requests, heads_kv, rows, 1), jnp.float32),
+        ),
+        grid_spec=pltpu.PrefetchScalarGridSpec(
+            num_scalar_prefetch=1,
+            grid=(requests,),
+            in_specs=[per_row, per_cache, per_cache, per_head],
+            out_specs=[per_row, per_head, per_head],
+        ),
+    )(limits, grouped, key_cache, value_cache, tail_highest)
 
 def run_experts(arriving, expert_gate_up, expert_down):
     hidden_units = expert_down.shape[1]
@@ -182,13 +181,11 @@
     tail_scores = jnp.where(tail_valid, tail_scores, -jnp.inf)
     tail_highest = jnp.max(tail_scores, axis=3)
     limits = lengths - 1
-    keys_grid = key_cache.reshape(requests, slots_all, heads_kv, head_dim)
-    values_grid = value_cache.reshape(requests, slots_all, heads_kv, head_dim)
-    block = math.gcd(slots_all, 256)
-    slot_order = jnp.arange(slots_all, dtype=jnp.int32)
-    buffer, blocks = first_pass(keys_grid, grouped, slot_order, limits, block, scale)
-    highest = jnp.maximum(jnp.max(buffer, axis=3), tail_highest)
-    summed, totals = second_pass(values_grid, buffer, highest, blocks, block)
+    summed, totals, highest = cache_attention(
+        grouped, key_cache, value_cache, limits, tail_highest[..., None], scale
+    )
+    totals = totals[..., 0]
+    highest = highest[..., 0]
     tail_raw = jnp.exp(tail_scores - highest[..., None])
     totals = totals + jnp.sum(tail_raw, axis=3)
     tail_weights = tail_raw.astype(jnp.bfloat16).reshape(

time: 271 us -> 252 us (0.930)
  Pallas kernels: 0 us -> 25.3 us
  local copies, waits for them, and re-layouts: 81.4 us -> 58.8 us
  blocking collectives: 64.8 us -> 53.6 us
  matrix products: 31.9 us -> 21.7 us
    unnamed x57 -> x43, local copies, waits for them, and re-layouts: 28.7 us -> 3.44 us
    pallas_call x0 -> x1, Pallas kernels: none -> 25.3 us  [cache_attention(): pl.pallas_call(kernel, out_shape=(jax.ShapeDtypeStruct((requests, heads_k...]
    all_to_all x1, blocking collectives: 24.9 us -> 13.7 us  [shards(): lax.all_to_all(attended.reshape(rows, lines, query_width // lines), 'y',...]
    dot_general x2 -> x0, matrix products: 10.2 us -> none  [the longest x1 5.79 us: second_advance(): jnp.einsum('ngqk,nkgd->ngqd', raw.astype(jnp.bfloat16), value_block, pref...]
    reduce_max x2 -> x0, other arithmetic: 3.25 us -> none  [the longest x1 2.62 us: shards(): highest = jnp.maximum(jnp.max(buffer, axis=3), tail_highest)]
  transfers between devices with their start and end apart: 3 -> 3, of which waited for: 2 -> 2; matrix products, arithmetic and copies ran while one was open for 34% -> 24% of each run, Pallas kernels for 0% -> 10%
where the time goes in v2:
time: 252 us; the launch traced here: 250 us
  local copies, waits for them, and re-layouts  58.8 us (23%)
  blocking collectives  53.6 us (21%)
  waiting for transfers between devices  49.2 us (20%)
  Pallas kernels  25.3 us (10%)
  matrix products  21.7 us (9%)
  other arithmetic  21.6 us (9%)
  between operations  14.5 us (6%)
  starting transfers between devices  5.63 us (2%)
    all_to_all x1, blocking collectives, shards(): lax.all_to_all(outgoing.reshape(experts_all, capacity, width), ('dp', 'y'...  39.9 us
    all_to_all x1, waiting for transfers between devices, shards(): lax.all_to_all(answer.reshape(sources * experts_local, depth, width), ('d...  26.2 us
    pallas_call x1, Pallas kernels, cache_attention(): pl.pallas_call(kernel, out_shape=(jax.ShapeDtypeStruct((requests, heads_k...  25.3 us
    reduce_scatter x1, waiting for transfers between devices, shards(): lax.psum_scatter(jnp.dot(spread, gathered, preferred_element_type=jnp.flo...  22.3 us
    all_to_all x1, blocking collectives, shards(): lax.all_to_all(attended.reshape(rows, lines, query_width // lines), 'y',...  13.7 us
    dot_general x1, matrix products, run_experts(): jnp.einsum('sjcd,jdf->sjcf', arriving, expert_gate_up, preferred_element_...  9.14 us
    dot_general x1, matrix products, shards(): jnp.dot(spread, gathered, preferred_element_type=jnp.float32)  5.91 us
    all_to_all x1, starting transfers between devices, shards(): lax.all_to_all(answer.reshape(sources * experts_local, depth, width), ('d...  5.55 us
  transfers between devices with their start and end apart: 3, of which 2 were waited for; matrix products, arithmetic and copies ran while one was open for 24% of the time, Pallas kernels for 10%

profile of v2, /device:TPU:1, one launch (start us, length us, event | category | flops | bytes accessed | tf_op | source)
XLA Modules:
  0.0 250.2 jit_solution(9808644879683078403)
XLA Ops:
  7.2 0.7 all-gather.2.cloned.1.call-update
  8.0 1.4 select_bitcast_fusion
  9.4 1.3 add_select_fusion
  12.4 0.7 fusion.47
  13.1 1.5 gather_fusion.2
  14.5 1.5 gather_fusion.1
  16.0 1.3 copy.105
  17.3 1.3 fusion.51
  18.7 0.7 copy.109
  19.3 0.7 copy.104
  20.0 1.3 slice_bitcast_fusion
  21.3 0.7 copy.107
  22.5 1.6 slice_convert_fusion
  24.0 0.8 div.72
  24.8 0.8 broadcast_in_dim.148
  25.6 0.8 mul.179
  26.3 0.8 mul.176
  27.3 0.6 reduce_sum.93
  27.9 1.3 copy.113
  29.2 1.3 copy.116
  30.6 1.3 copy.112
  31.8 1.3 copy.115
  33.8 0.6 reshape.353
  34.5 0.7 pad_add_fusion
  35.3 0.7 copy.102
  36.0 2.3 reshape.336
  38.3 1.9 copy.101
  40.2 0.8 fusion.43
  41.1 0.9 fusion.44
  42.0 1.6 broadcast_select_fusion
  43.5 1.5 fusion.56
  45.0 1.6 reshape.390.th_ref
  46.6 1.2 broadcast_add_fusion.limit_ref
  47.8 25.3 %shard_map.167 = (f32[16,4,32,128]{3,2,1,0:T(8,128)}, f32[16,4,32,1]{3,2,1,0:T(8,128)}, f32[16,4,32,1]{3,2,1,0:T(8,128)}) custom-call(s32[16]{0:T(128)} %broadcast_add_fusion.limit_ref, bf16[16,4,32,128]{3,2,1,0:T(8,128)(2,1)} %bitcast.158, bf16[16,512,512]{2,1,0:T(8,128)(2,1)} %k_ref.1, bf16[16,512,512]{2,1,0:T(8,128)(2,1)} %v_ref.1, ...), custom_call_target="tpu_custom_call" | custom-call | tf_op jit(solution)/shard_map/pallas_call | solution.py:105
  73.0 2.2 reduce.6
  75.2 0.9 reshape.388
  76.1 0.9 fusion.22
  77.0 2.4 reshape.391
  79.4 2.8 %add.145 = f32[16,4,32,1]{3,2,1,0:T(8,128)} add(f32[16,4,32,1]{3,2,1,0:T(8,128)} %get-tuple-element.7, f32[16,4,32,1]{3,2,1,0:T(8,128)} %reshape.391) | non-fusion elementwise | flops 2048 | bytes 24576 | tf_op jit(solution)/shard_map/add | solution.py:190
  82.2 2.3 copy.125
  84.4 0.9 copy.126
  85.3 1.2 fusion.24
  86.9 0.8 copy-done.1
  87.7 0.9 copy.174
  88.6 2.1 reshape_reshape.3
  90.7 13.7 %all_to_all.25 = bf16[32,4,2048]{2,0,1:T(8,128)(2,1)} all-to-all(bf16[32,4,2048]{2,0,1:T(8,128)(2,1)} %reshape_reshape.3), channel_id=1, replica_groups=mesh['dp'=4,'y'=4,'x'=4,'c'=2] {'y'}, dimensions={1} | all-to-all | bytes 1048576 | tf_op jit(solution)/shard_map/all_to_all | solution.py:208
  104.4 5.9 %fusion.57 = f32[128,2048]{1,0:T(8,128)} fusion(bf16[128,2048]{1,0:T(8,128)(2,1)} %bitcast.156, bf16[2048,2048]{1,0:T(8,128)(2,1)} %all-gather.2.cloned.1.call-done), kind=kOutput, calls=%fused_computation.109 | convolution fusion | flops 1073741824 | bytes 9961472 | tf_op jit(solution)/shard_map/dot_general | solution.py:217
  110.3 0.8 reshape.356
  111.9 22.3 %reduce-scatter.2.cloned.1.call-done = f32[32,2048]{1,0:T(8,128)} async-done(((f32[128,2048]{1,0:T(8,128)}), f32[32,2048]{1,0:T(8,128)}) %reduce-scatter.2.cloned.1.call-update) | async-done | bytes 262160 | tf_op jit(solution)/shard_map/reduce_scatter | solution.py:216
  134.2 1.2 multiply_reduce_fusion
  135.3 2.1 convolution_convert_fusion
  137.5 4.1 %reshape.344 = bf16[128,4,2048]{2,1,0:T(4,128)(2,1)} reshape(bf16[512,2048]{1,0:T(8,128)(2,1)} %convolution_convert_fusion) | data formatting | bytes 4194304 | tf_op jit(solution)/shard_map/reshape | solution.py:243
  141.6 39.9 %all_to_all.26 = bf16[128,4,2048]{2,1,0:T(4,128)(2,1)S(1)} all-to-all(bf16[128,4,2048]{2,1,0:T(4,128)(2,1)} %reshape.344), channel_id=1, replica_groups=mesh['dp'=4,'y'=4,'x'=4,'c'=2] {'dp','y','x','c'}, dimensions={0} | all-to-all | bytes 4194304 | tf_op jit(solution)/shard_map/all_to_all | solution.py:242
  181.5 9.1 %fusion.2 = f32[128,1,4,1536]{3,0,2,1:T(8,128)S(1)} fusion(bf16[1,2048,1536]{2,1,0:T(8,128)(2,1)} %param.28, bf16[128,4,2048]{2,1,0:T(4,128)(2,1)S(1)} %all_to_all.26), kind=kOutput, calls=%fused_computation.5 | convolution fusion | flops 3221225472 | bytes 11534336 | tf_op jit(solution)/shard_map/sjcd,jdf->sjcf/dot_general | solution.py:122
  190.6 1.8 fusion.7
  192.4 2.9 %copy.133 = bf16[128,4,2048]{2,1,0:T(4,128)(2,1)} copy(bf16[128,4,2048]{2,0,1:T(8,128)(2,1)S(1)} %fusion.7) | data formatting | bytes 4194304 | tf_op jit(solution)/shard_map/convert_element_type | solution.py:128
  195.4 5.6 %all-to-all-start.2 = ((bf16[128,4,2048]{2,1,0:T(4,128)(2,1)}), bf16[128,4,2048]{2,1,0:T(4,128)(2,1)}, u32[]{:S(2)}, u32[]{:S(2)}) async-start(bf16[128,4,2048]{2,1,0:T(4,128)(2,1)} %copy.133), calls=%async_computation.3 | async-start | bytes 4194304 | tf_op jit(solution)/shard_map/all_to_all | solution.py:254
  201.1 1.9 copy.128
  203.0 2.0 reshape.342
  205.0 26.2 %all-to-all-done.2 = bf16[128,4,2048]{2,1,0:T(4,128)(2,1)} async-done(((bf16[128,4,2048]{2,1,0:T(4,128)(2,1)}), bf16[128,4,2048]{2,1,0:T(4,128)(2,1)}, u32[]{:S(2)}, u32[]{:S(2)}) %all-to-all-start.2) | async-done | bytes 2097184 | tf_op jit(solution)/shard_map/all_to_all | solution.py:254
  231.2 4.0 %reshape.348 = bf16[512,2048]{1,0:T(8,128)(2,1)} reshape(bf16[128,4,2048]{2,1,0:T(4,128)(2,1)} %all-to-all-done.2) | data formatting | bytes 4194304 | tf_op jit(solution)/shard_map/reshape | solution.py:261
  235.2 5.2 %gather_fusion = bf16[256,2048]{1,0:T(8,128)(2,1)} fusion(bf16[512,2048]{1,0:T(8,128)(2,1)} %reshape.348, s32[1024]{0:T(1024)S(1)} %pad_clamp_fusion), kind=kCustom, calls=%fused_computation | custom fusion | bytes 2098176 | tf_op jit(solution)/shard_map/gather | solution.py:261
  240.4 2.2 fusion.10
  242.6 0.8 reshape.349
  (81 shorter events, 4.4 us)
Async XLA Ops:
  7.2 183.4 %copy-start = (bf16[1,768,2048]{2,1,0:T(8,128)(2,1)S(1)}, bf16[1,768,2048]{2,1,0:T(8,128)(2,1)}, u32[]{:S(2)}) copy-start(bf16[1,768,2048]{2,1,0:T(8,128)(2,1)} %param.29) | copy-start | bytes 9437188
  7.2 15.3 %copy-start.7 = (bf16[16,2,512]{2,1,0:T(2,128)(2,1)S(1)}, bf16[16,2,512]{2,1,0:T(2,128)(2,1)}, u32[]{:S(2)}) copy-start(bf16[16,2,512]{2,1,0:T(2,128)(2,1)} %param.18) | copy-start | bytes 98308
  7.2 97.2 %all-gather.2.cloned.1.call-start = ((), (), s32[]{:S(2)}) async-start(), calls=%async_computation.4 | async-start | bytes 9437184 | tf_op jit(solution)/shard_map/all_gather | solution.py:206
  7.9 126.2 %reduce-scatter.2.cloned.1.call-start = ((), (), s32[]{:S(2)}) async-start(), calls=%async_computation.5 | async-start | bytes 1310720 | tf_op jit(solution)/shard_map/reduce_scatter | solution.py:216
  10.7 0.5 copy-start.19
  11.4 0.6 copy-start.11
  11.5 10.9 %copy-start.10 = (pred[16,3,4]{1,2,0:T(4,128)(4,1)}, pred[16,3,4]{1,2,0:T(4,128)(4,1)S(1)}, u32[]{:S(2)}) copy-start(pred[16,3,4]{1,2,0:T(4,128)(4,1)S(1)} %get-tuple-element.45) | copy-start | bytes 580
  27.2 13.0 %copy-start.12 = (f32[16,4]{1,0:T(8,128)S(1)}, f32[16,4]{1,0:T(8,128)}, u32[]{:S(2)}) copy-start(f32[16,4]{1,0:T(8,128)} %copy.105) | copy-start | bytes 772
  27.2 13.0 %copy-start.13 = (f32[16,4]{1,0:T(8,128)S(1)}, f32[16,4]{1,0:T(8,128)}, u32[]{:S(2)}) copy-start(f32[16,4]{1,0:T(8,128)} %copy.109) | copy-start | bytes 772
  27.2 13.0 %copy-start.14 = (f32[16,4]{1,0:T(8,128)S(1)}, f32[16,4]{1,0:T(8,128)}, u32[]{:S(2)}) copy-start(f32[16,4]{1,0:T(8,128)} %copy.107) | copy-start | bytes 772
  33.2 7.9 %copy-start.4 = (f32[16,4,128]{2,1,0:T(4,128)S(1)}, f32[16,4,128]{2,1,0:T(4,128)}, u32[]{:S(2)}) copy-start(f32[16,4,128]{2,1,0:T(4,128)} %reduce_sum.93) | copy-start | bytes 98308
  33.8 6.4 %copy-start.5 = (f32[16,4,128]{2,1,0:T(4,128)S(1)}, f32[16,4,128]{2,1,0:T(4,128)}, u32[]{:S(2)}) copy-start(f32[16,4,128]{2,1,0:T(4,128)} %reshape.350) | copy-start | bytes 98308
  34.5 5.7 %copy-start.6 = (f32[16,4,128]{2,1,0:T(4,128)S(1)}, f32[16,4,128]{2,1,0:T(4,128)}, u32[]{:S(2)}) copy-start(f32[16,4,128]{2,1,0:T(4,128)} %reshape.353) | copy-start | bytes 98308
  34.5 6.6 %copy-start.8 = (f32[16,1,512]{2,1,0:T(1,128)S(1)}, f32[16,1,512]{2,1,0:T(1,128)}, u32[]{:S(2)}) copy-start(f32[16,1,512]{2,1,0:T(1,128)} %get-tuple-element.27) | copy-start | bytes 98308
  34.5 6.6 %copy-start.9 = (f32[16,1,512]{2,1,0:T(1,128)S(1)}, f32[16,1,512]{2,1,0:T(1,128)}, u32[]{:S(2)}) copy-start(f32[16,1,512]{2,1,0:T(1,128)} %get-tuple-element.43) | copy-start | bytes 98308
  34.5 6.6 %copy-start.15 = (f32[16,4]{1,0:T(8,128)S(1)}, f32[16,4]{1,0:T(8,128)}, u32[]{:S(2)}) copy-start(f32[16,4]{1,0:T(8,128)} %copy.113) | copy-start | bytes 772
  84.4 2.1 copy-start.2
  86.9 0.8 copy-start.1
  104.4 5.9 %copy-start.3 = (bf16[16,2,2048]{2,1,0:T(2,128)(2,1)S(1)}, bf16[16,2,2048]{2,1,0:T(2,128)(2,1)}, u32[]{:S(2)}) copy-start(bf16[16,2,2048]{2,1,0:T(2,128)(2,1)} %param.25) | copy-start | bytes 393220
  104.4 6.7 %copy-start.16 = (s32[16,2,8]{0,2,1:T(8,128)S(1)}, s32[16,2,8]{0,2,1:T(8,128)}, u32[]{:S(2)}) copy-start(s32[16,2,8]{0,2,1:T(8,128)} %param.30) | copy-start | bytes 3076
  110.3 25.0 %copy-start.17 = (f32[2048]{0:T(1024)S(1)}, f32[2048]{0:T(1024)}, u32[]{:S(2)}) copy-start(f32[2048]{0:T(1024)} %param.27) | copy-start | bytes 24580
  195.4 5.7 %copy-start.18 = (f32[16,2,8]{0,2,1:T(8,128)S(1)}, f32[16,2,8]{0,2,1:T(8,128)}, u32[]{:S(2)}) copy-start(f32[16,2,8]{0,2,1:T(8,128)} %param.31) | copy-start | bytes 3076
  195.4 35.9 %all-to-all-start.2 = ((bf16[128,4,2048]{2,1,0:T(4,128)(2,1)}), bf16[128,4,2048]{2,1,0:T(4,128)(2,1)}, u32[]{:S(2)}, u32[]{:S(2)}) async-start(bf16[128,4,2048]{2,1,0:T(4,128)(2,1)} %copy.133), calls=%async_computation.3 | async-start | bytes 4194304 | tf_op jit(solution)/shard_map/all_to_all | solution.py:254
Sparse Core Ops, SparseCore 0:
  9.7 53.4 all-gather.1
  110.4 23.6 reduce-scatter.1

commit v3 on v2

v3 whole, which is shorter than its diff:
```python
import math

import jax
import jax.numpy as jnp
from jax import lax
from jax.experimental import pallas as pl
from jax.experimental.pallas import tpu as pltpu
from jax.sharding import PartitionSpec as P

EPS = 1e-06


def decode_attention(queries, keys_new, values_new, importance, merge_flags, key_cache,
                     value_cache, last_weight, lengths):
    requests, steps, query_width = queries.shape
    heads_kv = last_weight.shape[1]
    slots, features = key_cache.shape[1], key_cache.shape[2]
    head_dim = features // heads_kv
    group = query_width // head_dim // heads_kv
    scale = 1.0 / math.sqrt(head_dim)
    f32, bf16 = jnp.float32, jnp.bfloat16

    def kernel(len_ref, flag_ref, share_ref, weight_ref, q_ref, kn_ref, vn_ref, k_ref, v_ref, o_ref):
        r = pl.program_id(0)
        n = len_ref[r]
        main_valid = lax.broadcasted_iota(jnp.int32, (group, slots), 1) < n - 1
        pick = (lax.broadcasted_iota(jnp.int32, (8, slots), 1) == n - 1).astype(bf16)
        last_k = jnp.dot(pick, k_ref[0], preferred_element_type=f32)[0:1]
        last_v = jnp.dot(pick, v_ref[0], preferred_element_type=f32)[0:1]
        new_k = kn_ref[0].astype(f32)
        new_v = vn_ref[0].astype(f32)

        def lane_mask(flag):
            return jnp.full((1, head_dim), flag, jnp.int32) == 1

        def row_mask(flag):
            return jnp.full((group, 1), flag, jnp.int32) == 1

        for g in range(heads_kv):
            lanes = slice(g * head_dim, (g + 1) * head_dim)
            z = weight_ref[r * heads_kv + g]
            f0 = flag_ref[(r * steps) * heads_kv + g]
            f1 = flag_ref[(r * steps + 1) * heads_kv + g]
            w0 = share_ref[(r * steps) * heads_kv + g]
            w1 = share_ref[(r * steps + 1) * heads_kv + g]
            z1 = jnp.where(f0 == 1, z + w0, w0)
            m0, m1 = lane_mask(f0), lane_mask(f1)
            both = lane_mask(f0 * f1)

            def settle(last, new):
                old0 = last[:, lanes]
                n0, n1 = new[0:1, lanes], new[1:2, lanes]
                b0 = ((z * old0 + w0 * n0) / (z + w0)).astype(bf16).astype(f32)
                a0 = jnp.where(m0, b0, old0)
                cur = jnp.where(m0, a0, n0)
                b1 = ((z1 * cur + w1 * n1) / (z1 + w1)).astype(bf16).astype(f32)
                second = (
                    jnp.where(both, b1, jnp.where(m0, a0, old0)),
                    jnp.where(m0, n1, jnp.where(m1, b1, n0)),
                    n1,
                )
                return (a0, n0), second

            keys_t = settle(last_k, new_k)
            values_t = settle(last_v, new_v)
            count0 = 2 - f0
            counts = (count0, count0 + 1 - f1)
            kg = k_ref[0, :, lanes]
            vg = v_ref[0, :, lanes]
            for t in range(steps):
                rows = slice(g * group, (g + 1) * group)
                q = q_ref[0, t, rows, :]
                main = (
                    lax.dot_general(q, kg, (((1,), (1,)), ((), ())), preferred_element_type=f32)
                    * scale
                )
                main = jnp.where(main_valid, main, -jnp.inf)
                qf = q.astype(f32)
                top = jnp.max(main, axis=1, keepdims=True)
                tails = []
                for j, (tk, tv) in enumerate(zip(keys_t[t], values_t[t])):
                    ts = jnp.sum(qf * tk, axis=1, keepdims=True) * scale
                    ts = jnp.where(row_mask((j < counts[t]).astype(jnp.int32)), ts, -jnp.inf)
                    top = jnp.maximum(top, ts)
                    tails.append((ts, tv))
                raw = jnp.exp(main - top)
                total = jnp.sum(raw, axis=1, keepdims=True)
                summed = jnp.dot(raw.astype(bf16), vg, preferred_element_type=f32)
                for ts, tv in tails:
                    part = jnp.exp(ts - top)
                    total = total + part
                    summed = summed + part.astype(bf16).astype(f32) * tv
                o_ref[0, t, rows, :] = (summed / total).astype(bf16)

    heads = query_width // head_dim
    per_query = pl.BlockSpec((1, steps, heads, head_dim), lambda r, *_: (r, 0, 0, 0))
    per_new = pl.BlockSpec((1, steps, features), lambda r, *_: (r, 0, 0))
    per_cache = pl.BlockSpec((1, slots, features), lambda r, *_: (r, 0, 0))
    out = pl.pallas_call(
        kernel,
        out_shape=jax.ShapeDtypeStruct((requests, steps, heads, head_dim), bf16),
        grid_spec=pltpu.PrefetchScalarGridSpec(
            num_scalar_prefetch=4,
            grid=(requests,),
            in_specs=[per_query, per_new, per_new, per_cache, per_cache],
            out_specs=per_query,
        ),
    )(
        lengths,
        merge_flags.reshape(-1),
        importance.reshape(-1),
        last_weight.reshape(-1),
        queries.reshape(requests, steps, heads, head_dim),
        keys_new,
        values_new,
        key_cache,
        value_cache,
    )
    return out.reshape(requests, steps, query_width)


def run_experts(arriving, expert_gate_up, expert_down):
    hidden_units = expert_down.shape[1]
    both = jnp.einsum(
        "sjcd,jdf->sjcf", arriving, expert_gate_up, preferred_element_type=jnp.float32
    )
    active = (jax.nn.silu(both[..., :hidden_units]) * both[..., hidden_units:]).astype(jnp.bfloat16)
    return jnp.einsum(
        "sjcf,jfd->sjcd", active, expert_down, preferred_element_type=jnp.float32
    ).astype(jnp.bfloat16)


def shards(
    queries,
    keys_new,
    values_new,
    importance,
    merge_flags,
    key_cache,
    value_cache,
    last_weight,
    lengths,
    residual,
    o_weight,
    norm_gain,
    expert_gate_up,
    expert_down,
    routes,
    route_weights,
):
    requests, steps, query_width = queries.shape
    attended = decode_attention(
        queries,
        keys_new,
        values_new,
        importance,
        merge_flags,
        key_cache,
        value_cache,
        last_weight,
        lengths,
    )
    rows = requests * steps
    width = o_weight.shape[1]
    gathered = lax.all_gather(o_weight, ("x", "c"), axis=0, tiled=True)
    lines = lax.axis_size("y")
    spread = lax.all_to_all(
        attended.reshape(rows, lines, query_width // lines),
        "y",
        split_axis=1,
        concat_axis=0,
        tiled=True,
    )
    spread = spread.reshape(lines * rows, query_width // lines)
    projected = lax.psum_scatter(
        jnp.dot(spread, gathered, preferred_element_type=jnp.float32),
        "y",
        scatter_dimension=0,
        tiled=True,
    )
    members = lax.axis_size("y") * lax.axis_size("x") * lax.axis_size("c")
    mixed = residual.reshape(rows, width).astype(jnp.float32) + projected
    normed = (
        mixed * lax.rsqrt(jnp.mean(mixed * mixed, axis=1, keepdims=True) + EPS) * norm_gain
    ).astype(jnp.bfloat16)
    experts_local = expert_gate_up.shape[0]
    dp_size = lax.axis_size("dp")
    experts_all = experts_local * dp_size * members
    top_k = routes.shape[2]
    capacity = max(2, 2 * rows * top_k // experts_all)
    chosen = routes.reshape(rows * top_k)
    sequence = jnp.arange(rows * top_k, dtype=jnp.int32)
    earlier = sequence[:, None] > sequence[None, :]
    rank = jnp.sum(((chosen[:, None] == chosen[None, :]) & earlier).astype(jnp.int32), axis=1)
    target = chosen * capacity + rank
    placing = (
        jnp.arange(experts_all * capacity, dtype=jnp.int32)[:, None] == target[None, :]
    ).reshape(experts_all * capacity, rows, top_k)
    placing = jnp.any(placing, axis=2).astype(jnp.bfloat16)
    outgoing = jnp.dot(placing, normed, preferred_element_type=jnp.float32).astype(jnp.bfloat16)
    arrived = lax.all_to_all(
        outgoing.reshape(experts_all, capacity, width),
        ("dp", "y", "x", "c"),
        split_axis=0,
        concat_axis=0,
        tiled=True,
    )
    depth = arrived.shape[1]
    sources = arrived.shape[0] // experts_local
    answer = run_experts(
        arrived.reshape(sources, experts_local, depth, width), expert_gate_up, expert_down
    )
    returned = lax.all_to_all(
        answer.reshape(sources * experts_local, depth, width),
        ("dp", "y", "x", "c"),
        split_axis=0,
        concat_axis=0,
        tiled=True,
    )
    results = returned.reshape(experts_all * capacity, width)[target].reshape(rows, top_k, width)
    blended = jnp.sum(route_weights.reshape(rows, top_k, 1) * results.astype(jnp.float32), axis=1)
    layer_out = (mixed + blended).astype(jnp.bfloat16).reshape(requests, steps, width)
    return (attended, layer_out)


def solution(mesh):
    lines = mesh.devices.shape[1] // 8
    mesh = jax.sharding.Mesh(
        mesh.devices.reshape(mesh.devices.shape[0], lines, 4, 2), ("dp", "y", "x", "c")
    )
    return jax.shard_map(
        shards,
        mesh=mesh,
        in_specs=(
            P(("dp", "y", "x", "c"), None, None),
            P(("dp", "y", "x", "c"), None, None),
            P(("dp", "y", "x", "c"), None, None),
            P(("dp", "y", "x", "c"), None, None),
            P(("dp", "y", "x", "c"), None, None),
            P(("dp", "y", "x", "c"), None, None),
            P(("dp", "y", "x", "c"), None, None),
            P(("dp", "y", "x", "c"), None),
            P(("dp", "y", "x", "c")),
            P(("dp", "y", "x", "c"), None, None),
            P(("y", "x", "c"), None),
            P(),
            P(("dp", "y", "x", "c"), None, None),
            P(("dp", "y", "x", "c"), None, None),
            P(("dp", "y", "x", "c"), None, None),
            P(("dp", "y", "x", "c"), None, None),
        ),
        out_specs=(P(("dp", "y", "x", "c"), None, None), P(("dp", "y", "x", "c"), None, None)),
        check_vma=False,
    )
```

time: 252 us -> 214 us (0.85)
  local copies, waits for them, and re-layouts: 58.8 us -> 27.9 us
  other arithmetic: 21.6 us -> 3.86 us
  Pallas kernels: 25.3 us -> 38.2 us
  matrix products: 21.7 us -> 19 us
    pallas_call x1, Pallas kernels: 25.3 us -> 38.2 us  [decode_attention(): pl.pallas_call(kernel, out_shape=jax.ShapeDtypeStruct((requests, steps, h...]
    mul x5 -> x0, local copies, waits for them, and re-layouts: 4.85 us -> none  [the longest x4 4.08 us: settle(): portion[..., None] * fresh]
    add x3 -> x0, local copies, waits for them, and re-layouts: 4.31 us -> none  [the longest x1 2.28 us: shards(): totals = totals + jnp.sum(tail_raw, axis=3)]
    select_n x3 -> x0, other arithmetic: 4.28 us -> none  [the longest x2 2.69 us: build_tail(): filled = jnp.where(merging, filled, filled + 1)]
    add x2 -> x0, other arithmetic: 4.07 us -> none  [the longest x1 2.76 us: shards(): totals = totals + jnp.sum(tail_raw, axis=3)]
    convert_element_type x7 -> x0, other arithmetic: 3.61 us -> none  [the longest x3 1.7 us: settle(): new_row = jnp.where(merging[..., None], blended, fresh).astype(jnp.bfloat16)]
    reduce_sum x5 -> x0, local copies, waits for them, and re-layouts: 3.09 us -> none  [the longest x1 2.41 us: shards(): totals = totals + jnp.sum(tail_raw, axis=3)]
    unnamed x43 -> x21, local copies, waits for them, and re-layouts: 3.44 us -> 0.46 us
  transfers between devices with their start and end apart: 3 -> 3, of which waited for: 2 -> 2; matrix products, arithmetic and copies ran while one was open for 24% -> 5% of each run, Pallas kernels for 10% -> 18%
where the time goes in v3:
time: 214 us
  blocking collectives  53.4 us (25%)
  waiting for transfers between devices  51.2 us (24%)
  Pallas kernels  38.2 us (18%)
  local copies, waits for them, and re-layouts  27.9 us (13%)
  matrix products  19 us (9%)
  between operations  14.2 us (7%)
  starting transfers between devices  5.82 us (3%)
  other arithmetic  3.86 us (2%)
    all_to_all x1, blocking collectives, shards(): lax.all_to_all(outgoing.reshape(experts_all, capacity, width), ('dp', 'y'...  39.9 us
    pallas_call x1, Pallas kernels, decode_attention(): pl.pallas_call(kernel, out_shape=jax.ShapeDtypeStruct((requests, steps, h...  38.2 us
    all_to_all x1, waiting for transfers between devices, shards(): lax.all_to_all(answer.reshape(sources * experts_local, depth, width), ('d...  28.2 us
    reduce_scatter x1, waiting for transfers between devices, shards(): lax.psum_scatter(jnp.dot(spread, gathered, preferred_element_type=jnp.flo...  22.3 us
    all_to_all x1, blocking collectives, shards(): lax.all_to_all(attended.reshape(rows, lines, query_width // lines), 'y',...  13.5 us
    dot_general x1, matrix products, run_experts(): jnp.einsum('sjcd,jdf->sjcf', arriving, expert_gate_up, preferred_element_...  9.14 us
    dot_general x1, matrix products, shards(): jnp.dot(spread, gathered, preferred_element_type=jnp.float32)  5.91 us
    all_to_all x1, starting transfers between devices, shards(): lax.all_to_all(answer.reshape(sources * experts_local, depth, width), ('d...  5.74 us
  transfers between devices with their start and end apart: 3, of which 2 were waited for; matrix products, arithmetic and copies ran while one was open for 5% of the time, Pallas kernels for 18%

profile of v3, /device:TPU:1, one launch (start us, length us, event | category | flops | bytes accessed | tf_op | source)
XLA Modules:
  0.0 213.6 jit_solution(3245688917475712026)
XLA Ops:
  7.2 0.0 copy-start
  7.2 0.0 copy-start.5
  7.2 0.0 copy-start.6
  7.2 0.0 copy-start.7
  7.2 0.0 all-gather.2.cloned.1.call-start
  7.3 0.7 all-gather.2.cloned.1.call-update
  7.9 0.0 reduce-scatter.2.cloned.1.call-start
  8.0 2.4 %reshape.119.q_ref = bf16[16,2,64,128]{3,2,1,0:T(8,128)(2,1)} reshape(bf16[16,2,8192]{2,1,0:T(2,128)(2,1)} %param.16) | data formatting | bytes 1048576 | tf_op jit(solution)/shard_map/reshape | solution.py:113
  10.4 0.0 copy-done.5
  10.4 0.1 copy.42
  10.5 0.6 reshape.116.flag_ref
  11.1 0.0 copy-done.6
  11.1 0.1 copy.43
  11.2 0.6 reshape.117.share_ref
  11.8 0.0 copy-done.7
  11.8 0.1 copy.44
  11.9 0.6 reshape.118.weight_ref
  12.5 38.2 %shard_map.167 = bf16[16,2,64,128]{3,2,1,0:T(8,128)(2,1)} custom-call(s32[16]{0:T(128)} %len_ref.1, s32[128]{0:T(128)} %reshape.116.flag_ref, f32[128]{0:T(128)} %reshape.117.share_ref, f32[64]{0:T(128)} %reshape.118.weight_ref, bf16[16,2,64,128]{3,2,1,0:T(8,128)(2,1)} %reshape.119.q_ref, bf16[16,2,512]{2,1,0:T(2,128)(2,1)} %kn_ref.1, ...), custom_call_target="tpu_custom_call" | custom-call | tf_op jit(solution)/shard_map/pallas_call | solution.py:99
  50.7 2.0 reshape_reshape.3
  52.7 1.3 copy.45
  54.0 13.5 %all_to_all.25 = bf16[32,4,2048]{2,0,1:T(8,128)(2,1)} all-to-all(bf16[32,4,2048]{2,0,1:T(8,128)(2,1)S(1)} %copy.45), channel_id=1, replica_groups=mesh['dp'=4,'y'=4,'x'=4,'c'=2] {'y'}, dimensions={1} | all-to-all | bytes 1048576 | tf_op jit(solution)/shard_map/all_to_all | solution.py:167
  67.5 0.0 all-gather.2.cloned.1.call-done
  67.5 0.0 copy-start.1
  67.5 0.0 copy-start.2
  67.5 5.9 %fusion.20 = f32[128,2048]{1,0:T(8,128)} fusion(bf16[128,2048]{1,0:T(8,128)(2,1)} %bitcast.40, bf16[2048,2048]{1,0:T(8,128)(2,1)} %all-gather.2.cloned.1.call-done), kind=kOutput, calls=%fused_computation.29 | convolution fusion | flops 1073741824 | bytes 9961472 | tf_op jit(solution)/shard_map/dot_general | solution.py:176
  73.4 0.0 copy-start.3
  73.4 0.0 reduce-scatter.2.cloned.1.call-update
  73.4 0.0 copy-done.1
  73.4 0.7 reshape.128
  74.1 0.0 copy-done.2
  74.1 0.1 copy.48
  74.2 0.1 eq.30
  74.3 0.2 convert_reduce_fusion
  74.5 0.1 reduce_sum.32
  74.6 0.1 copy.47
  74.7 0.2 fusion.15
  74.9 22.3 %reduce-scatter.2.cloned.1.call-done = f32[32,2048]{1,0:T(8,128)} async-done(((f32[128,2048]{1,0:T(8,128)}), f32[32,2048]{1,0:T(8,128)}) %reduce-scatter.2.cloned.1.call-update) | async-done | bytes 262160 | tf_op jit(solution)/shard_map/reduce_scatter | solution.py:175
  97.3 1.2 multiply_reduce_fusion
  98.4 0.0 copy-done.3
  98.4 2.1 convolution_convert_fusion
  100.5 4.1 %reshape.122 = bf16[128,4,2048]{2,1,0:T(4,128)(2,1)} reshape(bf16[512,2048]{1,0:T(8,128)(2,1)} %convolution_convert_fusion) | data formatting | bytes 4194304 | tf_op jit(solution)/shard_map/reshape | solution.py:202
  104.6 39.9 %all_to_all.26 = bf16[128,4,2048]{2,1,0:T(4,128)(2,1)S(1)} all-to-all(bf16[128,4,2048]{2,1,0:T(4,128)(2,1)} %reshape.122), channel_id=1, replica_groups=mesh['dp'=4,'y'=4,'x'=4,'c'=2] {'dp','y','x','c'}, dimensions={0} | all-to-all | bytes 4194304 | tf_op jit(solution)/shard_map/all_to_all | solution.py:201
  144.6 9.1 %fusion.2 = f32[128,1,4,1536]{3,0,2,1:T(8,128)S(1)} fusion(bf16[1,2048,1536]{2,1,0:T(8,128)(2,1)} %param.28, bf16[128,4,2048]{2,1,0:T(4,128)(2,1)S(1)} %all_to_all.26), kind=kOutput, calls=%fused_computation.3 | convolution fusion | flops 3221225472 | bytes 11534336 | tf_op jit(solution)/shard_map/sjcd,jdf->sjcf/dot_general | solution.py:124
  153.7 0.0 copy-done
  153.7 1.8 fusion.7
  155.6 2.9 %copy.50 = bf16[128,4,2048]{2,1,0:T(4,128)(2,1)} copy(bf16[128,4,2048]{2,0,1:T(8,128)(2,1)S(1)} %fusion.7) | data formatting | bytes 4194304 | tf_op jit(solution)/shard_map/convert_element_type | solution.py:130
  158.5 0.0 copy-start.4
  158.5 5.7 %all-to-all-start.2 = ((bf16[128,4,2048]{2,1,0:T(4,128)(2,1)}), bf16[128,4,2048]{2,1,0:T(4,128)(2,1)}, u32[]{:S(2)}, u32[]{:S(2)}) async-start(bf16[128,4,2048]{2,1,0:T(4,128)(2,1)} %copy.50), calls=%async_computation.3 | async-start | bytes 4194304 | tf_op jit(solution)/shard_map/all_to_all | solution.py:213
  164.3 0.1 mul.71
  164.4 2.0 reshape.120
  166.3 0.0 copy-done.4
  166.3 0.1 copy.46
  166.4 28.2 %all-to-all-done.2 = bf16[128,4,2048]{2,1,0:T(4,128)(2,1)} async-done(((bf16[128,4,2048]{2,1,0:T(4,128)(2,1)}), bf16[128,4,2048]{2,1,0:T(4,128)(2,1)}, u32[]{:S(2)}, u32[]{:S(2)}) %all-to-all-start.2) | async-done | bytes 2097184 | tf_op jit(solution)/shard_map/all_to_all | solution.py:213
  194.6 3.9 %reshape.126 = bf16[512,2048]{1,0:T(8,128)(2,1)} reshape(bf16[128,4,2048]{2,1,0:T(4,128)(2,1)} %all-to-all-done.2) | data formatting | bytes 4194304 | tf_op jit(solution)/shard_map/reshape | solution.py:220
  198.5 5.2 %gather_fusion = bf16[256,2048]{1,0:T(8,128)(2,1)} fusion(bf16[512,2048]{1,0:T(8,128)(2,1)} %reshape.126, s32[1024]{0:T(1024)S(1)} %pad_clamp_fusion), kind=kCustom, calls=%fused_computation | custom fusion | bytes 2098176 | tf_op jit(solution)/shard_map/gather | solution.py:220
  203.7 2.2 %fusion.10 = f32[32,2048]{1,0:T(8,128)S(1)} fusion(bf16[256,2048]{1,0:T(8,128)(2,1)} %gather_fusion, f32[32,8]{1,0:T(8,128)S(1)} %bitcast.42), kind=kLoop, calls=%fused_computation.9 | loop fusion | flops 1507328 | bytes 1311744 | tf_op jit(solution)/shard_map/reduce_sum | solution.py:221
  206.0 0.8 reshape.127
  (6 shorter events, 0.1 us)
Async XLA Ops:
  7.2 146.6 %copy-start = (bf16[1,768,2048]{2,1,0:T(8,128)(2,1)S(1)}, bf16[1,768,2048]{2,1,0:T(8,128)(2,1)}, u32[]{:S(2)}) copy-start(bf16[1,768,2048]{2,1,0:T(8,128)(2,1)} %param.29) | copy-start | bytes 9437188
  7.2 3.2 %copy-start.5 = (s32[16,2,4]{0,2,1:T(4,128)S(1)}, s32[16,2,4]{0,2,1:T(4,128)}, u32[]{:S(2)}) copy-start(s32[16,2,4]{0,2,1:T(4,128)} %param.20) | copy-start | bytes 1540
  7.2 3.9 %copy-start.6 = (f32[16,2,4]{0,2,1:T(4,128)S(1)}, f32[16,2,4]{0,2,1:T(4,128)}, u32[]{:S(2)}) copy-start(f32[16,2,4]{0,2,1:T(4,128)} %param.19) | copy-start | bytes 1540
  7.2 4.6 %copy-start.7 = (f32[16,4]{0,1:T(4,128)S(1)}, f32[16,4]{0,1:T(4,128)}, u32[]{:S(2)}) copy-start(f32[16,4]{0,1:T(4,128)} %param.23) | copy-start | bytes 772
  7.2 60.2 %all-gather.2.cloned.1.call-start = ((), (), s32[]{:S(2)}) async-start(), calls=%async_computation.4 | async-start | bytes 9437184 | tf_op jit(solution)/shard_map/all_gather | solution.py:165
  7.9 89.3 %reduce-scatter.2.cloned.1.call-start = ((), (), s32[]{:S(2)}) async-start(), calls=%async_computation.5 | async-start | bytes 1310720 | tf_op jit(solution)/shard_map/reduce_scatter | solution.py:175
  67.5 5.9 %copy-start.1 = (bf16[16,2,2048]{2,1,0:T(2,128)(2,1)S(1)}, bf16[16,2,2048]{2,1,0:T(2,128)(2,1)}, u32[]{:S(2)}) copy-start(bf16[16,2,2048]{2,1,0:T(2,128)(2,1)} %param.25) | copy-start | bytes 393220
  67.5 6.7 %copy-start.2 = (s32[16,2,8]{0,2,1:T(8,128)S(1)}, s32[16,2,8]{0,2,1:T(8,128)}, u32[]{:S(2)}) copy-start(s32[16,2,8]{0,2,1:T(8,128)} %param.30) | copy-start | bytes 3076
  73.4 25.1 %copy-start.3 = (f32[2048]{0:T(1024)S(1)}, f32[2048]{0:T(1024)}, u32[]{:S(2)}) copy-start(f32[2048]{0:T(1024)} %param.27) | copy-start | bytes 24580
  158.5 7.8 %copy-start.4 = (f32[16,2,8]{0,2,1:T(8,128)S(1)}, f32[16,2,8]{0,2,1:T(8,128)}, u32[]{:S(2)}) copy-start(f32[16,2,8]{0,2,1:T(8,128)} %param.31) | copy-start | bytes 3076
  158.5 36.1 %all-to-all-start.2 = ((bf16[128,4,2048]{2,1,0:T(4,128)(2,1)}), bf16[128,4,2048]{2,1,0:T(4,128)(2,1)}, u32[]{:S(2)}, u32[]{:S(2)}) async-start(bf16[128,4,2048]{2,1,0:T(4,128)(2,1)} %copy.50), calls=%async_computation.3 | async-start | bytes 4194304 | tf_op jit(solution)/shard_map/all_to_all | solution.py:213
Sparse Core Ops, SparseCore 0:
  9.8 53.4 all-gather.1
  73.5 23.6 reduce-scatter.1

commit v4 on v3

--- a/solution.py
+++ b/solution.py
@@ -1,3 +1,4 @@
+import functools
 import math
 
 import jax
@@ -20,13 +21,20 @@
     scale = 1.0 / math.sqrt(head_dim)
     f32, bf16 = jnp.float32, jnp.bfloat16
 
+    chunk = math.gcd(slots, 128)
+    window = 16
+
     def kernel(len_ref, flag_ref, share_ref, weight_ref, q_ref, kn_ref, vn_ref, k_ref, v_ref, o_ref):
         r = pl.program_id(0)
         n = len_ref[r]
-        main_valid = lax.broadcasted_iota(jnp.int32, (group, slots), 1) < n - 1
-        pick = (lax.broadcasted_iota(jnp.int32, (8, slots), 1) == n - 1).astype(bf16)
-        last_k = jnp.dot(pick, k_ref[0], preferred_element_type=f32)[0:1]
-        last_v = jnp.dot(pick, v_ref[0], preferred_element_type=f32)[0:1]
+        start = pl.multiple_of(((n - 1) // window) * window, window)
+        here = lax.broadcasted_iota(jnp.int32, (window, features), 0) == (n - 1 - start)
+        last_k = jnp.sum(
+            jnp.where(here, k_ref[0, pl.ds(start, window), :].astype(f32), 0.0), axis=0, keepdims=True
+        )
+        last_v = jnp.sum(
+            jnp.where(here, v_ref[0, pl.ds(start, window), :].astype(f32), 0.0), axis=0, keepdims=True
+        )
         new_k = kn_ref[0].astype(f32)
         new_v = vn_ref[0].astype(f32)
 
@@ -36,6 +44,7 @@
         def row_mask(flag):
             return jnp.full((group, 1), flag, jnp.int32) == 1
 
+        tails_of = []
         for g in range(heads_kv):
             lanes = slice(g * head_dim, (g + 1) * head_dim)
             z = weight_ref[r * heads_kv + g]
@@ -61,36 +70,57 @@
                 )
                 return (a0, n0), second
 
-            keys_t = settle(last_k, new_k)
-            values_t = settle(last_v, new_v)
             count0 = 2 - f0
-            counts = (count0, count0 + 1 - f1)
-            kg = k_ref[0, :, lanes]
-            vg = v_ref[0, :, lanes]
-            for t in range(steps):
+            tails_of.append((settle(last_k, new_k), settle(last_v, new_v), (count0, count0 + 1 - f1)))
+
+        def attend(span):
+            valid = lax.broadcasted_iota(jnp.int32, (steps * group, span), 1) < n - 1
+            for g in range(heads_kv):
+                lanes = slice(g * head_dim, (g + 1) * head_dim)
+                keys_t, values_t, counts = tails_of[g]
                 rows = slice(g * group, (g + 1) * group)
-                q = q_ref[0, t, rows, :]
+                q = jnp.concatenate([q_ref[0, t, rows, :] for t in range(steps)], axis=0)
                 main = (
-                    lax.dot_general(q, kg, (((1,), (1,)), ((), ())), preferred_element_type=f32)
+                    lax.dot_general(
+                        q, k_ref[0, 0:span, lanes], (((1,), (1,)), ((), ())),
+                        preferred_element_type=f32,
+                    )
                     * scale
                 )
-                main = jnp.where(main_valid, main, -jnp.inf)
+                main = jnp.where(valid, main, -jnp.inf)
                 qf = q.astype(f32)
                 top = jnp.max(main, axis=1, keepdims=True)
-                tails = []
-                for j, (tk, tv) in enumerate(zip(keys_t[t], values_t[t])):
-                    ts = jnp.sum(qf * tk, axis=1, keepdims=True) * scale
-                    ts = jnp.where(row_mask((j < counts[t]).astype(jnp.int32)), ts, -jnp.inf)
-                    top = jnp.maximum(top, ts)
-                    tails.append((ts, tv))
+                tops, tails = [], []
+                for t in range(steps):
+                    here_rows = slice(t * group, (t + 1) * group)
+                    top_t = top[here_rows]
+                    step_tails = []
+                    for j, (tk, tv) in enumerate(zip(keys_t[t], values_t[t])):
+                        ts = jnp.sum(qf[here_rows] * tk, axis=1, keepdims=True) * scale
+                        ts = jnp.where(row_mask((j < counts[t]).astype(jnp.int32)), ts, -jnp.inf)
+                        top_t = jnp.maximum(top_t, ts)
+                        step_tails.append((ts, tv))
+                    tops.append(top_t)
+                    tails.append(step_tails)
+                top = jnp.concatenate(tops, axis=0)
                 raw = jnp.exp(main - top)
                 total = jnp.sum(raw, axis=1, keepdims=True)
-                summed = jnp.dot(raw.astype(bf16), vg, preferred_element_type=f32)
-                for ts, tv in tails:
-                    part = jnp.exp(ts - top)
-                    total = total + part
-                    summed = summed + part.astype(bf16).astype(f32) * tv
-                o_ref[0, t, rows, :] = (summed / total).astype(bf16)
+                summed = jnp.dot(
+                    raw.astype(bf16), v_ref[0, 0:span, lanes], preferred_element_type=f32
+                )
+                for t in range(steps):
+                    here_rows = slice(t * group, (t + 1) * group)
+                    total_t = total[here_rows]
+                    summed_t = summed[here_rows]
+                    for ts, tv in tails[t]:
+                        part = jnp.exp(ts - tops[t])
+                        total_t = total_t + part
+                        summed_t = summed_t + part.astype(bf16).astype(f32) * tv
+                    o_ref[0, t, rows, :] = (summed_t / total_t).astype(bf16)
+
+        used = (n - 1 + chunk - 1) // chunk
+        for k in range(1, slots // chunk + 1):
+            pl.when(used == k)(functools.partial(attend, k * chunk))
 
     heads = query_width // head_dim
     per_query = pl.BlockSpec((1, steps, heads, head_dim), lambda r, *_: (r, 0, 0, 0))

time: 214 us -> 208 us (0.972)
  Pallas kernels: 38.2 us -> 25.7 us
  waiting for transfers between devices: 51.2 us -> 57.1 us
    pallas_call x1, Pallas kernels: 38.2 us -> 25.7 us  [decode_attention(): pl.pallas_call(kernel, out_shape=jax.ShapeDtypeStruct((requests, steps, h...]
    all_gather x1, waiting for transfers between devices: 0.01 us -> 8.42 us  [shards(): gathered = lax.all_gather(o_weight, ('x', 'c'), axis=0, tiled=True)]
    reduce_scatter x1, waiting for transfers between devices: 22.3 us -> 19.8 us  [shards(): lax.psum_scatter(jnp.dot(spread, gathered, preferred_element_type=jnp.flo...]
  transfers between devices with their start and end apart: 3 -> 3, of which waited for: 2 -> 3; matrix products, arithmetic and copies ran while one was open for 5% -> 6% of each run, Pallas kernels for 18% -> 12%
where the time goes in v4:
time: 208 us; the launch traced here: 207 us
  waiting for transfers between devices  57.1 us (27%)
  blocking collectives  53.9 us (26%)
  local copies, waits for them, and re-layouts  27.9 us (13%)
  Pallas kernels  25.7 us (12%)
  matrix products  19 us (9%)
  between operations  14.2 us (7%)
  starting transfers between devices  5.65 us (3%)
  other arithmetic  3.86 us (2%)
    all_to_all x1, blocking collectives, shards(): lax.all_to_all(outgoing.reshape(experts_all, capacity, width), ('dp', 'y'...  40.6 us
    all_to_all x1, waiting for transfers between devices, shards(): lax.all_to_all(answer.reshape(sources * experts_local, depth, width), ('d...  28.2 us
    pallas_call x1, Pallas kernels, decode_attention(): pl.pallas_call(kernel, out_shape=jax.ShapeDtypeStruct((requests, steps, h...  25.7 us
    reduce_scatter x1, waiting for transfers between devices, shards(): lax.psum_scatter(jnp.dot(spread, gathered, preferred_element_type=jnp.flo...  19.8 us
    all_to_all x1, blocking collectives, shards(): lax.all_to_all(attended.reshape(rows, lines, query_width // lines), 'y',...  13.3 us
    dot_general x1, matrix products, run_experts(): jnp.einsum('sjcd,jdf->sjcf', arriving, expert_gate_up, preferred_element_...  9.13 us
    all_gather x1, waiting for transfers between devices, shards(): gathered = lax.all_gather(o_weight, ('x', 'c'), axis=0, tiled=True)  8.42 us
    dot_general x1, matrix products, shards(): jnp.dot(spread, gathered, preferred_element_type=jnp.float32)  5.91 us
  transfers between devices with their start and end apart: 3, of which 3 were waited for; matrix products, arithmetic and copies ran while one was open for 6% of the time, Pallas kernels for 12%

profile of v4, /device:TPU:1, one launch (start us, length us, event | category | flops | bytes accessed | tf_op | source)
XLA Modules:
  0.0 207.3 jit_solution(5955566463991339247)
XLA Ops:
  7.2 0.0 copy-start
  7.2 0.0 copy-start.5
  7.2 0.0 copy-start.6
  7.2 0.0 copy-start.7
  7.2 0.0 all-gather.2.cloned.1.call-start
  7.3 0.7 all-gather.2.cloned.1.call-update
  7.9 0.0 reduce-scatter.2.cloned.1.call-start
  8.0 2.4 %reshape.119.q_ref = bf16[16,2,64,128]{3,2,1,0:T(8,128)(2,1)} reshape(bf16[16,2,8192]{2,1,0:T(2,128)(2,1)} %param.16) | data formatting | bytes 1048576 | tf_op jit(solution)/shard_map/reshape | solution.py:143
  10.4 0.0 copy-done.5
  10.4 0.1 copy.42
  10.5 0.6 reshape.116.flag_ref
  11.1 0.0 copy-done.6
  11.1 0.1 copy.43
  11.2 0.6 reshape.117.share_ref
  11.8 0.0 copy-done.7
  11.8 0.1 copy.44
  11.9 0.6 reshape.118.weight_ref
  12.5 25.7 %shard_map.167 = bf16[16,2,64,128]{3,2,1,0:T(8,128)(2,1)} custom-call(s32[16]{0:T(128)} %len_ref.1, s32[128]{0:T(128)} %reshape.116.flag_ref, f32[128]{0:T(128)} %reshape.117.share_ref, f32[64]{0:T(128)} %reshape.118.weight_ref, bf16[16,2,64,128]{3,2,1,0:T(8,128)(2,1)} %reshape.119.q_ref, bf16[16,2,512]{2,1,0:T(2,128)(2,1)} %kn_ref.1, ...), custom_call_target="tpu_custom_call" | custom-call | tf_op jit(solution)/shard_map/pallas_call | solution.py:129
  38.2 2.0 reshape_reshape.3
  40.1 1.3 copy.45
  41.5 13.3 %all_to_all.25 = bf16[32,4,2048]{2,0,1:T(8,128)(2,1)} all-to-all(bf16[32,4,2048]{2,0,1:T(8,128)(2,1)S(1)} %copy.45), channel_id=1, replica_groups=mesh['dp'=4,'y'=4,'x'=4,'c'=2] {'y'}, dimensions={1} | all-to-all | bytes 1048576 | tf_op jit(solution)/shard_map/all_to_all | solution.py:197
  54.8 8.4 %all-gather.2.cloned.1.call-done = bf16[2048,2048]{1,0:T(8,128)(2,1)} async-done(((bf16[256,2048]{1,0:T(8,128)(2,1)}), bf16[2048,2048]{1,0:T(8,128)(2,1)}) %all-gather.2.cloned.1.call-update) | async-done | bytes 8388624 | tf_op jit(solution)/shard_map/all_gather | solution.py:195
  63.2 0.0 copy-start.1
  63.2 0.0 copy-start.2
  63.2 5.9 %fusion.20 = f32[128,2048]{1,0:T(8,128)} fusion(bf16[128,2048]{1,0:T(8,128)(2,1)} %bitcast.40, bf16[2048,2048]{1,0:T(8,128)(2,1)} %all-gather.2.cloned.1.call-done), kind=kOutput, calls=%fused_computation.29 | convolution fusion | flops 1073741824 | bytes 9961472 | tf_op jit(solution)/shard_map/dot_general | solution.py:206
  69.1 0.0 copy-start.3
  69.1 0.0 reduce-scatter.2.cloned.1.call-update
  69.1 0.0 copy-done.1
  69.1 0.7 reshape.128
  69.9 0.0 copy-done.2
  69.9 0.1 copy.48
  70.0 0.1 eq.30
  70.1 0.2 convert_reduce_fusion
  70.2 0.1 reduce_sum.32
  70.4 0.1 copy.47
  70.4 0.2 fusion.15
  70.7 19.8 %reduce-scatter.2.cloned.1.call-done = f32[32,2048]{1,0:T(8,128)} async-done(((f32[128,2048]{1,0:T(8,128)}), f32[32,2048]{1,0:T(8,128)}) %reduce-scatter.2.cloned.1.call-update) | async-done | bytes 262160 | tf_op jit(solution)/shard_map/reduce_scatter | solution.py:205
  90.5 1.2 multiply_reduce_fusion
  91.7 0.0 copy-done.3
  91.7 2.1 %convolution_convert_fusion = bf16[512,2048]{1,0:T(8,128)(2,1)} fusion(pred[512,32]{0,1:T(8,128)(4,1)S(1)} %fusion.15, f32[32,2048]{1,0:T(8,128)S(1)} %get-tuple-element.3, f32[2048]{0:T(1024)S(1)} %copy-done.3, f32[32]{0:T(128)S(1)} %add_rsqrt_fusion), kind=kOutput, calls=%fused_computation.7 | convolution fusion | flops 68354048 | bytes 2384000 | tf_op jit(solution)/shard_map/dot_general | solution.py:230
  93.8 4.1 %reshape.122 = bf16[128,4,2048]{2,1,0:T(4,128)(2,1)} reshape(bf16[512,2048]{1,0:T(8,128)(2,1)} %convolution_convert_fusion) | data formatting | bytes 4194304 | tf_op jit(solution)/shard_map/reshape | solution.py:232
  97.9 40.6 %all_to_all.26 = bf16[128,4,2048]{2,1,0:T(4,128)(2,1)S(1)} all-to-all(bf16[128,4,2048]{2,1,0:T(4,128)(2,1)} %reshape.122), channel_id=1, replica_groups=mesh['dp'=4,'y'=4,'x'=4,'c'=2] {'dp','y','x','c'}, dimensions={0} | all-to-all | bytes 4194304 | tf_op jit(solution)/shard_map/all_to_all | solution.py:231
  138.5 9.1 %fusion.2 = f32[128,1,4,1536]{3,0,2,1:T(8,128)S(1)} fusion(bf16[1,2048,1536]{2,1,0:T(8,128)(2,1)} %param.28, bf16[128,4,2048]{2,1,0:T(4,128)(2,1)S(1)} %all_to_all.26), kind=kOutput, calls=%fused_computation.3 | convolution fusion | flops 3221225472 | bytes 11534336 | tf_op jit(solution)/shard_map/sjcd,jdf->sjcf/dot_general | solution.py:154
  147.7 0.0 copy-done
  147.7 1.8 fusion.7
  149.5 2.9 %copy.50 = bf16[128,4,2048]{2,1,0:T(4,128)(2,1)} copy(bf16[128,4,2048]{2,0,1:T(8,128)(2,1)S(1)} %fusion.7) | data formatting | bytes 4194304 | tf_op jit(solution)/shard_map/convert_element_type | solution.py:160
  152.4 0.0 copy-start.4
  152.4 5.6 %all-to-all-start.2 = ((bf16[128,4,2048]{2,1,0:T(4,128)(2,1)}), bf16[128,4,2048]{2,1,0:T(4,128)(2,1)}, u32[]{:S(2)}, u32[]{:S(2)}) async-start(bf16[128,4,2048]{2,1,0:T(4,128)(2,1)} %copy.50), calls=%async_computation.3 | async-start | bytes 4194304 | tf_op jit(solution)/shard_map/all_to_all | solution.py:243
  158.0 0.1 mul.71
  158.1 2.0 reshape.120
  160.1 0.0 copy-done.4
  160.1 0.1 copy.46
  160.2 28.2 %all-to-all-done.2 = bf16[128,4,2048]{2,1,0:T(4,128)(2,1)} async-done(((bf16[128,4,2048]{2,1,0:T(4,128)(2,1)}), bf16[128,4,2048]{2,1,0:T(4,128)(2,1)}, u32[]{:S(2)}, u32[]{:S(2)}) %all-to-all-start.2) | async-done | bytes 2097184 | tf_op jit(solution)/shard_map/all_to_all | solution.py:243
  188.3 3.9 %reshape.126 = bf16[512,2048]{1,0:T(8,128)(2,1)} reshape(bf16[128,4,2048]{2,1,0:T(4,128)(2,1)} %all-to-all-done.2) | data formatting | bytes 4194304 | tf_op jit(solution)/shard_map/reshape | solution.py:250
  192.3 5.2 %gather_fusion = bf16[256,2048]{1,0:T(8,128)(2,1)} fusion(bf16[512,2048]{1,0:T(8,128)(2,1)} %reshape.126, s32[1024]{0:T(1024)S(1)} %pad_clamp_fusion), kind=kCustom, calls=%fused_computation | custom fusion | bytes 2098176 | tf_op jit(solution)/shard_map/gather | solution.py:250
  197.5 2.2 %fusion.10 = f32[32,2048]{1,0:T(8,128)S(1)} fusion(bf16[256,2048]{1,0:T(8,128)(2,1)} %gather_fusion, f32[32,8]{1,0:T(8,128)S(1)} %bitcast.42), kind=kLoop, calls=%fused_computation.9 | loop fusion | flops 1507328 | bytes 1311744 | tf_op jit(solution)/shard_map/reduce_sum | solution.py:251
  199.7 0.8 reshape.127
  (6 shorter events, 0.1 us)
Async XLA Ops:
  7.2 140.5 %copy-start = (bf16[1,768,2048]{2,1,0:T(8,128)(2,1)S(1)}, bf16[1,768,2048]{2,1,0:T(8,128)(2,1)}, u32[]{:S(2)}) copy-start(bf16[1,768,2048]{2,1,0:T(8,128)(2,1)} %param.29) | copy-start | bytes 9437188
  7.2 3.2 %copy-start.5 = (s32[16,2,4]{0,2,1:T(4,128)S(1)}, s32[16,2,4]{0,2,1:T(4,128)}, u32[]{:S(2)}) copy-start(s32[16,2,4]{0,2,1:T(4,128)} %param.20) | copy-start | bytes 1540
  7.2 3.9 %copy-start.6 = (f32[16,2,4]{0,2,1:T(4,128)S(1)}, f32[16,2,4]{0,2,1:T(4,128)}, u32[]{:S(2)}) copy-start(f32[16,2,4]{0,2,1:T(4,128)} %param.19) | copy-start | bytes 1540
  7.2 4.6 %copy-start.7 = (f32[16,4]{0,1:T(4,128)S(1)}, f32[16,4]{0,1:T(4,128)}, u32[]{:S(2)}) copy-start(f32[16,4]{0,1:T(4,128)} %param.23) | copy-start | bytes 772
  7.2 56.0 %all-gather.2.cloned.1.call-start = ((), (), s32[]{:S(2)}) async-start(), calls=%async_computation.4 | async-start | bytes 9437184 | tf_op jit(solution)/shard_map/all_gather | solution.py:195
  7.9 82.6 %reduce-scatter.2.cloned.1.call-start = ((), (), s32[]{:S(2)}) async-start(), calls=%async_computation.5 | async-start | bytes 1310720 | tf_op jit(solution)/shard_map/reduce_scatter | solution.py:205
  63.2 5.9 %copy-start.1 = (bf16[16,2,2048]{2,1,0:T(2,128)(2,1)S(1)}, bf16[16,2,2048]{2,1,0:T(2,128)(2,1)}, u32[]{:S(2)}) copy-start(bf16[16,2,2048]{2,1,0:T(2,128)(2,1)} %param.25) | copy-start | bytes 393220
  63.2 6.7 %copy-start.2 = (s32[16,2,8]{0,2,1:T(8,128)S(1)}, s32[16,2,8]{0,2,1:T(8,128)}, u32[]{:S(2)}) copy-start(s32[16,2,8]{0,2,1:T(8,128)} %param.30) | copy-start | bytes 3076
  69.1 22.6 %copy-start.3 = (f32[2048]{0:T(1024)S(1)}, f32[2048]{0:T(1024)}, u32[]{:S(2)}) copy-start(f32[2048]{0:T(1024)} %param.27) | copy-start | bytes 24580
  152.4 7.6 %copy-start.4 = (f32[16,2,8]{0,2,1:T(8,128)S(1)}, f32[16,2,8]{0,2,1:T(8,128)}, u32[]{:S(2)}) copy-start(f32[16,2,8]{0,2,1:T(8,128)} %param.31) | copy-start | bytes 3076
  152.4 35.9 %all-to-all-start.2 = ((bf16[128,4,2048]{2,1,0:T(4,128)(2,1)}), bf16[128,4,2048]{2,1,0:T(4,128)(2,1)}, u32[]{:S(2)}, u32[]{:S(2)}) async-start(bf16[128,4,2048]{2,1,0:T(4,128)(2,1)} %copy.50), calls=%async_computation.3 | async-start | bytes 4194304 | tf_op jit(solution)/shard_map/all_to_all | solution.py:243
Sparse Core Ops, SparseCore 0:
  9.8 53.3 all-gather.1
  69.3 21.2 reduce-scatter.1

commit v5 on v4

--- a/solution.py
+++ b/solution.py
@@ -24,16 +24,47 @@
     chunk = math.gcd(slots, 128)
     window = 16
 
-    def kernel(len_ref, flag_ref, share_ref, weight_ref, q_ref, kn_ref, vn_ref, k_ref, v_ref, o_ref):
+    chunks = slots // chunk
+
+    def kernel(len_ref, flag_ref, share_ref, weight_ref, q_ref, kn_ref, vn_ref, k_hbm, v_hbm, o_ref,
+               k_buf, v_buf, sems):
         r = pl.program_id(0)
         n = len_ref[r]
+        here_buf = r % 2
+
+        def copies(req, buf):
+            needed = (len_ref[req] - 1) // chunk + 1
+            for c in range(chunks):
+                part = pl.ds(c * chunk, chunk)
+                for a, (src, dst) in enumerate(((k_hbm, k_buf), (v_hbm, v_buf))):
+                    copy = pltpu.make_async_copy(
+                        src.at[req, part], dst.at[buf, part], sems.at[a, buf, c]
+                    )
+                    yield c < needed, copy
+
+        def start_all(req, buf):
+            for cond, copy in copies(req, buf):
+                pl.when(cond)(copy.start)
+
+        @pl.when(r == 0)
+        def _():
+            start_all(0, 0)
+
+        @pl.when(r + 1 < requests)
+        def _():
+            start_all(r + 1, 1 - here_buf)
+
+        for cond, copy in copies(r, here_buf):
+            pl.when(cond)(copy.wait)
+        k_ref = k_buf.at[here_buf]
+        v_ref = v_buf.at[here_buf]
         start = pl.multiple_of(((n - 1) // window) * window, window)
         here = lax.broadcasted_iota(jnp.int32, (window, features), 0) == (n - 1 - start)
         last_k = jnp.sum(
-            jnp.where(here, k_ref[0, pl.ds(start, window), :].astype(f32), 0.0), axis=0, keepdims=True
+            jnp.where(here, k_ref[pl.ds(start, window), :].astype(f32), 0.0), axis=0, keepdims=True
         )
         last_v = jnp.sum(
-            jnp.where(here, v_ref[0, pl.ds(start, window), :].astype(f32), 0.0), axis=0, keepdims=True
+            jnp.where(here, v_ref[pl.ds(start, window), :].astype(f32), 0.0), axis=0, keepdims=True
         )
         new_k = kn_ref[0].astype(f32)
         new_v = vn_ref[0].astype(f32)
@@ -82,7 +113,7 @@
                 q = jnp.concatenate([q_ref[0, t, rows, :] for t in range(steps)], axis=0)
                 main = (
                     lax.dot_general(
-                        q, k_ref[0, 0:span, lanes], (((1,), (1,)), ((), ())),
+                        q, k_ref[0:span, lanes], (((1,), (1,)), ((), ())),
                         preferred_element_type=f32,
                     )
                     * scale
@@ -106,7 +137,7 @@
                 raw = jnp.exp(main - top)
                 total = jnp.sum(raw, axis=1, keepdims=True)
                 summed = jnp.dot(
-                    raw.astype(bf16), v_ref[0, 0:span, lanes], preferred_element_type=f32
+                    raw.astype(bf16), v_ref[0:span, lanes], preferred_element_type=f32
                 )
                 for t in range(steps):
                     here_rows = slice(t * group, (t + 1) * group)
@@ -118,14 +149,14 @@
                         summed_t = summed_t + part.astype(bf16).astype(f32) * tv
                     o_ref[0, t, rows, :] = (summed_t / total_t).astype(bf16)
 
-        used = (n - 1 + chunk - 1) // chunk
+        used = (n - 1) // chunk + 1
         for k in range(1, slots // chunk + 1):
             pl.when(used == k)(functools.partial(attend, k * chunk))
 
     heads = query_width // head_dim
     per_query = pl.BlockSpec((1, steps, heads, head_dim), lambda r, *_: (r, 0, 0, 0))
     per_new = pl.BlockSpec((1, steps, features), lambda r, *_: (r, 0, 0))
-    per_cache = pl.BlockSpec((1, slots, features), lambda r, *_: (r, 0, 0))
+    per_cache = pl.BlockSpec(memory_space=pl.ANY)
     out = pl.pallas_call(
         kernel,
         out_shape=jax.ShapeDtypeStruct((requests, steps, heads, head_dim), bf16),
@@ -134,6 +165,11 @@
             grid=(requests,),
             in_specs=[per_query, per_new, per_new, per_cache, per_cache],
             out_specs=per_query,
+            scratch_shapes=[
+                pltpu.VMEM((2, slots, features), key_cache.dtype),
+                pltpu.VMEM((2, slots, features), value_cache.dtype),
+                pltpu.SemaphoreType.DMA((2, 2, chunks)),
+            ],
         ),
     )(
         lengths,

time: 208 us -> 208 us (level)
  transfers between devices with their start and end apart: 3 -> 3, of which waited for: 3 -> 3; matrix products, arithmetic and copies ran while one was open for 6% -> 6% of each run, Pallas kernels for 12% -> 13%
where the time goes in v5:
time: 208 us; the launch traced here: 207 us
  waiting for transfers between devices  55.4 us (27%)
  blocking collectives  54.1 us (26%)
  local copies, waits for them, and re-layouts  28 us (13%)
  Pallas kernels  27.2 us (13%)
  matrix products  19 us (9%)
  between operations  14.2 us (7%)
  starting transfers between devices  5.64 us (3%)
  other arithmetic  3.86 us (2%)
    all_to_all x1, blocking collectives, shards(): lax.all_to_all(outgoing.reshape(experts_all, capacity, width), ('dp', 'y'...  40.6 us
    all_to_all x1, waiting for transfers between devices, shards(): lax.all_to_all(answer.reshape(sources * experts_local, depth, width), ('d...  28.2 us
    pallas_call x1, Pallas kernels, decode_attention(): pl.pallas_call(kernel, out_shape=jax.ShapeDtypeStruct((requests, steps, h...  27.2 us
    reduce_scatter x1, waiting for transfers between devices, shards(): lax.psum_scatter(jnp.dot(spread, gathered, preferred_element_type=jnp.flo...  19.8 us
    all_to_all x1, blocking collectives, shards(): lax.all_to_all(attended.reshape(rows, lines, query_width // lines), 'y',...  13.5 us
    dot_general x1, matrix products, run_experts(): jnp.einsum('sjcd,jdf->sjcf', arriving, expert_gate_up, preferred_element_...  9.14 us
    all_gather x1, waiting for transfers between devices, shards(): gathered = lax.all_gather(o_weight, ('x', 'c'), axis=0, tiled=True)  6.71 us
    dot_general x1, matrix products, shards(): jnp.dot(spread, gathered, preferred_element_type=jnp.float32)  5.91 us
  transfers between devices with their start and end apart: 3, of which 3 were waited for; matrix products, arithmetic and copies ran while one was open for 6% of the time, Pallas kernels for 13%

profile of v5, /device:TPU:1, one launch (start us, length us, event | category | flops | bytes accessed | tf_op | source)
XLA Modules:
  0.0 207.3 jit_solution(3652219576472789430)
XLA Ops:
  7.2 0.0 copy-start
  7.2 0.0 copy-start.5
  7.2 0.0 copy-start.6
  7.2 0.0 copy-start.7
  7.2 0.0 all-gather.2.cloned.1.call-start
  7.3 0.7 all-gather.2.cloned.1.call-update
  7.9 0.0 reduce-scatter.2.cloned.1.call-start
  8.0 2.4 %reshape.119.q_ref = bf16[16,2,64,128]{3,2,1,0:T(8,128)(2,1)} reshape(bf16[16,2,8192]{2,1,0:T(2,128)(2,1)} %param.16) | data formatting | bytes 1048576 | tf_op jit(solution)/shard_map/reshape | solution.py:179
  10.4 0.0 copy-done.5
  10.4 0.1 copy.42
  10.5 0.6 reshape.116.flag_ref
  11.1 0.0 copy-done.6
  11.1 0.1 copy.43
  11.2 0.6 reshape.117.share_ref
  11.8 0.0 copy-done.7
  11.8 0.1 copy.44
  11.9 0.6 reshape.118.weight_ref
  12.5 27.2 %shard_map.167 = bf16[16,2,64,128]{3,2,1,0:T(8,128)(2,1)} custom-call(s32[16]{0:T(128)} %len_ref.1, s32[128]{0:T(128)} %reshape.116.flag_ref, f32[128]{0:T(128)} %reshape.117.share_ref, f32[64]{0:T(128)} %reshape.118.weight_ref, bf16[16,2,64,128]{3,2,1,0:T(8,128)(2,1)} %reshape.119.q_ref, bf16[16,2,512]{2,1,0:T(2,128)(2,1)} %kn_ref.1, ...), custom_call_target="tpu_custom_call" | custom-call | tf_op jit(solution)/shard_map/pallas_call | solution.py:160
  39.7 2.0 reshape_reshape.3
  41.6 1.4 copy.45
  43.0 13.5 %all_to_all.25 = bf16[32,4,2048]{2,0,1:T(8,128)(2,1)} all-to-all(bf16[32,4,2048]{2,0,1:T(8,128)(2,1)S(1)} %copy.45), channel_id=1, replica_groups=mesh['dp'=4,'y'=4,'x'=4,'c'=2] {'y'}, dimensions={1} | all-to-all | bytes 1048576 | tf_op jit(solution)/shard_map/all_to_all | solution.py:233
  56.5 6.7 %all-gather.2.cloned.1.call-done = bf16[2048,2048]{1,0:T(8,128)(2,1)} async-done(((bf16[256,2048]{1,0:T(8,128)(2,1)}), bf16[2048,2048]{1,0:T(8,128)(2,1)}) %all-gather.2.cloned.1.call-update) | async-done | bytes 8388624 | tf_op jit(solution)/shard_map/all_gather | solution.py:231
  63.2 0.0 copy-start.1
  63.2 0.0 copy-start.2
  63.2 5.9 %fusion.20 = f32[128,2048]{1,0:T(8,128)} fusion(bf16[128,2048]{1,0:T(8,128)(2,1)} %bitcast.40, bf16[2048,2048]{1,0:T(8,128)(2,1)} %all-gather.2.cloned.1.call-done), kind=kOutput, calls=%fused_computation.29 | convolution fusion | flops 1073741824 | bytes 9961472 | tf_op jit(solution)/shard_map/dot_general | solution.py:242
  69.1 0.0 copy-start.3
  69.1 0.0 reduce-scatter.2.cloned.1.call-update
  69.1 0.0 copy-done.1
  69.1 0.7 reshape.128
  69.9 0.0 copy-done.2
  69.9 0.1 copy.48
  70.0 0.1 eq.30
  70.1 0.2 convert_reduce_fusion
  70.2 0.1 reduce_sum.32
  70.3 0.1 copy.47
  70.4 0.2 fusion.15
  70.7 19.8 %reduce-scatter.2.cloned.1.call-done = f32[32,2048]{1,0:T(8,128)} async-done(((f32[128,2048]{1,0:T(8,128)}), f32[32,2048]{1,0:T(8,128)}) %reduce-scatter.2.cloned.1.call-update) | async-done | bytes 262160 | tf_op jit(solution)/shard_map/reduce_scatter | solution.py:241
  90.5 1.2 multiply_reduce_fusion
  91.7 0.0 copy-done.3
  91.7 2.1 %convolution_convert_fusion = bf16[512,2048]{1,0:T(8,128)(2,1)} fusion(pred[512,32]{0,1:T(8,128)(4,1)S(1)} %fusion.15, f32[32,2048]{1,0:T(8,128)S(1)} %get-tuple-element.3, f32[2048]{0:T(1024)S(1)} %copy-done.3, f32[32]{0:T(128)S(1)} %add_rsqrt_fusion), kind=kOutput, calls=%fused_computation.7 | convolution fusion | flops 68354048 | bytes 2384000 | tf_op jit(solution)/shard_map/dot_general | solution.py:266
  93.8 4.1 %reshape.122 = bf16[128,4,2048]{2,1,0:T(4,128)(2,1)} reshape(bf16[512,2048]{1,0:T(8,128)(2,1)} %convolution_convert_fusion) | data formatting | bytes 4194304 | tf_op jit(solution)/shard_map/reshape | solution.py:268
  97.9 40.6 %all_to_all.26 = bf16[128,4,2048]{2,1,0:T(4,128)(2,1)S(1)} all-to-all(bf16[128,4,2048]{2,1,0:T(4,128)(2,1)} %reshape.122), channel_id=1, replica_groups=mesh['dp'=4,'y'=4,'x'=4,'c'=2] {'dp','y','x','c'}, dimensions={0} | all-to-all | bytes 4194304 | tf_op jit(solution)/shard_map/all_to_all | solution.py:267
  138.5 9.1 %fusion.2 = f32[128,1,4,1536]{3,0,2,1:T(8,128)S(1)} fusion(bf16[1,2048,1536]{2,1,0:T(8,128)(2,1)} %param.28, bf16[128,4,2048]{2,1,0:T(4,128)(2,1)S(1)} %all_to_all.26), kind=kOutput, calls=%fused_computation.3 | convolution fusion | flops 3221225472 | bytes 11534336 | tf_op jit(solution)/shard_map/sjcd,jdf->sjcf/dot_general | solution.py:190
  147.7 0.0 copy-done
  147.7 1.8 fusion.7
  149.5 2.9 %copy.50 = bf16[128,4,2048]{2,1,0:T(4,128)(2,1)} copy(bf16[128,4,2048]{2,0,1:T(8,128)(2,1)S(1)} %fusion.7) | data formatting | bytes 4194304 | tf_op jit(solution)/shard_map/convert_element_type | solution.py:196
  152.5 0.0 copy-start.4
  152.5 5.6 %all-to-all-start.2 = ((bf16[128,4,2048]{2,1,0:T(4,128)(2,1)}), bf16[128,4,2048]{2,1,0:T(4,128)(2,1)}, u32[]{:S(2)}, u32[]{:S(2)}) async-start(bf16[128,4,2048]{2,1,0:T(4,128)(2,1)} %copy.50), calls=%async_computation.3 | async-start | bytes 4194304 | tf_op jit(solution)/shard_map/all_to_all | solution.py:279
  158.0 0.1 mul.71
  158.1 2.0 reshape.120
  160.1 0.0 copy-done.4
  160.1 0.1 copy.46
  160.2 28.2 %all-to-all-done.2 = bf16[128,4,2048]{2,1,0:T(4,128)(2,1)} async-done(((bf16[128,4,2048]{2,1,0:T(4,128)(2,1)}), bf16[128,4,2048]{2,1,0:T(4,128)(2,1)}, u32[]{:S(2)}, u32[]{:S(2)}) %all-to-all-start.2) | async-done | bytes 2097184 | tf_op jit(solution)/shard_map/all_to_all | solution.py:279
  188.3 3.9 %reshape.126 = bf16[512,2048]{1,0:T(8,128)(2,1)} reshape(bf16[128,4,2048]{2,1,0:T(4,128)(2,1)} %all-to-all-done.2) | data formatting | bytes 4194304 | tf_op jit(solution)/shard_map/reshape | solution.py:286
  192.3 5.2 %gather_fusion = bf16[256,2048]{1,0:T(8,128)(2,1)} fusion(bf16[512,2048]{1,0:T(8,128)(2,1)} %reshape.126, s32[1024]{0:T(1024)S(1)} %pad_clamp_fusion), kind=kCustom, calls=%fused_computation | custom fusion | bytes 2098176 | tf_op jit(solution)/shard_map/gather | solution.py:286
  197.5 2.2 %fusion.10 = f32[32,2048]{1,0:T(8,128)S(1)} fusion(bf16[256,2048]{1,0:T(8,128)(2,1)} %gather_fusion, f32[32,8]{1,0:T(8,128)S(1)} %bitcast.42), kind=kLoop, calls=%fused_computation.9 | loop fusion | flops 1507328 | bytes 1311744 | tf_op jit(solution)/shard_map/reduce_sum | solution.py:287
  199.7 0.8 reshape.127
  (6 shorter events, 0.1 us)
Async XLA Ops:
  7.2 140.5 %copy-start = (bf16[1,768,2048]{2,1,0:T(8,128)(2,1)S(1)}, bf16[1,768,2048]{2,1,0:T(8,128)(2,1)}, u32[]{:S(2)}) copy-start(bf16[1,768,2048]{2,1,0:T(8,128)(2,1)} %param.29) | copy-start | bytes 9437188
  7.2 3.2 %copy-start.5 = (s32[16,2,4]{0,2,1:T(4,128)S(1)}, s32[16,2,4]{0,2,1:T(4,128)}, u32[]{:S(2)}) copy-start(s32[16,2,4]{0,2,1:T(4,128)} %param.20) | copy-start | bytes 1540
  7.2 3.9 %copy-start.6 = (f32[16,2,4]{0,2,1:T(4,128)S(1)}, f32[16,2,4]{0,2,1:T(4,128)}, u32[]{:S(2)}) copy-start(f32[16,2,4]{0,2,1:T(4,128)} %param.19) | copy-start | bytes 1540
  7.2 4.6 %copy-start.7 = (f32[16,4]{0,1:T(4,128)S(1)}, f32[16,4]{0,1:T(4,128)}, u32[]{:S(2)}) copy-start(f32[16,4]{0,1:T(4,128)} %param.23) | copy-start | bytes 772
  7.2 56.0 %all-gather.2.cloned.1.call-start = ((), (), s32[]{:S(2)}) async-start(), calls=%async_computation.4 | async-start | bytes 9437184 | tf_op jit(solution)/shard_map/all_gather | solution.py:231
  7.9 82.6 %reduce-scatter.2.cloned.1.call-start = ((), (), s32[]{:S(2)}) async-start(), calls=%async_computation.5 | async-start | bytes 1310720 | tf_op jit(solution)/shard_map/reduce_scatter | solution.py:241
  63.2 5.9 %copy-start.1 = (bf16[16,2,2048]{2,1,0:T(2,128)(2,1)S(1)}, bf16[16,2,2048]{2,1,0:T(2,128)(2,1)}, u32[]{:S(2)}) copy-start(bf16[16,2,2048]{2,1,0:T(2,128)(2,1)} %param.25) | copy-start | bytes 393220
  63.2 6.7 %copy-start.2 = (s32[16,2,8]{0,2,1:T(8,128)S(1)}, s32[16,2,8]{0,2,1:T(8,128)}, u32[]{:S(2)}) copy-start(s32[16,2,8]{0,2,1:T(8,128)} %param.30) | copy-start | bytes 3076
  69.1 22.6 %copy-start.3 = (f32[2048]{0:T(1024)S(1)}, f32[2048]{0:T(1024)}, u32[]{:S(2)}) copy-start(f32[2048]{0:T(1024)} %param.27) | copy-start | bytes 24580
  152.5 7.6 %copy-start.4 = (f32[16,2,8]{0,2,1:T(8,128)S(1)}, f32[16,2,8]{0,2,1:T(8,128)}, u32[]{:S(2)}) copy-start(f32[16,2,8]{0,2,1:T(8,128)} %param.31) | copy-start | bytes 3076
  152.5 35.9 %all-to-all-start.2 = ((bf16[128,4,2048]{2,1,0:T(4,128)(2,1)}), bf16[128,4,2048]{2,1,0:T(4,128)(2,1)}, u32[]{:S(2)}, u32[]{:S(2)}) async-start(bf16[128,4,2048]{2,1,0:T(4,128)(2,1)} %copy.50), calls=%async_computation.3 | async-start | bytes 4194304 | tf_op jit(solution)/shard_map/all_to_all | solution.py:279
Sparse Core Ops, SparseCore 0:
  9.8 53.3 all-gather.1
  69.2 21.2 reduce-scatter.1

commit v6 on v5

--- a/solution.py
+++ b/solution.py
@@ -239,13 +239,13 @@
     )
     spread = spread.reshape(lines * rows, query_width // lines)
     projected = lax.psum_scatter(
-        jnp.dot(spread, gathered, preferred_element_type=jnp.float32),
+        jnp.dot(spread, gathered, preferred_element_type=jnp.float32).astype(jnp.bfloat16),
         "y",
         scatter_dimension=0,
         tiled=True,
     )
     members = lax.axis_size("y") * lax.axis_size("x") * lax.axis_size("c")
-    mixed = residual.reshape(rows, width).astype(jnp.float32) + projected
+    mixed = residual.reshape(rows, width).astype(jnp.float32) + projected.astype(jnp.float32)
     normed = (
         mixed * lax.rsqrt(jnp.mean(mixed * mixed, axis=1, keepdims=True) + EPS) * norm_gain
     ).astype(jnp.bfloat16)
@@ -283,8 +283,21 @@
         concat_axis=0,
         tiled=True,
     )
-    results = returned.reshape(experts_all * capacity, width)[target].reshape(rows, top_k, width)
-    blended = jnp.sum(route_weights.reshape(rows, top_k, 1) * results.astype(jnp.float32), axis=1)
+    slots_all = jnp.arange(experts_all * capacity, dtype=jnp.int32)
+    gathering = jnp.sum(
+        jnp.where(
+            slots_all[None, None, :] == target.reshape(rows, top_k, 1),
+            route_weights.reshape(rows, top_k, 1),
+            0.0,
+        ),
+        axis=1,
+    )
+    blended = jnp.dot(
+        gathering,
+        returned.reshape(experts_all * capacity, width).astype(jnp.float32),
+        precision=lax.Precision.HIGHEST,
+        preferred_element_type=jnp.float32,
+    )
     layer_out = (mixed + blended).astype(jnp.bfloat16).reshape(requests, steps, width)
     return (attended, layer_out)
 

time: 208 us -> 203 us (0.976)
  local copies, waits for them, and re-layouts: 28 us -> 23 us
  matrix products: 19 us -> 23 us
    gather x1 -> x0, local copies, waits for them, and re-layouts: 5.19 us -> none  [shards(): returned.reshape(experts_all * capacity, width)[target]]
    dot_general x0 -> x1, matrix products: none -> 3.4 us  [shards(): jnp.dot(gathering, returned.reshape(experts_all * capacity, width).astype...]
where the time goes in v6:
time: 203 us; the launch traced here: 202 us
  blocking collectives  53.6 us (26%)
  waiting for transfers between devices  53.4 us (26%)
  Pallas kernels  27.3 us (13%)
  local copies, waits for them, and re-layouts  23 us (11%)
  matrix products  23 us (11%)
  between operations  14.2 us (7%)
  starting transfers between devices  5.63 us (3%)
  other arithmetic  2.36 us (1%)
    all_to_all x1, blocking collectives, shards(): lax.all_to_all(outgoing.reshape(experts_all, capacity, width), ('dp', 'y'...  40.2 us
    all_to_all x1, waiting for transfers between devices, shards(): lax.all_to_all(answer.reshape(sources * experts_local, depth, width), ('d...  27.4 us
    pallas_call x1, Pallas kernels, decode_attention(): pl.pallas_call(kernel, out_shape=jax.ShapeDtypeStruct((requests, steps, h...  27.3 us
    reduce_scatter x1, waiting for transfers between devices, shards(): lax.psum_scatter(jnp.dot(spread, gathered, preferred_element_type=jnp.flo...  18.7 us
    all_to_all x1, blocking collectives, shards(): lax.all_to_all(attended.reshape(rows, lines, query_width // lines), 'y',...  13.4 us
    dot_general x1, matrix products, run_experts(): jnp.einsum('sjcd,jdf->sjcf', arriving, expert_gate_up, preferred_element_...  9.14 us
    all_gather x1, waiting for transfers between devices, shards(): gathered = lax.all_gather(o_weight, ('x', 'c'), axis=0, tiled=True)  6.56 us
    dot_general x1, matrix products, shards(): jnp.dot(spread, gathered, preferred_element_type=jnp.float32)  5.65 us
  transfers between devices with their start and end apart: 3, of which 3 were waited for; matrix products, arithmetic and copies ran while one was open for 6% of the time, Pallas kernels for 13%

profile of v6, /device:TPU:1, one launch (start us, length us, event | category | flops | bytes accessed | tf_op | source)
XLA Modules:
  0.0 202.5 jit_solution(4305190419981530675)
XLA Ops:
  7.2 0.0 copy-start
  7.2 0.0 copy-start.6
  7.2 0.0 copy-start.7
  7.2 0.0 copy-start.8
  7.2 0.0 all-gather.2.cloned.1.call-start
  7.3 0.7 all-gather.2.cloned.1.call-update
  7.9 0.0 reduce-scatter.2.cloned.1.call-start
  8.0 2.4 %reshape.99.q_ref = bf16[16,2,64,128]{3,2,1,0:T(8,128)(2,1)} reshape(bf16[16,2,8192]{2,1,0:T(2,128)(2,1)} %param.16) | data formatting | bytes 1048576 | tf_op jit(solution)/shard_map/reshape | solution.py:179
  10.4 0.0 copy-done.6
  10.4 0.1 copy.40
  10.5 0.6 reshape.96.flag_ref
  11.1 0.0 copy-done.7
  11.1 0.1 copy.41
  11.2 0.7 reshape.97.share_ref
  11.8 0.0 copy-done.8
  11.9 0.1 copy.42
  11.9 0.6 reshape.98.weight_ref
  12.6 27.3 %shard_map.167 = bf16[16,2,64,128]{3,2,1,0:T(8,128)(2,1)} custom-call(s32[16]{0:T(128)} %len_ref.1, s32[128]{0:T(128)} %reshape.96.flag_ref, f32[128]{0:T(128)} %reshape.97.share_ref, f32[64]{0:T(128)} %reshape.98.weight_ref, bf16[16,2,64,128]{3,2,1,0:T(8,128)(2,1)} %reshape.99.q_ref, bf16[16,2,512]{2,1,0:T(2,128)(2,1)} %kn_ref.1, ...), custom_call_target="tpu_custom_call" | custom-call | tf_op jit(solution)/shard_map/pallas_call | solution.py:160
  39.8 2.0 reshape_reshape.3
  41.8 1.4 copy.43
  43.2 13.4 %all_to_all.25 = bf16[32,4,2048]{2,0,1:T(8,128)(2,1)} all-to-all(bf16[32,4,2048]{2,0,1:T(8,128)(2,1)S(1)} %copy.43), channel_id=1, replica_groups=mesh['dp'=4,'y'=4,'x'=4,'c'=2] {'y'}, dimensions={1} | all-to-all | bytes 1048576 | tf_op jit(solution)/shard_map/all_to_all | solution.py:233
  56.7 6.6 %all-gather.2.cloned.1.call-done = bf16[2048,2048]{1,0:T(8,128)(2,1)} async-done(((bf16[256,2048]{1,0:T(8,128)(2,1)}), bf16[2048,2048]{1,0:T(8,128)(2,1)}) %all-gather.2.cloned.1.call-update) | async-done | bytes 8388624 | tf_op jit(solution)/shard_map/all_gather | solution.py:231
  63.2 0.0 copy-start.2
  63.2 0.0 copy-start.3
  63.2 0.0 copy-start.4
  63.2 5.6 %convolution_convert_fusion.1 = bf16[128,2048]{1,0:T(8,128)(2,1)} fusion(bf16[128,2048]{1,0:T(8,128)(2,1)} %bitcast.37, bf16[2048,2048]{1,0:T(8,128)(2,1)} %all-gather.2.cloned.1.call-done), kind=kOutput, calls=%fused_computation.7 | convolution fusion | flops 1074003968 | bytes 9437184 | tf_op jit(solution)/shard_map/dot_general | solution.py:242
  68.9 0.0 reduce-scatter.2.cloned.1.call-update
  68.9 0.0 copy-done.2
  68.9 0.0 copy-done.3
  69.0 0.1 copy.45
  69.0 0.1 eq.43
  69.1 0.2 convert_reduce_fusion
  69.3 0.1 reduce_sum.30
  69.4 0.1 copy.44
  69.5 0.2 fusion.15
  69.8 18.7 %reduce-scatter.2.cloned.1.call-done = bf16[32,2048]{1,0:T(8,128)(2,1)} async-done(((bf16[128,2048]{1,0:T(8,128)(2,1)}), bf16[32,2048]{1,0:T(8,128)(2,1)}) %reduce-scatter.2.cloned.1.call-update) | async-done | bytes 131088 | tf_op jit(solution)/shard_map/reduce_scatter | solution.py:241
  88.5 1.0 multiply_reduce_fusion
  89.5 0.0 copy-done.4
  89.5 3.0 %convolution_convert_fusion = bf16[512,2048]{1,0:T(8,128)(2,1)} fusion(pred[512,32]{0,1:T(8,128)(4,1)S(1)} %fusion.15, f32[2048]{0:T(1024)S(1)} %copy-done.4, f32[32]{0:T(128)S(1)} %add_rsqrt_fusion, f32[32,2048]{1,0:T(8,128)S(1)} %reshape.108, bf16[32,2048]{1,0:T(8,128)(2,1)} %reduce-scatter.2.cloned.1.call-done), kind=kOutput, calls=%fused_computation.6 | convolution fusion | flops 68485120 | bytes 2515072 | tf_op jit(solution)/shard_map/dot_general | solution.py:266
  92.5 4.1 %reshape.102 = bf16[128,4,2048]{2,1,0:T(4,128)(2,1)} reshape(bf16[512,2048]{1,0:T(8,128)(2,1)} %convolution_convert_fusion) | data formatting | bytes 4194304 | tf_op jit(solution)/shard_map/reshape | solution.py:268
  96.6 40.2 %all_to_all.26 = bf16[128,4,2048]{2,1,0:T(4,128)(2,1)S(1)} all-to-all(bf16[128,4,2048]{2,1,0:T(4,128)(2,1)} %reshape.102), channel_id=1, replica_groups=mesh['dp'=4,'y'=4,'x'=4,'c'=2] {'dp','y','x','c'}, dimensions={0} | all-to-all | bytes 4194304 | tf_op jit(solution)/shard_map/all_to_all | solution.py:267
  136.9 9.1 %fusion.2 = f32[128,1,4,1536]{3,0,2,1:T(8,128)S(1)} fusion(bf16[1,2048,1536]{2,1,0:T(8,128)(2,1)} %param.28, bf16[128,4,2048]{2,1,0:T(4,128)(2,1)S(1)} %all_to_all.26), kind=kOutput, calls=%fused_computation.2 | convolution fusion | flops 3221225472 | bytes 11534336 | tf_op jit(solution)/shard_map/sjcd,jdf->sjcf/dot_general | solution.py:190
  146.0 0.0 copy-done
  146.0 1.8 fusion.7
  147.8 2.9 %copy.48 = bf16[128,4,2048]{2,1,0:T(4,128)(2,1)} copy(bf16[128,4,2048]{2,0,1:T(8,128)(2,1)S(1)} %fusion.7) | data formatting | bytes 4194304 | tf_op jit(solution)/shard_map/convert_element_type | solution.py:196
  150.8 0.0 copy-start.5
  150.8 5.6 %all-to-all-start.2 = ((bf16[128,4,2048]{2,1,0:T(4,128)(2,1)}), bf16[128,4,2048]{2,1,0:T(4,128)(2,1)}, u32[]{:S(2)}, u32[]{:S(2)}) async-start(bf16[128,4,2048]{2,1,0:T(4,128)(2,1)} %copy.48), calls=%async_computation.3 | async-start | bytes 4194304 | tf_op jit(solution)/shard_map/all_to_all | solution.py:279
  156.3 2.0 reshape.100
  158.3 0.0 copy-done.5
  158.3 0.1 copy.46
  158.4 0.9 select_reduce_fusion
  159.2 0.0 copy-start.1
  159.2 27.4 %all-to-all-done.2 = bf16[128,4,2048]{2,1,0:T(4,128)(2,1)} async-done(((bf16[128,4,2048]{2,1,0:T(4,128)(2,1)}), bf16[128,4,2048]{2,1,0:T(4,128)(2,1)}, u32[]{:S(2)}, u32[]{:S(2)}) %all-to-all-start.2) | async-done | bytes 2097184 | tf_op jit(solution)/shard_map/all_to_all | solution.py:279
  186.6 3.9 %reshape.106 = bf16[512,2048]{1,0:T(8,128)(2,1)} reshape(bf16[128,4,2048]{2,1,0:T(4,128)(2,1)} %all-to-all-done.2) | data formatting | bytes 4194304 | tf_op jit(solution)/shard_map/reshape | solution.py:297
  190.6 0.0 copy-done.1
  190.6 3.4 %fusion.10 = bf16[32,2048]{1,0:T(8,128)(2,1)} fusion(f32[32,512]{1,0:T(8,128)} %select_reduce_fusion, bf16[512,2048]{1,0:T(8,128)(2,1)} %reshape.106, f32[32,2048]{1,0:T(8,128)S(1)} %reshape.108, bf16[32,2048]{1,0:T(8,128)(2,1)S(1)} %copy-done.1), kind=kOutput, calls=%fused_computation.9 | convolution fusion | flops 402915328 | bytes 2686976 | tf_op jit(solution)/shard_map/dot_general | solution.py:295
  194.0 1.7 reshape.107
  (4 shorter events, 0.1 us)
Async XLA Ops:
  7.2 138.8 %copy-start = (bf16[1,768,2048]{2,1,0:T(8,128)(2,1)S(1)}, bf16[1,768,2048]{2,1,0:T(8,128)(2,1)}, u32[]{:S(2)}) copy-start(bf16[1,768,2048]{2,1,0:T(8,128)(2,1)} %param.29) | copy-start | bytes 9437188
  7.2 3.2 %copy-start.6 = (s32[16,2,4]{0,2,1:T(4,128)S(1)}, s32[16,2,4]{0,2,1:T(4,128)}, u32[]{:S(2)}) copy-start(s32[16,2,4]{0,2,1:T(4,128)} %param.20) | copy-start | bytes 1540
  7.2 3.9 %copy-start.7 = (f32[16,2,4]{0,2,1:T(4,128)S(1)}, f32[16,2,4]{0,2,1:T(4,128)}, u32[]{:S(2)}) copy-start(f32[16,2,4]{0,2,1:T(4,128)} %param.19) | copy-start | bytes 1540
  7.2 4.7 %copy-start.8 = (f32[16,4]{0,1:T(4,128)S(1)}, f32[16,4]{0,1:T(4,128)}, u32[]{:S(2)}) copy-start(f32[16,4]{0,1:T(4,128)} %param.23) | copy-start | bytes 772
  7.2 56.0 %all-gather.2.cloned.1.call-start = ((), (), s32[]{:S(2)}) async-start(), calls=%async_computation.4 | async-start | bytes 9437184 | tf_op jit(solution)/shard_map/all_gather | solution.py:231
  7.9 80.5 %reduce-scatter.2.cloned.1.call-start = ((), (), s32[]{:S(2)}) async-start(), calls=%async_computation.5 | async-start | bytes 655360 | tf_op jit(solution)/shard_map/reduce_scatter | solution.py:241
  63.2 5.7 %copy-start.2 = (bf16[16,2,2048]{2,1,0:T(2,128)(2,1)S(1)}, bf16[16,2,2048]{2,1,0:T(2,128)(2,1)}, u32[]{:S(2)}) copy-start(bf16[16,2,2048]{2,1,0:T(2,128)(2,1)} %param.25) | copy-start | bytes 393220
  63.2 5.7 %copy-start.3 = (s32[16,2,8]{0,2,1:T(8,128)S(1)}, s32[16,2,8]{0,2,1:T(8,128)}, u32[]{:S(2)}) copy-start(s32[16,2,8]{0,2,1:T(8,128)} %param.30) | copy-start | bytes 3076
  63.2 26.3 %copy-start.4 = (f32[2048]{0:T(1024)S(1)}, f32[2048]{0:T(1024)}, u32[]{:S(2)}) copy-start(f32[2048]{0:T(1024)} %param.27) | copy-start | bytes 24580
  150.8 7.5 %copy-start.5 = (f32[16,2,8]{0,2,1:T(8,128)S(1)}, f32[16,2,8]{0,2,1:T(8,128)}, u32[]{:S(2)}) copy-start(f32[16,2,8]{0,2,1:T(8,128)} %param.31) | copy-start | bytes 3076
  150.8 35.9 %all-to-all-start.2 = ((bf16[128,4,2048]{2,1,0:T(4,128)(2,1)}), bf16[128,4,2048]{2,1,0:T(4,128)(2,1)}, u32[]{:S(2)}, u32[]{:S(2)}) async-start(bf16[128,4,2048]{2,1,0:T(4,128)(2,1)} %copy.48), calls=%async_computation.3 | async-start | bytes 4194304 | tf_op jit(solution)/shard_map/all_to_all | solution.py:279
  159.2 31.4 %copy-start.1 = (bf16[32,2048]{1,0:T(8,128)(2,1)S(1)}, bf16[32,2048]{1,0:T(8,128)(2,1)}, u32[]{:S(2)}) copy-start(bf16[32,2048]{1,0:T(8,128)(2,1)} %reduce-scatter.2.cloned.1.call-done) | copy-start | bytes 393220
Sparse Core Ops, SparseCore 0:
  9.8 53.4 all-gather.1
  69.0 19.3 reduce-scatter.1

commit v7 on v6

--- a/solution.py
+++ b/solution.py
@@ -230,22 +230,25 @@
     width = o_weight.shape[1]
     gathered = lax.all_gather(o_weight, ("x", "c"), axis=0, tiled=True)
     lines = lax.axis_size("y")
-    spread = lax.all_to_all(
-        attended.reshape(rows, lines, query_width // lines),
-        "y",
-        split_axis=1,
-        concat_axis=0,
-        tiled=True,
-    )
-    spread = spread.reshape(lines * rows, query_width // lines)
-    projected = lax.psum_scatter(
-        jnp.dot(spread, gathered, preferred_element_type=jnp.float32).astype(jnp.bfloat16),
-        "y",
-        scatter_dimension=0,
-        tiled=True,
-    )
+    line = lax.axis_index("y")
+    block = query_width // lines
+    flat = attended.reshape(rows, query_width)
+
+    def shifted(value, shift):
+        return lax.ppermute(value, "y", [(j, (j + shift) % lines) for j in range(lines)])
+
+    pieces = [lax.dynamic_slice_in_dim(flat, line * block, block, 1)]
+    for shift in range(1, lines):
+        piece = lax.dynamic_slice_in_dim(flat, ((line + shift) % lines) * block, block, 1)
+        pieces.append(shifted(piece, shift))
+    partials = jnp.dot(
+        jnp.concatenate(pieces, axis=0), gathered, preferred_element_type=jnp.float32
+    ).reshape(lines, rows, width)
+    projected = partials[0]
+    for shift in range(1, lines):
+        projected = projected + shifted(partials[shift], lines - shift)
     members = lax.axis_size("y") * lax.axis_size("x") * lax.axis_size("c")
-    mixed = residual.reshape(rows, width).astype(jnp.float32) + projected.astype(jnp.float32)
+    mixed = residual.reshape(rows, width).astype(jnp.float32) + projected
     normed = (
         mixed * lax.rsqrt(jnp.mean(mixed * mixed, axis=1, keepdims=True) + EPS) * norm_gain
     ).astype(jnp.bfloat16)

time: 203 us -> 197 us (0.970)
  blocking collectives: 53.6 us -> 36.6 us
  starting transfers between devices: 5.63 us -> 15.3 us
  local copies, waits for them, and re-layouts: 23 us -> 26 us
  matrix products: 23 us -> 20.7 us
    reduce_scatter x1 -> x0, waiting for transfers between devices: 18.7 us -> none  [shards(): lax.psum_scatter(jnp.dot(spread, gathered, preferred_element_type=jnp.flo...]
    ppermute x0 -> x6, waiting for transfers between devices: none -> 16.8 us  [shifted(): lax.ppermute(value, 'y', [(j, (j + shift) % lines) for j in range(lines)])]
    all_to_all x1 -> x0, blocking collectives: 13.4 us -> none  [shards(): lax.all_to_all(attended.reshape(rows, lines, query_width // lines), 'y',...]
    ppermute x0 -> x6, starting transfers between devices: none -> 9.67 us  [shifted(): lax.ppermute(value, 'y', [(j, (j + shift) % lines) for j in range(lines)])]
    unnamed x23 -> x28, local copies, waits for them, and re-layouts: 0.47 us -> 4.35 us
    all_to_all x1, blocking collectives: 40.2 us -> 36.6 us  [shards(): lax.all_to_all(outgoing.reshape(experts_all, capacity, width), ('dp', 'y'...]
    another operation x2 -> x0, local copies, waits for them, and re-layouts: 3.39 us -> none  [shards(): attended.reshape(rows, lines, query_width // lines)]
    all_gather x1, waiting for transfers between devices: 6.56 us -> 8.77 us  [shards(): gathered = lax.all_gather(o_weight, ('x', 'c'), axis=0, tiled=True)]
  transfers between devices with their start and end apart: 3 -> 8, of which waited for: 3 -> 5; matrix products, arithmetic and copies ran while one was open for 6% -> 7% of each run, Pallas kernels for 13% -> 14%
where the time goes in v7:
time: 197 us; the launch traced here: 196 us
  waiting for transfers between devices  53.7 us (27%)
  blocking collectives  36.6 us (19%)
  Pallas kernels  27.2 us (14%)
  local copies, waits for them, and re-layouts  26 us (13%)
  matrix products  20.7 us (11%)
  starting transfers between devices  15.3 us (8%)
  between operations  14.2 us (7%)
  other arithmetic  2.74 us (1%)
    all_to_all x1, blocking collectives, shards(): lax.all_to_all(outgoing.reshape(experts_all, capacity, width), ('dp', 'y'...  36.6 us
    all_to_all x1, waiting for transfers between devices, shards(): lax.all_to_all(answer.reshape(sources * experts_local, depth, width), ('d...  27.4 us
    pallas_call x1, Pallas kernels, decode_attention(): pl.pallas_call(kernel, out_shape=jax.ShapeDtypeStruct((requests, steps, h...  27.2 us
    ppermute x6, waiting for transfers between devices, shifted(): lax.ppermute(value, 'y', [(j, (j + shift) % lines) for j in range(lines)])  16.8 us
    ppermute x6, starting transfers between devices, shifted(): lax.ppermute(value, 'y', [(j, (j + shift) % lines) for j in range(lines)])  9.67 us
    dot_general x1, matrix products, run_experts(): jnp.einsum('sjcd,jdf->sjcf', arriving, expert_gate_up, preferred_element_...  9.14 us
    all_gather x1, waiting for transfers between devices, shards(): gathered = lax.all_gather(o_weight, ('x', 'c'), axis=0, tiled=True)  8.77 us
    all_to_all x1, starting transfers between devices, shards(): lax.all_to_all(answer.reshape(sources * experts_local, depth, width), ('d...  5.58 us
  transfers between devices with their start and end apart: 8, of which 5 were waited for; matrix products, arithmetic and copies ran while one was open for 7% of the time, Pallas kernels for 14%

profile of v7, /device:TPU:1, one launch (start us, length us, event | category | flops | bytes accessed | tf_op | source)
XLA Modules:
  0.0 196.4 jit_solution(3237241634044007574)
XLA Ops:
  7.2 0.0 copy-start
  7.2 0.0 copy-start.8
  7.2 0.0 copy-start.9
  7.2 0.0 copy-start.10
  7.2 0.0 all-gather.2.cloned.1.call-start
  7.3 0.7 all-gather.2.cloned.1.call-update
  8.0 2.4 %reshape.104.q_ref = bf16[16,2,64,128]{3,2,1,0:T(8,128)(2,1)} reshape(bf16[16,2,8192]{2,1,0:T(2,128)(2,1)} %param.16) | data formatting | bytes 1048576 | tf_op jit(solution)/shard_map/reshape | solution.py:179
  10.4 0.0 copy-done.8
  10.4 0.1 copy.38
  10.5 0.6 reshape.101.flag_ref
  11.1 0.0 copy-done.9
  11.1 0.1 copy.39
  11.2 0.6 reshape.102.share_ref
  11.8 0.0 copy-done.10
  11.8 0.1 copy.40
  11.9 0.6 reshape.103.weight_ref
  12.5 27.2 %shard_map.167 = bf16[16,2,64,128]{3,2,1,0:T(8,128)(2,1)} custom-call(s32[16]{0:T(128)} %len_ref.1, s32[128]{0:T(128)} %reshape.101.flag_ref, f32[128]{0:T(128)} %reshape.102.share_ref, f32[64]{0:T(128)} %reshape.103.weight_ref, bf16[16,2,64,128]{3,2,1,0:T(8,128)(2,1)} %reshape.104.q_ref, bf16[16,2,512]{2,1,0:T(2,128)(2,1)} %kn_ref.1, ...), custom_call_target="tpu_custom_call" | custom-call | tf_op jit(solution)/shard_map/pallas_call | solution.py:160
  39.7 0.0 copy-start.3
  39.7 0.0 copy-start.4
  39.7 2.2 %copy.50 = bf16[4,8,64,128]{3,1,2,0:T(8,128)(2,1)} copy(bf16[4,8,64,128]{3,2,1,0:T(8,128)(2,1)} %bitcast.34) | data formatting | bytes 1048576
  41.9 1.9 constant_dynamic-slice_fusion.3
  43.8 2.1 %collective-permute-start = (bf16[32,2048]{1,0:T(8,128)(2,1)}, bf16[32,2048]{1,0:T(8,128)(2,1)}, u32[]{:S(2)}, u32[]{:S(2)}) collective-permute-start(bf16[32,2048]{1,0:T(8,128)(2,1)} %get-tuple-element.10), channel_id=1, source_target_pairs={{0,8},{8,16},{16,24},{24,0},{1,9},{9,17},{17,25},{25,1},{2,10},{10... | collective-permute-start | bytes 393224 | tf_op jit(solution)/shard_map/ppermute | solution.py:238
  45.9 2.6 %collective-permute-start.1 = (bf16[32,2048]{1,0:T(8,128)(2,1)}, bf16[32,2048]{1,0:T(8,128)(2,1)}, u32[]{:S(2)}, u32[]{:S(2)}) collective-permute-start(bf16[32,2048]{1,0:T(8,128)(2,1)} %get-tuple-element.9), channel_id=1, source_target_pairs={{0,16},{8,24},{16,0},{24,8},{1,17},{9,25},{17,1},{25,9},{2,18},{10... | collective-permute-start | bytes 393224 | tf_op jit(solution)/shard_map/ppermute | solution.py:238
  48.5 1.4 collective-permute-start.2
  49.9 0.0 copy-done.3
  49.9 0.7 reshape.112
  50.6 0.0 copy-done.4
  50.6 0.1 copy.42
  50.7 0.1 eq.47
  50.8 0.2 convert_reduce_fusion
  51.0 0.1 reduce_sum.30
  51.1 0.0 collective-permute-done
  51.1 3.4 %collective-permute-done.1 = bf16[32,2048]{1,0:T(8,128)(2,1)} collective-permute-done((bf16[32,2048]{1,0:T(8,128)(2,1)}, bf16[32,2048]{1,0:T(8,128)(2,1)}, u32[]{:S(2)}, u32[]{:S(2)}) %collective-permute-start.1) | collective-permute-done | bytes 131104 | tf_op jit(solution)/shard_map/ppermute | solution.py:238
  54.5 0.0 collective-permute-done.2
  54.5 8.8 %all-gather.2.cloned.1.call-done = bf16[2048,2048]{1,0:T(8,128)(2,1)} async-done(((bf16[256,2048]{1,0:T(8,128)(2,1)}), bf16[2048,2048]{1,0:T(8,128)(2,1)}) %all-gather.2.cloned.1.call-update) | async-done | bytes 8388624 | tf_op jit(solution)/shard_map/all_gather | solution.py:231
  63.2 4.9 %fusion.15 = f32[128,2048]{1,0:T(8,128)S(1)} fusion(bf16[2048,2048]{1,0:T(8,128)(2,1)} %all-gather.2.cloned.1.call-done, bf16[32,2048]{1,0:T(8,128)(2,1)} %collective-permute-done.2, bf16[32,2048]{1,0:T(8,128)(2,1)} %collective-permute-done.1, bf16[32,2048]{1,0:T(8,128)(2,1)} %collective-permute-done, bf16[32,2048]{1,0:T(8,128)(2,1)S(1)} %get-tuple-element.7), kind=kOutput, calls=%fused_computation.14 | convolution fusion | flops 1075838976 | bytes 9961472 | tf_op jit(solution)/shard_map/dot_general | solution.py:244
  68.1 0.0 copy-start.1
  68.1 1.0 copy-done.1
  69.1 0.9 fusion.33
  70.0 2.4 %collective-permute-start.3 = (f32[32,2048]{1,0:T(8,128)}, f32[32,2048]{1,0:T(8,128)S(1)}, u32[]{:S(2)}, u32[]{:S(2)}) collective-permute-start(f32[32,2048]{1,0:T(8,128)} %get-tuple-element.4), channel_id=1, source_target_pairs={{0,24},{8,0},{16,8},{24,16},{1,25},{9,1},{17,9},{25,17},{2,26},{10... | collective-permute-start | bytes 786440 | tf_op jit(solution)/shard_map/ppermute | solution.py:238
  72.4 0.6 collective-permute-start.4
  73.0 0.6 collective-permute-start.5
  73.6 0.1 copy.41
  73.7 0.2 fusion.23
  73.9 9.7 %collective-permute-done.3 = f32[32,2048]{1,0:T(8,128)S(1)} collective-permute-done((f32[32,2048]{1,0:T(8,128)}, f32[32,2048]{1,0:T(8,128)S(1)}, u32[]{:S(2)}, u32[]{:S(2)}) %collective-permute-start.3) | collective-permute-done | bytes 262176 | tf_op jit(solution)/shard_map/ppermute | solution.py:238
  83.6 0.0 collective-permute-done.4
  83.6 0.7 copy-done.2
  84.3 3.7 %collective-permute-done.5 = f32[32,2048]{1,0:T(8,128)} collective-permute-done((f32[32,2048]{1,0:T(8,128)}, f32[32,2048]{1,0:T(8,128)}, u32[]{:S(2)}, u32[]{:S(2)}) %collective-permute-start.5) | collective-permute-done | bytes 262176 | tf_op jit(solution)/shard_map/ppermute | solution.py:238
  88.0 1.4 multiply_reduce_fusion
  89.5 2.1 %convolution_convert_fusion = bf16[512,2048]{1,0:T(8,128)(2,1)} fusion(pred[512,32]{0,1:T(8,128)(4,1)S(1)} %fusion.23, f32[32,2048]{1,0:T(8,128)S(1)} %get-tuple-element.3, f32[2048]{0:T(1024)S(1)} %copy-done.6, f32[32]{0:T(128)S(1)} %add_rsqrt_fusion), kind=kOutput, calls=%fused_computation.6 | convolution fusion | flops 68354048 | bytes 2384000 | tf_op jit(solution)/shard_map/dot_general | solution.py:269
  91.6 4.1 %reshape.106 = bf16[128,4,2048]{2,1,0:T(4,128)(2,1)} reshape(bf16[512,2048]{1,0:T(8,128)(2,1)} %convolution_convert_fusion) | data formatting | bytes 4194304 | tf_op jit(solution)/shard_map/reshape | solution.py:271
  95.7 36.6 %all_to_all.10 = bf16[128,4,2048]{2,1,0:T(4,128)(2,1)S(1)} all-to-all(bf16[128,4,2048]{2,1,0:T(4,128)(2,1)} %reshape.106), channel_id=1, replica_groups=mesh['dp'=4,'y'=4,'x'=4,'c'=2] {'dp','y','x','c'}, dimensions={0} | all-to-all | bytes 4194304 | tf_op jit(solution)/shard_map/all_to_all | solution.py:270
  132.3 9.1 %fusion.2 = f32[128,1,4,1536]{3,0,2,1:T(8,128)S(1)} fusion(bf16[1,2048,1536]{2,1,0:T(8,128)(2,1)} %param.28, bf16[128,4,2048]{2,1,0:T(4,128)(2,1)S(1)} %all_to_all.10), kind=kOutput, calls=%fused_computation.2 | convolution fusion | flops 3221225472 | bytes 11534336 | tf_op jit(solution)/shard_map/sjcd,jdf->sjcf/dot_general | solution.py:190
  141.4 0.0 copy-done
  141.5 1.8 fusion.7
  143.3 2.9 %copy.45 = bf16[128,4,2048]{2,1,0:T(4,128)(2,1)} copy(bf16[128,4,2048]{2,0,1:T(8,128)(2,1)S(1)} %fusion.7) | data formatting | bytes 4194304 | tf_op jit(solution)/shard_map/convert_element_type | solution.py:196
  146.2 5.6 %all-to-all-start.1 = ((bf16[128,4,2048]{2,1,0:T(4,128)(2,1)}), bf16[128,4,2048]{2,1,0:T(4,128)(2,1)}, u32[]{:S(2)}, u32[]{:S(2)}) async-start(bf16[128,4,2048]{2,1,0:T(4,128)(2,1)} %copy.45), calls=%async_computation.1 | async-start | bytes 4194304 | tf_op jit(solution)/shard_map/all_to_all | solution.py:282
  151.8 2.0 reshape.105
  153.8 0.1 copy.43
  153.8 0.9 select_reduce_fusion
  154.7 27.4 %all-to-all-done.1 = bf16[128,4,2048]{2,1,0:T(4,128)(2,1)} async-done(((bf16[128,4,2048]{2,1,0:T(4,128)(2,1)}), bf16[128,4,2048]{2,1,0:T(4,128)(2,1)}, u32[]{:S(2)}, u32[]{:S(2)}) %all-to-all-start.1) | async-done | bytes 2097184 | tf_op jit(solution)/shard_map/all_to_all | solution.py:282
  182.1 3.9 %reshape.110 = bf16[512,2048]{1,0:T(8,128)(2,1)} reshape(bf16[128,4,2048]{2,1,0:T(4,128)(2,1)} %all-to-all-done.1) | data formatting | bytes 4194304 | tf_op jit(solution)/shard_map/reshape | solution.py:300
  186.1 2.7 %fusion.10 = bf16[32,2048]{1,0:T(8,128)(2,1)S(1)} fusion(f32[32,2048]{1,0:T(8,128)S(1)} %get-tuple-element.3, f32[32,512]{1,0:T(8,128)} %select_reduce_fusion, bf16[512,2048]{1,0:T(8,128)(2,1)} %reshape.110), kind=kOutput, calls=%fused_computation.8 | convolution fusion | flops 402784256 | bytes 2555904 | tf_op jit(solution)/shard_map/dot_general | solution.py:298
  188.8 0.8 reshape.111
  (10 shorter events, 0.0 us)
Async XLA Ops:
  7.2 134.3 %copy-start = (bf16[1,768,2048]{2,1,0:T(8,128)(2,1)S(1)}, bf16[1,768,2048]{2,1,0:T(8,128)(2,1)}, u32[]{:S(2)}) copy-start(bf16[1,768,2048]{2,1,0:T(8,128)(2,1)} %param.29) | copy-start | bytes 9437188
  7.2 3.2 %copy-start.8 = (s32[16,2,4]{0,2,1:T(4,128)S(1)}, s32[16,2,4]{0,2,1:T(4,128)}, u32[]{:S(2)}) copy-start(s32[16,2,4]{0,2,1:T(4,128)} %param.20) | copy-start | bytes 1540
  7.2 3.9 %copy-start.9 = (f32[16,2,4]{0,2,1:T(4,128)S(1)}, f32[16,2,4]{0,2,1:T(4,128)}, u32[]{:S(2)}) copy-start(f32[16,2,4]{0,2,1:T(4,128)} %param.19) | copy-start | bytes 1540
  7.2 4.6 %copy-start.10 = (f32[16,4]{0,1:T(4,128)S(1)}, f32[16,4]{0,1:T(4,128)}, u32[]{:S(2)}) copy-start(f32[16,4]{0,1:T(4,128)} %param.23) | copy-start | bytes 772
  7.2 56.0 %all-gather.2.cloned.1.call-start = ((), (), s32[]{:S(2)}) async-start(), calls=%async_computation.2 | async-start | bytes 9437184 | tf_op jit(solution)/shard_map/all_gather | solution.py:231
  39.7 10.2 %copy-start.3 = (bf16[16,2,2048]{2,1,0:T(2,128)(2,1)S(1)}, bf16[16,2,2048]{2,1,0:T(2,128)(2,1)}, u32[]{:S(2)}) copy-start(bf16[16,2,2048]{2,1,0:T(2,128)(2,1)} %param.25) | copy-start | bytes 393220
  39.7 10.9 %copy-start.4 = (s32[16,2,8]{0,2,1:T(8,128)S(1)}, s32[16,2,8]{0,2,1:T(8,128)}, u32[]{:S(2)}) copy-start(s32[16,2,8]{0,2,1:T(8,128)} %param.30) | copy-start | bytes 3076
  43.8 7.3 %collective-permute-start = (bf16[32,2048]{1,0:T(8,128)(2,1)}, bf16[32,2048]{1,0:T(8,128)(2,1)}, u32[]{:S(2)}, u32[]{:S(2)}) collective-permute-start(bf16[32,2048]{1,0:T(8,128)(2,1)} %get-tuple-element.10), channel_id=1, source_target_pairs={{0,8},{8,16},{16,24},{24,0},{1,9},{9,17},{17,25},{25,1},{2,10},{10... | collective-permute-start | bytes 393224 | tf_op jit(solution)/shard_map/ppermute | solution.py:238
  45.9 8.6 %collective-permute-start.1 = (bf16[32,2048]{1,0:T(8,128)(2,1)}, bf16[32,2048]{1,0:T(8,128)(2,1)}, u32[]{:S(2)}, u32[]{:S(2)}) collective-permute-start(bf16[32,2048]{1,0:T(8,128)(2,1)} %get-tuple-element.9), channel_id=1, source_target_pairs={{0,16},{8,24},{16,0},{24,8},{1,17},{9,25},{17,1},{25,9},{2,18},{10... | collective-permute-start | bytes 393224 | tf_op jit(solution)/shard_map/ppermute | solution.py:238
  48.5 5.9 %collective-permute-start.2 = (bf16[32,2048]{1,0:T(8,128)(2,1)S(1)}, bf16[32,2048]{1,0:T(8,128)(2,1)}, u32[]{:S(2)}, u32[]{:S(2)}) collective-permute-start(bf16[32,2048]{1,0:T(8,128)(2,1)S(1)} %get-tuple-element.8), channel_id=1, source_target_pairs={{0,24},{8,0},{16,8},{24,16},{1,25},{9,1},{17,9},{25,17},{2,26},{10... | collective-permute-start | bytes 393224 | tf_op jit(solution)/shard_map/ppermute | solution.py:238
  63.2 10.3 %copy-start.5 = (s32[16,2,8]{0,2,1:T(8,128)S(1)}, s32[16,2,8]{0,2,1:T(8,128)}, u32[]{:S(2)}) copy-start(s32[16,2,8]{0,2,1:T(8,128)} %param.30) | copy-start | bytes 3076
  68.1 1.0 copy-start.1
  69.1 20.4 %copy-start.6 = (f32[2048]{0:T(1024)S(1)}, f32[2048]{0:T(1024)}, u32[]{:S(2)}) copy-start(f32[2048]{0:T(1024)} %param.27) | copy-start | bytes 24580
  70.0 13.6 %collective-permute-start.3 = (f32[32,2048]{1,0:T(8,128)}, f32[32,2048]{1,0:T(8,128)S(1)}, u32[]{:S(2)}, u32[]{:S(2)}) collective-permute-start(f32[32,2048]{1,0:T(8,128)} %get-tuple-element.4), channel_id=1, source_target_pairs={{0,24},{8,0},{16,8},{24,16},{1,25},{9,1},{17,9},{25,17},{2,26},{10... | collective-permute-start | bytes 786440 | tf_op jit(solution)/shard_map/ppermute | solution.py:238
  72.4 11.3 %collective-permute-start.4 = (f32[32,2048]{1,0:T(8,128)}, f32[32,2048]{1,0:T(8,128)}, u32[]{:S(2)}, u32[]{:S(2)}) collective-permute-start(f32[32,2048]{1,0:T(8,128)} %get-tuple-element.6), channel_id=1, source_target_pairs={{0,16},{8,24},{16,0},{24,8},{1,17},{9,25},{17,1},{25,9},{2,18},{10... | collective-permute-start | bytes 786440 | tf_op jit(solution)/shard_map/ppermute | solution.py:238
  73.0 15.1 %collective-permute-start.5 = (f32[32,2048]{1,0:T(8,128)}, f32[32,2048]{1,0:T(8,128)}, u32[]{:S(2)}, u32[]{:S(2)}) collective-permute-start(f32[32,2048]{1,0:T(8,128)} %get-tuple-element.5), channel_id=1, source_target_pairs={{0,8},{8,16},{16,24},{24,0},{1,9},{9,17},{17,25},{25,1},{2,10},{10... | collective-permute-start | bytes 786440 | tf_op jit(solution)/shard_map/ppermute | solution.py:238
  83.6 0.7 copy-start.2
  146.2 7.5 %copy-start.7 = (f32[16,2,8]{0,2,1:T(8,128)S(1)}, f32[16,2,8]{0,2,1:T(8,128)}, u32[]{:S(2)}) copy-start(f32[16,2,8]{0,2,1:T(8,128)} %param.31) | copy-start | bytes 3076
  146.2 35.9 %all-to-all-start.1 = ((bf16[128,4,2048]{2,1,0:T(4,128)(2,1)}), bf16[128,4,2048]{2,1,0:T(4,128)(2,1)}, u32[]{:S(2)}, u32[]{:S(2)}) async-start(bf16[128,4,2048]{2,1,0:T(4,128)(2,1)} %copy.45), calls=%async_computation.1 | async-start | bytes 4194304 | tf_op jit(solution)/shard_map/all_to_all | solution.py:282
Sparse Core Ops, SparseCore 0:
  9.8 53.4 all-gather.1

commit v8 on v7

--- a/solution.py
+++ b/solution.py
@@ -267,12 +267,12 @@
     ).reshape(experts_all * capacity, rows, top_k)
     placing = jnp.any(placing, axis=2).astype(jnp.bfloat16)
     outgoing = jnp.dot(placing, normed, preferred_element_type=jnp.float32).astype(jnp.bfloat16)
+    ep_axes = ("y", "x", "c")
     arrived = lax.all_to_all(
-        outgoing.reshape(experts_all, capacity, width),
-        ("dp", "y", "x", "c"),
-        split_axis=0,
-        concat_axis=0,
-        tiled=True,
+        outgoing.reshape(dp_size, members, capacity, width), "dp", 0, 0, tiled=True
+    )
+    arrived = lax.all_to_all(arrived, ep_axes, 1, 1, tiled=True).reshape(
+        experts_all, capacity, width
     )
     depth = arrived.shape[1]
     sources = arrived.shape[0] // experts_local
@@ -280,12 +280,9 @@
         arrived.reshape(sources, experts_local, depth, width), expert_gate_up, expert_down
     )
     returned = lax.all_to_all(
-        answer.reshape(sources * experts_local, depth, width),
-        ("dp", "y", "x", "c"),
-        split_axis=0,
-        concat_axis=0,
-        tiled=True,
-    )
+        answer.reshape(dp_size, members, depth, width), ep_axes, 1, 1, tiled=True
+    )
+    returned = lax.all_to_all(returned, "dp", 0, 0, tiled=True)
     slots_all = jnp.arange(experts_all * capacity, dtype=jnp.int32)
     gathering = jnp.sum(
         jnp.where(

time: 197 us -> 249 us (1.26)
  blocking collectives: 36.6 us -> 95.3 us
  matrix products: 20.7 us -> 15 us
  local copies, waits for them, and re-layouts: 26 us -> 30.1 us
  waiting for transfers between devices: 53.7 us -> 49.6 us
    all_to_all x1 -> x3, blocking collectives: 36.6 us -> 95.3 us  [the longest x1 33.9 us: shards(): lax.all_to_all(arrived, ep_axes, 1, 1, tiled=True)]
    dot_general x1, matrix products: 9.14 us -> 3.41 us  [run_experts(): jnp.einsum('sjcd,jdf->sjcf', arriving, expert_gate_up, preferred_element_...]
    all_to_all x0 -> x3, local copies, waits for them, and re-layouts: none -> 5.17 us  [the longest x1 2.62 us: shards(): lax.all_to_all(answer.reshape(dp_size, members, depth, width), ep_axes, 1...]
    all_to_all x1, waiting for transfers between devices: 27.4 us -> 23.2 us  [shards(): returned = lax.all_to_all(returned, 'dp', 0, 0, tiled=True)]
    convert_element_type x1 -> x0, local copies, waits for them, and re-layouts: 2.93 us -> none  [run_experts(): return jnp.einsum('sjcf,jfd->sjcd', active, expert_down, preferred_elemen...]
    reshape x1 -> x2, local copies, waits for them, and re-layouts: 4.09 us -> 5.75 us  [the longest x1 4.13 us: shards(): outgoing.reshape(dp_size, members, capacity, width)]
  transfers between devices with their start and end apart: 8 -> 8, of which waited for: 5 -> 5; matrix products, arithmetic and copies ran while one was open for 7% -> 5% of each run, Pallas kernels for 14% -> 11%
where the time goes in v8:
time: 249 us; the launch traced here: 248 us
  blocking collectives  95.3 us (38%)
  waiting for transfers between devices  49.6 us (20%)
  local copies, waits for them, and re-layouts  30.1 us (12%)
  Pallas kernels  27.4 us (11%)
  matrix products  15 us (6%)
  between operations  14.3 us (6%)
  starting transfers between devices  13.9 us (6%)
  other arithmetic  2.74 us (1%)
    all_to_all x1, blocking collectives, shards(): lax.all_to_all(arrived, ep_axes, 1, 1, tiled=True)  33.9 us
    all_to_all x1, blocking collectives, shards(): lax.all_to_all(answer.reshape(dp_size, members, depth, width), ep_axes, 1...  31.9 us
    all_to_all x1, blocking collectives, shards(): lax.all_to_all(outgoing.reshape(dp_size, members, capacity, width), 'dp',...  29.5 us
    pallas_call x1, Pallas kernels, decode_attention(): pl.pallas_call(kernel, out_shape=jax.ShapeDtypeStruct((requests, steps, h...  27.4 us
    all_to_all x1, waiting for transfers between devices, shards(): returned = lax.all_to_all(returned, 'dp', 0, 0, tiled=True)  23.2 us
    ppermute x6, waiting for transfers between devices, shifted(): lax.ppermute(value, 'y', [(j, (j + shift) % lines) for j in range(lines)])  17 us
    ppermute x6, starting transfers between devices, shifted(): lax.ppermute(value, 'y', [(j, (j + shift) % lines) for j in range(lines)])  9.31 us
    all_gather x1, waiting for transfers between devices, shards(): gathered = lax.all_gather(o_weight, ('x', 'c'), axis=0, tiled=True)  8.71 us
  transfers between devices with their start and end apart: 8, of which 5 were waited for; matrix products, arithmetic and copies ran while one was open for 5% of the time, Pallas kernels for 11%

profile of v8, /device:TPU:1, one launch (start us, length us, event | category | flops | bytes accessed | tf_op | source)
XLA Modules:
  0.0 248.2 jit_solution(5972491548142962472)
XLA Ops:
  7.2 0.0 copy-start
  7.2 0.0 copy-start.8
  7.2 0.0 copy-start.9
  7.2 0.0 all-gather.2.cloned.1.call-start
  7.3 0.7 all-gather.2.cloned.1.call-update
  8.0 2.4 reshape.107.q_ref
  10.4 0.1 copy.50
  10.5 0.6 reshape.104.flag_ref
  11.1 0.1 copy.51
  11.2 0.7 reshape.105.share_ref
  11.9 0.0 copy-done.10
  11.9 0.1 copy.52
  12.0 0.6 reshape.106.weight_ref
  12.6 27.4 %shard_map.167 = bf16[16,2,64,128]{3,2,1,0:T(8,128)(2,1)} custom-call(s32[16]{0:T(128)} %len_ref.1, s32[128]{0:T(128)} %reshape.104.flag_ref, f32[128]{0:T(128)} %reshape.105.share_ref, f32[64]{0:T(128)} %reshape.106.weight_ref, bf16[16,2,64,128]{3,2,1,0:T(8,128)(2,1)} %reshape.107.q_ref, bf16[16,2,512]{2,1,0:T(2,128)(2,1)} %kn_ref.1, ...), custom_call_target="tpu_custom_call" | custom-call | tf_op jit(solution)/shard_map/pallas_call | solution.py:160
  40.0 0.0 copy-start.3
  40.0 0.0 copy-start.4
  40.0 2.2 copy.62
  42.2 1.8 constant_dynamic-slice_fusion.3
  44.1 2.0 collective-permute-start
  46.0 2.5 collective-permute-start.1
  48.5 1.3 collective-permute-start.2
  49.8 0.7 reshape.117
  50.5 0.0 copy-done.4
  50.5 0.1 copy.54
  50.6 0.1 eq.47
  50.7 0.2 convert_reduce_fusion
  50.9 0.1 reduce_sum.30
  51.0 0.0 collective-permute-done
  51.0 3.4 %collective-permute-done.1 = bf16[32,2048]{1,0:T(8,128)(2,1)} collective-permute-done((bf16[32,2048]{1,0:T(8,128)(2,1)}, bf16[32,2048]{1,0:T(8,128)(2,1)}, u32[]{:S(2)}, u32[]{:S(2)}) %collective-permute-start.1) | collective-permute-done | bytes 131104 | tf_op jit(solution)/shard_map/ppermute | solution.py:238
  54.4 0.0 collective-permute-done.2
  54.4 8.7 %all-gather.2.cloned.1.call-done = bf16[2048,2048]{1,0:T(8,128)(2,1)} async-done(((bf16[256,2048]{1,0:T(8,128)(2,1)}), bf16[2048,2048]{1,0:T(8,128)(2,1)}) %all-gather.2.cloned.1.call-update) | async-done | bytes 8388624 | tf_op jit(solution)/shard_map/all_gather | solution.py:231
  63.1 4.9 %fusion.14 = f32[128,2048]{1,0:T(8,128)S(1)} fusion(bf16[2048,2048]{1,0:T(8,128)(2,1)} %all-gather.2.cloned.1.call-done, bf16[32,2048]{1,0:T(8,128)(2,1)} %collective-permute-done.2, bf16[32,2048]{1,0:T(8,128)(2,1)} %collective-permute-done.1, bf16[32,2048]{1,0:T(8,128)(2,1)} %collective-permute-done, bf16[32,2048]{1,0:T(8,128)(2,1)S(1)} %get-tuple-element.7), kind=kOutput, calls=%fused_computation.13 | convolution fusion | flops 1075838976 | bytes 9961472 | tf_op jit(solution)/shard_map/dot_general | solution.py:244
  68.0 1.0 copy-done.1
  69.0 0.9 fusion.32
  69.9 2.5 %collective-permute-start.3 = (f32[32,2048]{1,0:T(8,128)}, f32[32,2048]{1,0:T(8,128)S(1)}, u32[]{:S(2)}, u32[]{:S(2)}) collective-permute-start(f32[32,2048]{1,0:T(8,128)} %get-tuple-element.4), channel_id=1, source_target_pairs={{0,24},{8,0},{16,8},{24,16},{1,25},{9,1},{17,9},{25,17},{2,26},{10... | collective-permute-start | bytes 786440 | tf_op jit(solution)/shard_map/ppermute | solution.py:238
  72.4 0.5 collective-permute-start.4
  72.9 0.6 collective-permute-start.5
  73.5 0.1 copy.53
  73.6 0.2 fusion.22
  73.8 9.8 %collective-permute-done.3 = f32[32,2048]{1,0:T(8,128)S(1)} collective-permute-done((f32[32,2048]{1,0:T(8,128)}, f32[32,2048]{1,0:T(8,128)S(1)}, u32[]{:S(2)}, u32[]{:S(2)}) %collective-permute-start.3) | collective-permute-done | bytes 262176 | tf_op jit(solution)/shard_map/ppermute | solution.py:238
  83.7 0.0 collective-permute-done.4
  83.7 0.7 copy-done.2
  84.4 3.7 %collective-permute-done.5 = f32[32,2048]{1,0:T(8,128)} collective-permute-done((f32[32,2048]{1,0:T(8,128)}, f32[32,2048]{1,0:T(8,128)}, u32[]{:S(2)}, u32[]{:S(2)}) %collective-permute-start.5) | collective-permute-done | bytes 262176 | tf_op jit(solution)/shard_map/ppermute | solution.py:238
  88.1 1.4 multiply_reduce_fusion
  89.5 2.1 convolution_convert_fusion
  91.7 4.1 %reshape.109 = bf16[4,32,4,2048]{3,2,1,0:T(4,128)(2,1)} reshape(bf16[512,2048]{1,0:T(8,128)(2,1)} %convolution_convert_fusion) | data formatting | bytes 4194304 | tf_op jit(solution)/shard_map/reshape | solution.py:272
  95.8 29.5 %all_to_all.20 = bf16[4,32,4,2048]{3,2,1,0:T(4,128)(2,1)S(1)} all-to-all(bf16[4,32,4,2048]{3,2,1,0:T(4,128)(2,1)} %reshape.109), channel_id=1, replica_groups=mesh['dp'=4,'y'=4,'x'=4,'c'=2] {'dp'}, dimensions={0} | all-to-all | bytes 4194304 | tf_op jit(solution)/shard_map/all_to_all | solution.py:271
  125.2 1.4 copy.56
  126.7 0.0 slice-start.1
  126.7 33.9 %all_to_all.21 = bf16[4,32,4,2048]{3,2,0,1:T(4,128)(2,1)S(1)} all-to-all(bf16[4,32,4,2048]{3,2,0,1:T(4,128)(2,1)S(1)} %copy.56), channel_id=1, replica_groups=mesh['dp'=4,'y'=4,'x'=4,'c'=2] {'y','x','c'}, dimensions={1} | all-to-all | bytes 4194304 | tf_op jit(solution)/shard_map/all_to_all | solution.py:274
  160.5 1.2 copy.57
  161.7 3.4 %fusion.2 = f32[128,1,4,1536]{3,0,2,1:T(8,128)S(1)} fusion(bf16[128,4,2048]{2,0,1:T(8,128)(2,1)S(1)} %bitcast.44, bf16[1,2048,1536]{2,1,0:T(8,128)(2,1)S(1)} %bitcast.50), kind=kOutput, calls=%fused_computation.2 | convolution fusion | flops 3221225472 | bytes 11534336 | tf_op jit(solution)/shard_map/sjcd,jdf->sjcf/dot_general | solution.py:190
  165.1 1.8 fusion.7
  167.0 1.6 copy.58
  168.6 31.9 %all_to_all.22 = bf16[4,32,4,2048]{3,2,0,1:T(4,128)(2,1)S(1)} all-to-all(bf16[4,32,4,2048]{3,2,0,1:T(4,128)(2,1)S(1)} %copy.58), channel_id=1, replica_groups=mesh['dp'=4,'y'=4,'x'=4,'c'=2] {'y','x','c'}, dimensions={1} | all-to-all | bytes 4194304 | tf_op jit(solution)/shard_map/all_to_all | solution.py:282
  200.5 2.6 %copy.59 = bf16[4,32,4,2048]{3,2,1,0:T(4,128)(2,1)} copy(bf16[4,32,4,2048]{3,2,0,1:T(4,128)(2,1)S(1)} %all_to_all.22) | data formatting | bytes 4194304 | tf_op jit(solution)/shard_map/all_to_all | solution.py:282
  203.2 4.6 %all-to-all-start.3 = ((bf16[4,32,4,2048]{3,2,1,0:T(4,128)(2,1)}), bf16[4,32,4,2048]{3,2,1,0:T(4,128)(2,1)}, u32[]{:S(2)}, u32[]{:S(2)}) async-start(bf16[4,32,4,2048]{3,2,1,0:T(4,128)(2,1)} %copy.59), calls=%async_computation.3 | async-start | bytes 4194304 | tf_op jit(solution)/shard_map/all_to_all | solution.py:285
  207.7 2.0 reshape.108
  209.7 0.1 copy.55
  209.8 0.9 select_reduce_fusion
  210.6 23.2 %all-to-all-done.3 = bf16[4,32,4,2048]{3,2,1,0:T(4,128)(2,1)} async-done(((bf16[4,32,4,2048]{3,2,1,0:T(4,128)(2,1)}), bf16[4,32,4,2048]{3,2,1,0:T(4,128)(2,1)}, u32[]{:S(2)}, u32[]{:S(2)}) %all-to-all-start.3) | async-done | bytes 2097184 | tf_op jit(solution)/shard_map/all_to_all | solution.py:285
  233.9 4.0 %reshape.115 = bf16[512,2048]{1,0:T(8,128)(2,1)} reshape(bf16[4,32,4,2048]{3,2,1,0:T(4,128)(2,1)} %all-to-all-done.3) | data formatting | bytes 4194304 | tf_op jit(solution)/shard_map/reshape | solution.py:297
  237.8 2.7 %fusion.10 = bf16[32,2048]{1,0:T(8,128)(2,1)S(1)} fusion(f32[32,2048]{1,0:T(8,128)S(1)} %get-tuple-element.3, f32[32,512]{1,0:T(8,128)} %select_reduce_fusion, bf16[512,2048]{1,0:T(8,128)(2,1)} %reshape.115), kind=kOutput, calls=%fused_computation.8 | convolution fusion | flops 402784256 | bytes 2555904 | tf_op jit(solution)/shard_map/dot_general | solution.py:295
  240.6 0.8 reshape.116
  (20 shorter events, 0.1 us)
Async XLA Ops:
  7.2 158.0 %copy-start = (bf16[1,768,2048]{2,1,0:T(8,128)(2,1)S(1)}, bf16[1,768,2048]{2,1,0:T(8,128)(2,1)}, u32[]{:S(2)}) copy-start(bf16[1,768,2048]{2,1,0:T(8,128)(2,1)} %param.29) | copy-start | bytes 9437188
  7.2 3.2 %copy-start.8 = (s32[16,2,4]{0,2,1:T(4,128)S(1)}, s32[16,2,4]{0,2,1:T(4,128)}, u32[]{:S(2)}) copy-start(s32[16,2,4]{0,2,1:T(4,128)} %param.20) | copy-start | bytes 1540
  7.2 3.9 %copy-start.9 = (f32[16,2,4]{0,2,1:T(4,128)S(1)}, f32[16,2,4]{0,2,1:T(4,128)}, u32[]{:S(2)}) copy-start(f32[16,2,4]{0,2,1:T(4,128)} %param.19) | copy-start | bytes 1540
  7.2 4.7 %copy-start.10 = (f32[16,4]{0,1:T(4,128)S(1)}, f32[16,4]{0,1:T(4,128)}, u32[]{:S(2)}) copy-start(f32[16,4]{0,1:T(4,128)} %param.23) | copy-start | bytes 772
  7.2 55.9 %all-gather.2.cloned.1.call-start = ((), (), s32[]{:S(2)}) async-start(), calls=%async_computation.4 | async-start | bytes 9437184 | tf_op jit(solution)/shard_map/all_gather | solution.py:231
  40.0 9.8 %copy-start.3 = (bf16[16,2,2048]{2,1,0:T(2,128)(2,1)S(1)}, bf16[16,2,2048]{2,1,0:T(2,128)(2,1)}, u32[]{:S(2)}) copy-start(bf16[16,2,2048]{2,1,0:T(2,128)(2,1)} %param.25) | copy-start | bytes 393220
  40.0 10.6 %copy-start.4 = (s32[16,2,8]{0,2,1:T(8,128)S(1)}, s32[16,2,8]{0,2,1:T(8,128)}, u32[]{:S(2)}) copy-start(s32[16,2,8]{0,2,1:T(8,128)} %param.30) | copy-start | bytes 3076
  44.1 6.9 %collective-permute-start = (bf16[32,2048]{1,0:T(8,128)(2,1)}, bf16[32,2048]{1,0:T(8,128)(2,1)}, u32[]{:S(2)}, u32[]{:S(2)}) collective-permute-start(bf16[32,2048]{1,0:T(8,128)(2,1)} %get-tuple-element.10), channel_id=1, source_target_pairs={{0,8},{8,16},{16,24},{24,0},{1,9},{9,17},{17,25},{25,1},{2,10},{10... | collective-permute-start | bytes 393224 | tf_op jit(solution)/shard_map/ppermute | solution.py:238
  46.0 8.4 %collective-permute-start.1 = (bf16[32,2048]{1,0:T(8,128)(2,1)}, bf16[32,2048]{1,0:T(8,128)(2,1)}, u32[]{:S(2)}, u32[]{:S(2)}) collective-permute-start(bf16[32,2048]{1,0:T(8,128)(2,1)} %get-tuple-element.9), channel_id=1, source_target_pairs={{0,16},{8,24},{16,0},{24,8},{1,17},{9,25},{17,1},{25,9},{2,18},{10... | collective-permute-start | bytes 393224 | tf_op jit(solution)/shard_map/ppermute | solution.py:238
  48.5 5.9 %collective-permute-start.2 = (bf16[32,2048]{1,0:T(8,128)(2,1)S(1)}, bf16[32,2048]{1,0:T(8,128)(2,1)}, u32[]{:S(2)}, u32[]{:S(2)}) collective-permute-start(bf16[32,2048]{1,0:T(8,128)(2,1)S(1)} %get-tuple-element.8), channel_id=1, source_target_pairs={{0,24},{8,0},{16,8},{24,16},{1,25},{9,1},{17,9},{25,17},{2,26},{10... | collective-permute-start | bytes 393224 | tf_op jit(solution)/shard_map/ppermute | solution.py:238
  63.1 10.4 %copy-start.5 = (s32[16,2,8]{0,2,1:T(8,128)S(1)}, s32[16,2,8]{0,2,1:T(8,128)}, u32[]{:S(2)}) copy-start(s32[16,2,8]{0,2,1:T(8,128)} %param.30) | copy-start | bytes 3076
  68.0 1.0 copy-start.1
  69.0 20.5 %copy-start.6 = (f32[2048]{0:T(1024)S(1)}, f32[2048]{0:T(1024)}, u32[]{:S(2)}) copy-start(f32[2048]{0:T(1024)} %param.27) | copy-start | bytes 24580
  69.9 13.8 %collective-permute-start.3 = (f32[32,2048]{1,0:T(8,128)}, f32[32,2048]{1,0:T(8,128)S(1)}, u32[]{:S(2)}, u32[]{:S(2)}) collective-permute-start(f32[32,2048]{1,0:T(8,128)} %get-tuple-element.4), channel_id=1, source_target_pairs={{0,24},{8,0},{16,8},{24,16},{1,25},{9,1},{17,9},{25,17},{2,26},{10... | collective-permute-start | bytes 786440 | tf_op jit(solution)/shard_map/ppermute | solution.py:238
  72.4 11.3 %collective-permute-start.4 = (f32[32,2048]{1,0:T(8,128)}, f32[32,2048]{1,0:T(8,128)}, u32[]{:S(2)}, u32[]{:S(2)}) collective-permute-start(f32[32,2048]{1,0:T(8,128)} %get-tuple-element.6), channel_id=1, source_target_pairs={{0,16},{8,24},{16,0},{24,8},{1,17},{9,25},{17,1},{25,9},{2,18},{10... | collective-permute-start | bytes 786440 | tf_op jit(solution)/shard_map/ppermute | solution.py:238
  72.9 15.2 %collective-permute-start.5 = (f32[32,2048]{1,0:T(8,128)}, f32[32,2048]{1,0:T(8,128)}, u32[]{:S(2)}, u32[]{:S(2)}) collective-permute-start(f32[32,2048]{1,0:T(8,128)} %get-tuple-element.5), channel_id=1, source_target_pairs={{0,8},{8,16},{16,24},{24,0},{1,9},{9,17},{17,25},{25,1},{2,10},{10... | collective-permute-start | bytes 786440 | tf_op jit(solution)/shard_map/ppermute | solution.py:238
  83.7 0.7 copy-start.2
  125.2 36.4 %slice-start = ((s8[6291456]{0:T(1024)(128)(4,1)}), s8[4194304]{0:T(1024)(128)(4,1)S(1)}, s32[]{:S(2)}) async-start(s8[6291456]{0:T(1024)(128)(4,1)} %bitcast.49), calls=%async_computation.5 | async-start | bytes 8388608
  126.7 35.1 %slice-start.1 = ((s8[6291456]{0:T(1024)(128)(4,1)}), s8[2097152]{0:T(1024)(128)(4,1)S(1)}, s32[]{:S(2)}) async-start(s8[6291456]{0:T(1024)(128)(4,1)} %bitcast.49), calls=%async_computation.6 | async-start | bytes 4194304
  203.2 6.5 %copy-start.7 = (f32[16,2,8]{0,2,1:T(8,128)S(1)}, f32[16,2,8]{0,2,1:T(8,128)}, u32[]{:S(2)}) copy-start(f32[16,2,8]{0,2,1:T(8,128)} %param.31) | copy-start | bytes 3076
  203.2 30.7 %all-to-all-start.3 = ((bf16[4,32,4,2048]{3,2,1,0:T(4,128)(2,1)}), bf16[4,32,4,2048]{3,2,1,0:T(4,128)(2,1)}, u32[]{:S(2)}, u32[]{:S(2)}) async-start(bf16[4,32,4,2048]{3,2,1,0:T(4,128)(2,1)} %copy.59), calls=%async_computation.3 | async-start | bytes 4194304 | tf_op jit(solution)/shard_map/all_to_all | solution.py:285
Sparse Core Ops, SparseCore 0:
  9.8 53.3 all-gather.1

commit v9 on v7

--- a/solution.py
+++ b/solution.py
@@ -246,7 +246,8 @@
     ).reshape(lines, rows, width)
     projected = partials[0]
     for shift in range(1, lines):
-        projected = projected + shifted(partials[shift], lines - shift)
+        sent = shifted(partials[shift].astype(jnp.bfloat16), lines - shift)
+        projected = projected + sent.astype(jnp.float32)
     members = lax.axis_size("y") * lax.axis_size("x") * lax.axis_size("c")
     mixed = residual.reshape(rows, width).astype(jnp.float32) + projected
     normed = (

time: 197 us -> 192 us (0.975)
  waiting for transfers between devices: 53.7 us -> 46.4 us
    ppermute x6, waiting for transfers between devices: 16.8 us -> 9.65 us  [shifted(): lax.ppermute(value, 'y', [(j, (j + shift) % lines) for j in range(lines)])]
    unnamed x28 -> x24, local copies, waits for them, and re-layouts: 4.35 us -> 3.35 us
  transfers between devices with their start and end apart: 8 -> 8, of which waited for: 5 -> 6; matrix products, arithmetic and copies ran while one was open for 7% -> 8% of each run, Pallas kernels for 14% -> 14%
where the time goes in v9:
time: 192 us; the launch traced here: 191 us
  waiting for transfers between devices  46.4 us (24%)
  blocking collectives  36.7 us (19%)
  Pallas kernels  27.2 us (14%)
  local copies, waits for them, and re-layouts  25.6 us (13%)
  matrix products  22.5 us (12%)
  starting transfers between devices  15 us (8%)
  between operations  14.2 us (7%)
  other arithmetic  3.94 us (2%)
    all_to_all x1, blocking collectives, shards(): lax.all_to_all(outgoing.reshape(experts_all, capacity, width), ('dp', 'y'...  36.7 us
    all_to_all x1, waiting for transfers between devices, shards(): lax.all_to_all(answer.reshape(sources * experts_local, depth, width), ('d...  27.4 us
    pallas_call x1, Pallas kernels, decode_attention(): pl.pallas_call(kernel, out_shape=jax.ShapeDtypeStruct((requests, steps, h...  27.2 us
    ppermute x6, waiting for transfers between devices, shifted(): lax.ppermute(value, 'y', [(j, (j + shift) % lines) for j in range(lines)])  9.65 us
    ppermute x6, starting transfers between devices, shifted(): lax.ppermute(value, 'y', [(j, (j + shift) % lines) for j in range(lines)])  9.39 us
    dot_general x1, matrix products, run_experts(): jnp.einsum('sjcd,jdf->sjcf', arriving, expert_gate_up, preferred_element_...  9.14 us
    all_gather x1, waiting for transfers between devices, shards(): gathered = lax.all_gather(o_weight, ('x', 'c'), axis=0, tiled=True)  8.67 us
    dot_general x1, matrix products, shards(): jnp.dot(jnp.concatenate(pieces, axis=0), gathered, preferred_element_type...  5.96 us
  transfers between devices with their start and end apart: 8, of which 6 were waited for; matrix products, arithmetic and copies ran while one was open for 8% of the time, Pallas kernels for 14%

profile of v9, /device:TPU:1, one launch (start us, length us, event | category | flops | bytes accessed | tf_op | source)
XLA Modules:
  0.0 191.4 jit_solution(3856224399704997569)
XLA Ops:
  7.2 0.0 copy-start
  7.2 0.0 copy-start.6
  7.2 0.0 copy-start.7
  7.2 0.0 copy-start.8
  7.2 0.0 all-gather.2.cloned.1.call-start
  7.3 0.7 all-gather.2.cloned.1.call-update
  8.0 2.4 %reshape.104.q_ref = bf16[16,2,64,128]{3,2,1,0:T(8,128)(2,1)} reshape(bf16[16,2,8192]{2,1,0:T(2,128)(2,1)} %param.16) | data formatting | bytes 1048576 | tf_op jit(solution)/shard_map/reshape | solution.py:179
  10.4 0.0 copy-done.6
  10.4 0.1 copy.38
  10.5 0.6 reshape.101.flag_ref
  11.1 0.0 copy-done.7
  11.1 0.1 copy.39
  11.2 0.7 reshape.102.share_ref
  11.9 0.0 copy-done.8
  11.9 0.1 copy.40
  12.0 0.7 reshape.103.weight_ref
  12.6 27.2 %shard_map.167 = bf16[16,2,64,128]{3,2,1,0:T(8,128)(2,1)} custom-call(s32[16]{0:T(128)} %len_ref.1, s32[128]{0:T(128)} %reshape.101.flag_ref, f32[128]{0:T(128)} %reshape.102.share_ref, f32[64]{0:T(128)} %reshape.103.weight_ref, bf16[16,2,64,128]{3,2,1,0:T(8,128)(2,1)} %reshape.104.q_ref, bf16[16,2,512]{2,1,0:T(2,128)(2,1)} %kn_ref.1, ...), custom_call_target="tpu_custom_call" | custom-call | tf_op jit(solution)/shard_map/pallas_call | solution.py:160
  39.8 2.2 %copy.50 = bf16[4,8,64,128]{3,1,2,0:T(8,128)(2,1)} copy(bf16[4,8,64,128]{3,2,1,0:T(8,128)(2,1)} %bitcast.34) | data formatting | bytes 1048576
  42.0 1.8 constant_dynamic-slice_fusion.3
  43.8 2.0 %collective-permute-start = (bf16[32,2048]{1,0:T(8,128)(2,1)}, bf16[32,2048]{1,0:T(8,128)(2,1)}, u32[]{:S(2)}, u32[]{:S(2)}) collective-permute-start(bf16[32,2048]{1,0:T(8,128)(2,1)} %get-tuple-element.10), channel_id=1, source_target_pairs={{0,8},{8,16},{16,24},{24,0},{1,9},{9,17},{17,25},{25,1},{2,10},{10... | collective-permute-start | bytes 393224 | tf_op jit(solution)/shard_map/ppermute | solution.py:238
  45.9 2.7 %collective-permute-start.1 = (bf16[32,2048]{1,0:T(8,128)(2,1)S(1)}, bf16[32,2048]{1,0:T(8,128)(2,1)}, u32[]{:S(2)}, u32[]{:S(2)}) collective-permute-start(bf16[32,2048]{1,0:T(8,128)(2,1)S(1)} %get-tuple-element.9), channel_id=1, source_target_pairs={{0,16},{8,24},{16,0},{24,8},{1,17},{9,25},{17,1},{25,9},{2,18},{10... | collective-permute-start | bytes 393224 | tf_op jit(solution)/shard_map/ppermute | solution.py:238
  48.6 1.1 collective-permute-start.2
  49.7 0.8 copy.42
  50.5 0.7 eq.47
  51.1 1.3 broadcast_multiply_fusion
  52.4 0.0 collective-permute-done
  52.4 2.1 %collective-permute-done.1 = bf16[32,2048]{1,0:T(8,128)(2,1)} collective-permute-done((bf16[32,2048]{1,0:T(8,128)(2,1)S(1)}, bf16[32,2048]{1,0:T(8,128)(2,1)}, u32[]{:S(2)}, u32[]{:S(2)}) %collective-permute-start.1) | collective-permute-done | bytes 131104 | tf_op jit(solution)/shard_map/ppermute | solution.py:238
  54.5 0.0 collective-permute-done.2
  54.5 8.7 %all-gather.2.cloned.1.call-done = bf16[2048,2048]{1,0:T(8,128)(2,1)} async-done(((bf16[256,2048]{1,0:T(8,128)(2,1)}), bf16[2048,2048]{1,0:T(8,128)(2,1)}) %all-gather.2.cloned.1.call-update) | async-done | bytes 8388624 | tf_op jit(solution)/shard_map/all_gather | solution.py:231
  63.2 0.0 copy-start.4
  63.2 6.0 %fusion.34 = (bf16[128,2048]{1,0:T(8,128)(2,1)S(1)}, f32[128,2048]{1,0:T(8,128)}) fusion(bf16[2048,2048]{1,0:T(8,128)(2,1)} %all-gather.2.cloned.1.call-done, bf16[32,2048]{1,0:T(8,128)(2,1)} %collective-permute-done.2, bf16[32,2048]{1,0:T(8,128)(2,1)} %collective-permute-done.1, bf16[32,2048]{1,0:T(8,128)(2,1)} %collective-permute-done, ...), kind=kOutput, calls=%fused_computation.46 | convolution fusion | flops 1076101120 | bytes 10485760 | tf_op jit(solution)/shard_map/dot_general | solution.py:244
  69.2 0.8 fusion.33
  69.9 2.4 %collective-permute-start.3 = (bf16[32,2048]{1,0:T(8,128)(2,1)}, bf16[32,2048]{1,0:T(8,128)(2,1)S(1)}, u32[]{:S(2)}, u32[]{:S(2)}) collective-permute-start(bf16[32,2048]{1,0:T(8,128)(2,1)} %get-tuple-element.4), channel_id=1, source_target_pairs={{0,24},{8,0},{16,8},{24,16},{1,25},{9,1},{17,9},{25,17},{2,26},{10... | collective-permute-start | bytes 393224 | tf_op jit(solution)/shard_map/ppermute | solution.py:238
  72.3 0.5 collective-permute-start.4
  72.9 0.6 collective-permute-start.5
  73.5 0.0 copy-done.4
  73.5 0.2 convert_reduce_fusion
  73.6 0.0 copy-done.1
  73.6 0.7 reshape.112
  74.4 0.1 reduce_sum.30
  74.5 0.0 copy-done.3
  74.5 0.1 copy.41
  74.6 0.2 fusion.23
  74.8 3.1 %collective-permute-done.3 = bf16[32,2048]{1,0:T(8,128)(2,1)S(1)} collective-permute-done((bf16[32,2048]{1,0:T(8,128)(2,1)}, bf16[32,2048]{1,0:T(8,128)(2,1)S(1)}, u32[]{:S(2)}, u32[]{:S(2)}) %collective-permute-start.3) | collective-permute-done | bytes 131104 | tf_op jit(solution)/shard_map/ppermute | solution.py:238
  77.9 0.6 collective-permute-done.4
  78.6 3.8 %collective-permute-done.5 = bf16[32,2048]{1,0:T(8,128)(2,1)} collective-permute-done((bf16[32,2048]{1,0:T(8,128)(2,1)}, bf16[32,2048]{1,0:T(8,128)(2,1)}, u32[]{:S(2)}, u32[]{:S(2)}) %collective-permute-start.5) | collective-permute-done | bytes 131104 | tf_op jit(solution)/shard_map/ppermute | solution.py:238
  82.4 0.0 copy-done.2
  82.4 1.3 multiply_reduce_fusion
  83.7 2.8 %convolution_convert_fusion = bf16[512,2048]{1,0:T(8,128)(2,1)} fusion(pred[512,32]{0,1:T(8,128)(4,1)S(1)} %fusion.23, f32[32,2048]{1,0:T(8,128)S(1)} %get-tuple-element.3, f32[2048]{0:T(1024)} %param.27, f32[32]{0:T(128)S(1)} %add_rsqrt_fusion), kind=kOutput, calls=%fused_computation.6 | convolution fusion | flops 68354048 | bytes 2384000 | tf_op jit(solution)/shard_map/dot_general | solution.py:270
  86.5 4.1 %reshape.106 = bf16[128,4,2048]{2,1,0:T(4,128)(2,1)} reshape(bf16[512,2048]{1,0:T(8,128)(2,1)} %convolution_convert_fusion) | data formatting | bytes 4194304 | tf_op jit(solution)/shard_map/reshape | solution.py:272
  90.6 36.7 %all_to_all.10 = bf16[128,4,2048]{2,1,0:T(4,128)(2,1)S(1)} all-to-all(bf16[128,4,2048]{2,1,0:T(4,128)(2,1)} %reshape.106), channel_id=1, replica_groups=mesh['dp'=4,'y'=4,'x'=4,'c'=2] {'dp','y','x','c'}, dimensions={0} | all-to-all | bytes 4194304 | tf_op jit(solution)/shard_map/all_to_all | solution.py:271
  127.3 9.1 %fusion.2 = f32[128,1,4,1536]{3,0,2,1:T(8,128)S(1)} fusion(bf16[1,2048,1536]{2,1,0:T(8,128)(2,1)} %param.28, bf16[128,4,2048]{2,1,0:T(4,128)(2,1)S(1)} %all_to_all.10), kind=kOutput, calls=%fused_computation.2 | convolution fusion | flops 3221225472 | bytes 11534336 | tf_op jit(solution)/shard_map/sjcd,jdf->sjcf/dot_general | solution.py:190
  136.5 0.0 copy-done
  136.5 1.8 fusion.7
  138.3 2.9 %copy.45 = bf16[128,4,2048]{2,1,0:T(4,128)(2,1)} copy(bf16[128,4,2048]{2,0,1:T(8,128)(2,1)S(1)} %fusion.7) | data formatting | bytes 4194304 | tf_op jit(solution)/shard_map/convert_element_type | solution.py:196
  141.2 5.6 %all-to-all-start.1 = ((bf16[128,4,2048]{2,1,0:T(4,128)(2,1)}), bf16[128,4,2048]{2,1,0:T(4,128)(2,1)}, u32[]{:S(2)}, u32[]{:S(2)}) async-start(bf16[128,4,2048]{2,1,0:T(4,128)(2,1)} %copy.45), calls=%async_computation.1 | async-start | bytes 4194304 | tf_op jit(solution)/shard_map/all_to_all | solution.py:283
  146.8 2.0 %reshape.105 = bf16[16,2,8192]{2,1,0:T(2,128)(2,1)} reshape(bf16[16,2,64,128]{3,2,1,0:T(8,128)(2,1)} %shard_map.167) | data formatting | bytes 1048576 | tf_op jit(solution)/shard_map/reshape | solution.py:185
  148.8 0.0 copy-done.5
  148.8 0.1 copy.43
  148.8 0.9 select_reduce_fusion
  149.7 27.4 %all-to-all-done.1 = bf16[128,4,2048]{2,1,0:T(4,128)(2,1)} async-done(((bf16[128,4,2048]{2,1,0:T(4,128)(2,1)}), bf16[128,4,2048]{2,1,0:T(4,128)(2,1)}, u32[]{:S(2)}, u32[]{:S(2)}) %all-to-all-start.1) | async-done | bytes 2097184 | tf_op jit(solution)/shard_map/all_to_all | solution.py:283
  177.1 4.0 %reshape.110 = bf16[512,2048]{1,0:T(8,128)(2,1)} reshape(bf16[128,4,2048]{2,1,0:T(4,128)(2,1)} %all-to-all-done.1) | data formatting | bytes 4194304 | tf_op jit(solution)/shard_map/reshape | solution.py:301
  181.1 2.7 %fusion.10 = bf16[32,2048]{1,0:T(8,128)(2,1)S(1)} fusion(f32[32,2048]{1,0:T(8,128)S(1)} %get-tuple-element.3, f32[32,512]{1,0:T(8,128)} %select_reduce_fusion, bf16[512,2048]{1,0:T(8,128)(2,1)} %reshape.110), kind=kOutput, calls=%fused_computation.8 | convolution fusion | flops 402784256 | bytes 2555904 | tf_op jit(solution)/shard_map/dot_general | solution.py:299
  183.8 0.8 reshape.111
  (6 shorter events, 0.0 us)
Async XLA Ops:
  7.2 129.3 %copy-start = (bf16[1,768,2048]{2,1,0:T(8,128)(2,1)S(1)}, bf16[1,768,2048]{2,1,0:T(8,128)(2,1)}, u32[]{:S(2)}) copy-start(bf16[1,768,2048]{2,1,0:T(8,128)(2,1)} %param.29) | copy-start | bytes 9437188
  7.2 3.2 %copy-start.6 = (s32[16,2,4]{0,2,1:T(4,128)S(1)}, s32[16,2,4]{0,2,1:T(4,128)}, u32[]{:S(2)}) copy-start(s32[16,2,4]{0,2,1:T(4,128)} %param.20) | copy-start | bytes 1540
  7.2 3.9 %copy-start.7 = (f32[16,2,4]{0,2,1:T(4,128)S(1)}, f32[16,2,4]{0,2,1:T(4,128)}, u32[]{:S(2)}) copy-start(f32[16,2,4]{0,2,1:T(4,128)} %param.19) | copy-start | bytes 1540
  7.2 4.7 %copy-start.8 = (f32[16,4]{0,1:T(4,128)S(1)}, f32[16,4]{0,1:T(4,128)}, u32[]{:S(2)}) copy-start(f32[16,4]{0,1:T(4,128)} %param.23) | copy-start | bytes 772
  7.2 56.0 %all-gather.2.cloned.1.call-start = ((), (), s32[]{:S(2)}) async-start(), calls=%async_computation.2 | async-start | bytes 9437184 | tf_op jit(solution)/shard_map/all_gather | solution.py:231
  43.8 8.6 %collective-permute-start = (bf16[32,2048]{1,0:T(8,128)(2,1)}, bf16[32,2048]{1,0:T(8,128)(2,1)}, u32[]{:S(2)}, u32[]{:S(2)}) collective-permute-start(bf16[32,2048]{1,0:T(8,128)(2,1)} %get-tuple-element.10), channel_id=1, source_target_pairs={{0,8},{8,16},{16,24},{24,0},{1,9},{9,17},{17,25},{25,1},{2,10},{10... | collective-permute-start | bytes 393224 | tf_op jit(solution)/shard_map/ppermute | solution.py:238
  45.9 8.6 %collective-permute-start.1 = (bf16[32,2048]{1,0:T(8,128)(2,1)S(1)}, bf16[32,2048]{1,0:T(8,128)(2,1)}, u32[]{:S(2)}, u32[]{:S(2)}) collective-permute-start(bf16[32,2048]{1,0:T(8,128)(2,1)S(1)} %get-tuple-element.9), channel_id=1, source_target_pairs={{0,16},{8,24},{16,0},{24,8},{1,17},{9,25},{17,1},{25,9},{2,18},{10... | collective-permute-start | bytes 393224 | tf_op jit(solution)/shard_map/ppermute | solution.py:238
  48.6 5.9 %collective-permute-start.2 = (bf16[32,2048]{1,0:T(8,128)(2,1)S(1)}, bf16[32,2048]{1,0:T(8,128)(2,1)}, u32[]{:S(2)}, u32[]{:S(2)}) collective-permute-start(bf16[32,2048]{1,0:T(8,128)(2,1)S(1)} %get-tuple-element.8), channel_id=1, source_target_pairs={{0,24},{8,0},{16,8},{24,16},{1,25},{9,1},{17,9},{25,17},{2,26},{10... | collective-permute-start | bytes 393224 | tf_op jit(solution)/shard_map/ppermute | solution.py:238
  63.2 10.3 %copy-start.4 = (s32[256]{0:T(256)S(1)}, s32[256]{0:T(256)}, u32[]{:S(2)}) copy-start(s32[256]{0:T(256)} %eq.47) | copy-start | bytes 3076
  63.2 10.4 %copy-start.1 = (bf16[16,2,2048]{2,1,0:T(2,128)(2,1)S(1)}, bf16[16,2,2048]{2,1,0:T(2,128)(2,1)}, u32[]{:S(2)}) copy-start(bf16[16,2,2048]{2,1,0:T(2,128)(2,1)} %param.25) | copy-start | bytes 393220
  63.2 11.3 %copy-start.3 = (s32[16,2,8]{0,2,1:T(8,128)S(1)}, s32[16,2,8]{0,2,1:T(8,128)}, u32[]{:S(2)}) copy-start(s32[16,2,8]{0,2,1:T(8,128)} %broadcast_multiply_fusion) | copy-start | bytes 3076
  69.9 8.0 %collective-permute-start.3 = (bf16[32,2048]{1,0:T(8,128)(2,1)}, bf16[32,2048]{1,0:T(8,128)(2,1)S(1)}, u32[]{:S(2)}, u32[]{:S(2)}) collective-permute-start(bf16[32,2048]{1,0:T(8,128)(2,1)} %get-tuple-element.4), channel_id=1, source_target_pairs={{0,24},{8,0},{16,8},{24,16},{1,25},{9,1},{17,9},{25,17},{2,26},{10... | collective-permute-start | bytes 393224 | tf_op jit(solution)/shard_map/ppermute | solution.py:238
  72.3 6.3 %collective-permute-start.4 = (bf16[32,2048]{1,0:T(8,128)(2,1)}, bf16[32,2048]{1,0:T(8,128)(2,1)S(1)}, u32[]{:S(2)}, u32[]{:S(2)}) collective-permute-start(bf16[32,2048]{1,0:T(8,128)(2,1)} %get-tuple-element.6), channel_id=1, source_target_pairs={{0,16},{8,24},{16,0},{24,8},{1,17},{9,25},{17,1},{25,9},{2,18},{10... | collective-permute-start | bytes 393224 | tf_op jit(solution)/shard_map/ppermute | solution.py:238
  72.9 9.5 %collective-permute-start.5 = (bf16[32,2048]{1,0:T(8,128)(2,1)}, bf16[32,2048]{1,0:T(8,128)(2,1)}, u32[]{:S(2)}, u32[]{:S(2)}) collective-permute-start(bf16[32,2048]{1,0:T(8,128)(2,1)} %get-tuple-element.5), channel_id=1, source_target_pairs={{0,8},{8,16},{16,24},{24,0},{1,9},{9,17},{17,25},{25,1},{2,10},{10... | collective-permute-start | bytes 393224 | tf_op jit(solution)/shard_map/ppermute | solution.py:238
  78.6 3.8 %copy-start.2 = (bf16[32,2048]{1,0:T(8,128)(2,1)}, bf16[32,2048]{1,0:T(8,128)(2,1)S(1)}, u32[]{:S(2)}) copy-start(bf16[32,2048]{1,0:T(8,128)(2,1)S(1)} %collective-permute-done.4) | copy-start | bytes 393220
  141.2 7.5 %copy-start.5 = (f32[16,2,8]{0,2,1:T(8,128)S(1)}, f32[16,2,8]{0,2,1:T(8,128)}, u32[]{:S(2)}) copy-start(f32[16,2,8]{0,2,1:T(8,128)} %param.31) | copy-start | bytes 3076
  141.2 35.9 %all-to-all-start.1 = ((bf16[128,4,2048]{2,1,0:T(4,128)(2,1)}), bf16[128,4,2048]{2,1,0:T(4,128)(2,1)}, u32[]{:S(2)}, u32[]{:S(2)}) async-start(bf16[128,4,2048]{2,1,0:T(4,128)(2,1)} %copy.45), calls=%async_computation.1 | async-start | bytes 4194304 | tf_op jit(solution)/shard_map/all_to_all | solution.py:283
Sparse Core Ops, SparseCore 0:
  9.8 53.3 all-gather.1

commit v10 on v9

--- a/solution.py
+++ b/solution.py
@@ -228,14 +228,15 @@
     )
     rows = requests * steps
     width = o_weight.shape[1]
-    gathered = lax.all_gather(o_weight, ("x", "c"), axis=0, tiled=True)
-    lines = lax.axis_size("y")
-    line = lax.axis_index("y")
+    gathered = lax.all_gather(o_weight, ("xl", "c"), axis=0, tiled=True)
+    across = ("y", "xh")
+    lines = lax.axis_size(across)
+    line = lax.axis_index(across)
     block = query_width // lines
     flat = attended.reshape(rows, query_width)
 
     def shifted(value, shift):
-        return lax.ppermute(value, "y", [(j, (j + shift) % lines) for j in range(lines)])
+        return lax.ppermute(value, across, [(j, (j + shift) % lines) for j in range(lines)])
 
     pieces = [lax.dynamic_slice_in_dim(flat, line * block, block, 1)]
     for shift in range(1, lines):
@@ -248,7 +249,7 @@
     for shift in range(1, lines):
         sent = shifted(partials[shift].astype(jnp.bfloat16), lines - shift)
         projected = projected + sent.astype(jnp.float32)
-    members = lax.axis_size("y") * lax.axis_size("x") * lax.axis_size("c")
+    members = lax.axis_size(("y", "xh", "xl", "c"))
     mixed = residual.reshape(rows, width).astype(jnp.float32) + projected
     normed = (
         mixed * lax.rsqrt(jnp.mean(mixed * mixed, axis=1, keepdims=True) + EPS) * norm_gain
@@ -270,7 +271,7 @@
     outgoing = jnp.dot(placing, normed, preferred_element_type=jnp.float32).astype(jnp.bfloat16)
     arrived = lax.all_to_all(
         outgoing.reshape(experts_all, capacity, width),
-        ("dp", "y", "x", "c"),
+        ("dp", "y", "xh", "xl", "c"),
         split_axis=0,
         concat_axis=0,
         tiled=True,
@@ -282,7 +283,7 @@
     )
     returned = lax.all_to_all(
         answer.reshape(sources * experts_local, depth, width),
-        ("dp", "y", "x", "c"),
+        ("dp", "y", "xh", "xl", "c"),
         split_axis=0,
         concat_axis=0,
         tiled=True,
@@ -309,29 +310,29 @@
 def solution(mesh):
     lines = mesh.devices.shape[1] // 8
     mesh = jax.sharding.Mesh(
-        mesh.devices.reshape(mesh.devices.shape[0], lines, 4, 2), ("dp", "y", "x", "c")
+        mesh.devices.reshape(mesh.devices.shape[0], lines, 2, 2, 2), ("dp", "y", "xh", "xl", "c")
     )
     return jax.shard_map(
         shards,
         mesh=mesh,
         in_specs=(
-            P(("dp", "y", "x", "c"), None, None),
-            P(("dp", "y", "x", "c"), None, None),
-            P(("dp", "y", "x", "c"), None, None),
-            P(("dp", "y", "x", "c"), None, None),
-            P(("dp", "y", "x", "c"), None, None),
-            P(("dp", "y", "x", "c"), None, None),
-            P(("dp", "y", "x", "c"), None, None),
-            P(("dp", "y", "x", "c"), None),
-            P(("dp", "y", "x", "c")),
-            P(("dp", "y", "x", "c"), None, None),
-            P(("y", "x", "c"), None),
+            P(("dp", "y", "xh", "xl", "c"), None, None),
+            P(("dp", "y", "xh", "xl", "c"), None, None),
+            P(("dp", "y", "xh", "xl", "c"), None, None),
+            P(("dp", "y", "xh", "xl", "c"), None, None),
+            P(("dp", "y", "xh", "xl", "c"), None, None),
+            P(("dp", "y", "xh", "xl", "c"), None, None),
+            P(("dp", "y", "xh", "xl", "c"), None, None),
+            P(("dp", "y", "xh", "xl", "c"), None),
+            P(("dp", "y", "xh", "xl", "c")),
+            P(("dp", "y", "xh", "xl", "c"), None, None),
+            P(("y", "xh", "xl", "c"), None),
             P(),
-            P(("dp", "y", "x", "c"), None, None),
-            P(("dp", "y", "x", "c"), None, None),
-            P(("dp", "y", "x", "c"), None, None),
-            P(("dp", "y", "x", "c"), None, None),
+            P(("dp", "y", "xh", "xl", "c"), None, None),
+            P(("dp", "y", "xh", "xl", "c"), None, None),
+            P(("dp", "y", "xh", "xl", "c"), None, None),
+            P(("dp", "y", "xh", "xl", "c"), None, None),
         ),
-        out_specs=(P(("dp", "y", "x", "c"), None, None), P(("dp", "y", "x", "c"), None, None)),
+        out_specs=(P(("dp", "y", "xh", "xl", "c"), None, None), P(("dp", "y", "xh", "xl", "c"), None, None)),
         check_vma=False,
     )

time: 192 us -> 208 us (1.083)
  starting transfers between devices: 15 us -> 31.7 us
  waiting for transfers between devices: 46.4 us -> 29.9 us
  local copies, waits for them, and re-layouts: 25.6 us -> 36.2 us
  blocking collectives: 36.7 us -> 43 us
    ppermute x6 -> x14, starting transfers between devices: 9.39 us -> 26.1 us  [shifted(): lax.ppermute(value, across, [(j, (j + shift) % lines) for j in range(line...]
    all_gather x1, waiting for transfers between devices: 8.67 us -> 0.01 us  [shards(): gathered = lax.all_gather(o_weight, ('xl', 'c'), axis=0, tiled=True)]
    unnamed x24 -> x30, local copies, waits for them, and re-layouts: 3.35 us -> 11.3 us
    ppermute x6 -> x14, waiting for transfers between devices: 9.65 us -> 1.85 us  [shifted(): lax.ppermute(value, across, [(j, (j + shift) % lines) for j in range(line...]
    all_to_all x1, blocking collectives: 36.7 us -> 43 us  [shards(): lax.all_to_all(outgoing.reshape(experts_all, capacity, width), ('dp', 'y'...]
  transfers between devices with their start and end apart: 8 -> 16, of which waited for: 6 -> 2; matrix products, arithmetic and copies ran while one was open for 8% -> 12% of each run, Pallas kernels for 14% -> 13%
where the time goes in v10:
time: 208 us
  blocking collectives  43 us (21%)
  local copies, waits for them, and re-layouts  36.2 us (17%)
  starting transfers between devices  31.7 us (15%)
  waiting for transfers between devices  29.9 us (14%)
  Pallas kernels  27.2 us (13%)
  matrix products  21.5 us (10%)
  between operations  14.3 us (7%)
  other arithmetic  3.68 us (2%)
    all_to_all x1, blocking collectives, shards(): lax.all_to_all(outgoing.reshape(experts_all, capacity, width), ('dp', 'y'...  43 us
    all_to_all x1, waiting for transfers between devices, shards(): lax.all_to_all(answer.reshape(sources * experts_local, depth, width), ('d...  27.4 us
    pallas_call x1, Pallas kernels, decode_attention(): pl.pallas_call(kernel, out_shape=jax.ShapeDtypeStruct((requests, steps, h...  27.2 us
    ppermute x14, starting transfers between devices, shifted(): lax.ppermute(value, across, [(j, (j + shift) % lines) for j in range(line...  26.1 us
    unnamed x30, local copies, waits for them, and re-layouts  11.3 us
    dot_general x1, matrix products, run_experts(): jnp.einsum('sjcd,jdf->sjcf', arriving, expert_gate_up, preferred_element_...  9.14 us
    all_to_all x1, starting transfers between devices, shards(): lax.all_to_all(answer.reshape(sources * experts_local, depth, width), ('d...  5.56 us
    dot_general x1, matrix products, shards(): jnp.dot(jnp.concatenate(pieces, axis=0), gathered, preferred_element_type...  4.98 us
  transfers between devices with their start and end apart: 16, of which 2 were waited for; matrix products, arithmetic and copies ran while one was open for 12% of the time, Pallas kernels for 13%

profile of v10, /device:TPU:1, one launch (start us, length us, event | category | flops | bytes accessed | tf_op | source)
XLA Modules:
  0.0 207.5 jit_solution(11580747942563244115)
XLA Ops:
  7.2 0.0 copy-start
  7.2 0.0 all-gather.2.cloned.1.call-start
  7.3 0.7 all-gather.2.cloned.1.call-update
  8.0 2.3 %reshape.112.q_ref = bf16[16,2,64,128]{3,2,1,0:T(8,128)(2,1)} reshape(bf16[16,2,8192]{2,1,0:T(2,128)(2,1)} %param.16) | data formatting | bytes 1048576 | tf_op jit(solution)/shard_map/reshape | solution.py:179
  10.4 0.1 copy.38
  10.5 0.6 reshape.109.flag_ref
  11.1 0.1 copy.39
  11.2 0.7 reshape.110.share_ref
  11.9 0.1 copy.40
  12.0 0.7 reshape.111.weight_ref
  12.7 27.2 %shard_map.167 = bf16[16,2,64,128]{3,2,1,0:T(8,128)(2,1)} custom-call(s32[16]{0:T(128)} %len_ref.1, s32[128]{0:T(128)} %reshape.109.flag_ref, f32[128]{0:T(128)} %reshape.110.share_ref, f32[64]{0:T(128)} %reshape.111.weight_ref, bf16[16,2,64,128]{3,2,1,0:T(8,128)(2,1)} %reshape.112.q_ref, bf16[16,2,512]{2,1,0:T(2,128)(2,1)} %kn_ref.1, ...), custom_call_target="tpu_custom_call" | custom-call | tf_op jit(solution)/shard_map/pallas_call | solution.py:160
  39.8 2.2 %copy.50 = bf16[4,8,64,128]{3,1,2,0:T(8,128)(2,1)} copy(bf16[4,8,64,128]{3,2,1,0:T(8,128)(2,1)} %bitcast.35) | data formatting | bytes 1048576
  42.0 1.8 constant_dynamic-slice_fusion
  43.8 3.7 %collective-permute-start = (bf16[32,1024]{1,0:T(8,128)(2,1)}, bf16[32,1024]{1,0:T(8,128)(2,1)}, u32[]{:S(2)}, u32[]{:S(2)}) collective-permute-start(bf16[32,1024]{1,0:T(8,128)(2,1)} %get-tuple-element.17), channel_id=1, source_target_pairs={{0,4},{4,8},{8,12},{12,16},{16,20},{20,24},{24,28},{28,0},{1,5},{5... | collective-permute-start | bytes 196616 | tf_op jit(solution)/shard_map/ppermute | solution.py:239
  47.5 1.3 collective-permute-start.1
  48.8 1.9 collective-permute-start.2
  50.7 1.4 collective-permute-start.3
  52.1 5.0 %collective-permute-start.4 = (bf16[32,1024]{1,0:T(8,128)(2,1)S(1)}, bf16[32,1024]{1,0:T(8,128)(2,1)}, u32[]{:S(2)}, u32[]{:S(2)}) collective-permute-start(bf16[32,1024]{1,0:T(8,128)(2,1)S(1)} %get-tuple-element.13), channel_id=1, source_target_pairs={{0,20},{4,24},{8,28},{12,0},{16,4},{20,8},{24,12},{28,16},{1,21},{... | collective-permute-start | bytes 196616 | tf_op jit(solution)/shard_map/ppermute | solution.py:239
  57.1 0.8 copy.42
  57.9 0.7 eq.51
  58.5 0.0 collective-permute-done
  58.5 0.6 collective-permute-start.5
  59.1 1.5 constant_dynamic-update-slice_fusion.6
  60.6 0.0 collective-permute-done.1
  60.6 0.0 collective-permute-start.6
  60.6 1.5 constant_dynamic-update-slice_fusion.5
  62.1 0.0 collective-permute-done.2
  62.1 1.5 constant_dynamic-update-slice_fusion.4
  63.5 0.0 collective-permute-done.3
  63.5 1.5 constant_dynamic-update-slice_fusion.3
  65.0 0.0 collective-permute-done.4
  65.0 1.5 constant_dynamic-update-slice_fusion.2
  66.5 0.6 constant_dynamic-update-slice_fusion.1
  67.1 0.6 constant_dynamic-update-slice_fusion
  67.8 5.0 %fusion.29 = (bf16[256,2048]{1,0:T(8,128)(2,1)S(1)}, f32[256,2048]{1,0:T(8,128)}) fusion(bf16[256,1024]{1,0:T(8,128)(2,1)} %constant_dynamic-update-slice_fusion, bf16[1024,2048]{1,0:T(8,128)(2,1)} %all-gather.2.cloned.1.call-done), kind=kOutput, calls=%fused_computation.52 | convolution fusion | flops 1074266112 | bytes 7864320 | tf_op jit(solution)/shard_map/dot_general | solution.py:245
  72.7 0.8 fusion.28
  73.5 1.5 collective-permute-start.10
  75.0 2.1 %collective-permute-start.11 = (bf16[32,2048]{1,0:T(8,128)(2,1)S(1)}, bf16[32,2048]{1,0:T(8,128)(2,1)S(1)}, u32[]{:S(2)}, u32[]{:S(2)}) collective-permute-start(bf16[32,2048]{1,0:T(8,128)(2,1)S(1)} %get-tuple-element.7), channel_id=1, source_target_pairs={{0,12},{4,16},{8,20},{12,24},{16,28},{20,0},{24,4},{28,8},{1,13},{... | collective-permute-start | bytes 393224 | tf_op jit(solution)/shard_map/ppermute | solution.py:239
  77.1 1.8 collective-permute-start.12
  78.8 1.2 collective-permute-start.13
  80.0 3.9 %collective-permute-start.7 = (bf16[32,2048]{1,0:T(8,128)(2,1)S(1)}, bf16[32,2048]{1,0:T(8,128)(2,1)}, u32[]{:S(2)}, u32[]{:S(2)}) collective-permute-start(bf16[32,2048]{1,0:T(8,128)(2,1)S(1)} %get-tuple-element.4), channel_id=1, source_target_pairs={{0,28},{4,0},{8,4},{12,8},{16,12},{20,16},{24,20},{28,24},{1,29},{... | collective-permute-start | bytes 393224 | tf_op jit(solution)/shard_map/ppermute | solution.py:239
  83.9 1.8 collective-permute-start.9
  85.8 0.2 convert_reduce_fusion
  85.9 1.7 reshape.120
  87.6 0.7 reduce_sum.30
  88.3 0.7 copy.41
  89.0 0.7 add.154
  89.7 0.2 fusion.15
  90.0 1.8 collective-permute-done.9
  91.8 1.7 multiply_reduce_fusion
  93.5 2.8 %convolution_convert_fusion = bf16[512,2048]{1,0:T(8,128)(2,1)} fusion(pred[512,32]{0,1:T(8,128)(4,1)S(1)} %fusion.15, f32[32,2048]{1,0:T(8,128)S(1)} %get-tuple-element.3, f32[2048]{0:T(1024)} %param.27, f32[32]{0:T(128)S(1)} %add_rsqrt_fusion), kind=kOutput, calls=%fused_computation.6 | convolution fusion | flops 68354048 | bytes 2384000 | tf_op jit(solution)/shard_map/dot_general | solution.py:271
  96.3 4.1 %reshape.114 = bf16[128,4,2048]{2,1,0:T(4,128)(2,1)} reshape(bf16[512,2048]{1,0:T(8,128)(2,1)} %convolution_convert_fusion) | data formatting | bytes 4194304 | tf_op jit(solution)/shard_map/reshape | solution.py:273
  100.4 43.0 %all_to_all.10 = bf16[128,4,2048]{2,1,0:T(4,128)(2,1)S(1)} all-to-all(bf16[128,4,2048]{2,1,0:T(4,128)(2,1)} %reshape.114), channel_id=1, replica_groups=mesh['dp'=4,'y'=4,'xh'=2,'xl'=2,'c'=2] {'dp','y','xh','xl','c'}, dimensions={0} | all-to-all | bytes 4194304 | tf_op jit(solution)/shard_map/all_to_all | solution.py:272
  143.4 9.1 %fusion.2 = f32[128,1,4,1536]{3,0,2,1:T(8,128)S(1)} fusion(bf16[1,2048,1536]{2,1,0:T(8,128)(2,1)} %param.28, bf16[128,4,2048]{2,1,0:T(4,128)(2,1)S(1)} %all_to_all.10), kind=kOutput, calls=%fused_computation.2 | convolution fusion | flops 3221225472 | bytes 11534336 | tf_op jit(solution)/shard_map/sjcd,jdf->sjcf/dot_general | solution.py:190
  152.6 1.8 fusion.7
  154.4 2.9 %copy.45 = bf16[128,4,2048]{2,1,0:T(4,128)(2,1)} copy(bf16[128,4,2048]{2,0,1:T(8,128)(2,1)S(1)} %fusion.7) | data formatting | bytes 4194304 | tf_op jit(solution)/shard_map/convert_element_type | solution.py:196
  157.3 5.6 %all-to-all-start.1 = ((bf16[128,4,2048]{2,1,0:T(4,128)(2,1)}), bf16[128,4,2048]{2,1,0:T(4,128)(2,1)}, u32[]{:S(2)}, u32[]{:S(2)}) async-start(bf16[128,4,2048]{2,1,0:T(4,128)(2,1)} %copy.45), calls=%async_computation.1 | async-start | bytes 4194304 | tf_op jit(solution)/shard_map/all_to_all | solution.py:284
  162.9 2.0 reshape.113
  164.9 0.1 copy.43
  164.9 0.9 select_reduce_fusion
  165.8 27.4 %all-to-all-done.1 = bf16[128,4,2048]{2,1,0:T(4,128)(2,1)} async-done(((bf16[128,4,2048]{2,1,0:T(4,128)(2,1)}), bf16[128,4,2048]{2,1,0:T(4,128)(2,1)}, u32[]{:S(2)}, u32[]{:S(2)}) %all-to-all-start.1) | async-done | bytes 2097184 | tf_op jit(solution)/shard_map/all_to_all | solution.py:284
  193.2 3.9 %reshape.118 = bf16[512,2048]{1,0:T(8,128)(2,1)} reshape(bf16[128,4,2048]{2,1,0:T(4,128)(2,1)} %all-to-all-done.1) | data formatting | bytes 4194304 | tf_op jit(solution)/shard_map/reshape | solution.py:302
  197.1 2.7 %fusion.10 = bf16[32,2048]{1,0:T(8,128)(2,1)S(1)} fusion(f32[32,2048]{1,0:T(8,128)S(1)} %get-tuple-element.3, f32[32,512]{1,0:T(8,128)} %select_reduce_fusion, bf16[512,2048]{1,0:T(8,128)(2,1)} %reshape.118), kind=kOutput, calls=%fused_computation.8 | convolution fusion | flops 402784256 | bytes 2555904 | tf_op jit(solution)/shard_map/dot_general | solution.py:300
  199.9 0.8 reshape.119
  (29 shorter events, 0.1 us)
Async XLA Ops:
  7.2 145.4 %copy-start = (bf16[1,768,2048]{2,1,0:T(8,128)(2,1)S(1)}, bf16[1,768,2048]{2,1,0:T(8,128)(2,1)}, u32[]{:S(2)}) copy-start(bf16[1,768,2048]{2,1,0:T(8,128)(2,1)} %param.29) | copy-start | bytes 9437188
  7.2 3.2 %copy-start.6 = (s32[16,2,4]{0,2,1:T(4,128)S(1)}, s32[16,2,4]{0,2,1:T(4,128)}, u32[]{:S(2)}) copy-start(s32[16,2,4]{0,2,1:T(4,128)} %param.20) | copy-start | bytes 1540
  7.2 3.9 %copy-start.7 = (f32[16,2,4]{0,2,1:T(4,128)S(1)}, f32[16,2,4]{0,2,1:T(4,128)}, u32[]{:S(2)}) copy-start(f32[16,2,4]{0,2,1:T(4,128)} %param.19) | copy-start | bytes 1540
  7.2 4.7 %copy-start.8 = (f32[16,4]{0,1:T(4,128)S(1)}, f32[16,4]{0,1:T(4,128)}, u32[]{:S(2)}) copy-start(f32[16,4]{0,1:T(4,128)} %param.23) | copy-start | bytes 772
  7.2 60.5 %all-gather.2.cloned.1.call-start = ((), (), s32[]{:S(2)}) async-start(), calls=%async_computation.2 | async-start | bytes 5242880 | tf_op jit(solution)/shard_map/all_gather | solution.py:231
  43.8 14.7 %collective-permute-start = (bf16[32,1024]{1,0:T(8,128)(2,1)}, bf16[32,1024]{1,0:T(8,128)(2,1)}, u32[]{:S(2)}, u32[]{:S(2)}) collective-permute-start(bf16[32,1024]{1,0:T(8,128)(2,1)} %get-tuple-element.17), channel_id=1, source_target_pairs={{0,4},{4,8},{8,12},{12,16},{16,20},{20,24},{24,28},{28,0},{1,5},{5... | collective-permute-start | bytes 196616 | tf_op jit(solution)/shard_map/ppermute | solution.py:239
  47.5 13.1 %collective-permute-start.1 = (bf16[32,1024]{1,0:T(8,128)(2,1)S(1)}, bf16[32,1024]{1,0:T(8,128)(2,1)}, u32[]{:S(2)}, u32[]{:S(2)}) collective-permute-start(bf16[32,1024]{1,0:T(8,128)(2,1)S(1)} %get-tuple-element.16), channel_id=1, source_target_pairs={{0,8},{4,12},{8,16},{12,20},{16,24},{20,28},{24,0},{28,4},{1,9},{5... | collective-permute-start | bytes 196616 | tf_op jit(solution)/shard_map/ppermute | solution.py:239
  48.8 13.3 %collective-permute-start.2 = (bf16[32,1024]{1,0:T(8,128)(2,1)S(1)}, bf16[32,1024]{1,0:T(8,128)(2,1)}, u32[]{:S(2)}, u32[]{:S(2)}) collective-permute-start(bf16[32,1024]{1,0:T(8,128)(2,1)S(1)} %get-tuple-element.15), channel_id=1, source_target_pairs={{0,12},{4,16},{8,20},{12,24},{16,28},{20,0},{24,4},{28,8},{1,13},{... | collective-permute-start | bytes 196616 | tf_op jit(solution)/shard_map/ppermute | solution.py:239
  50.7 12.8 %collective-permute-start.3 = (bf16[32,1024]{1,0:T(8,128)(2,1)S(1)}, bf16[32,1024]{1,0:T(8,128)(2,1)}, u32[]{:S(2)}, u32[]{:S(2)}) collective-permute-start(bf16[32,1024]{1,0:T(8,128)(2,1)S(1)} %get-tuple-element.14), channel_id=1, source_target_pairs={{0,16},{4,20},{8,24},{12,28},{16,0},{20,4},{24,8},{28,12},{1,17},{... | collective-permute-start | bytes 196616 | tf_op jit(solution)/shard_map/ppermute | solution.py:239
  52.1 12.9 %collective-permute-start.4 = (bf16[32,1024]{1,0:T(8,128)(2,1)S(1)}, bf16[32,1024]{1,0:T(8,128)(2,1)}, u32[]{:S(2)}, u32[]{:S(2)}) collective-permute-start(bf16[32,1024]{1,0:T(8,128)(2,1)S(1)} %get-tuple-element.13), channel_id=1, source_target_pairs={{0,20},{4,24},{8,28},{12,0},{16,4},{20,8},{24,12},{28,16},{1,21},{... | collective-permute-start | bytes 196616 | tf_op jit(solution)/shard_map/ppermute | solution.py:239
  58.5 8.0 %collective-permute-start.5 = (bf16[32,1024]{1,0:T(8,128)(2,1)S(1)}, bf16[32,1024]{1,0:T(8,128)(2,1)S(1)}, u32[]{:S(2)}, u32[]{:S(2)}) collective-permute-start(bf16[32,1024]{1,0:T(8,128)(2,1)S(1)} %get-tuple-element.12), channel_id=1, source_target_pairs={{0,24},{4,28},{8,0},{12,4},{16,8},{20,12},{24,16},{28,20},{1,25},{... | collective-permute-start | bytes 196616 | tf_op jit(solution)/shard_map/ppermute | solution.py:239
  60.6 6.5 %collective-permute-start.6 = (bf16[32,1024]{1,0:T(8,128)(2,1)S(1)}, bf16[32,1024]{1,0:T(8,128)(2,1)S(1)}, u32[]{:S(2)}, u32[]{:S(2)}) collective-permute-start(bf16[32,1024]{1,0:T(8,128)(2,1)S(1)} %get-tuple-element.11), channel_id=1, source_target_pairs={{0,28},{4,0},{8,4},{12,8},{16,12},{20,16},{24,20},{28,24},{1,29},{... | collective-permute-start | bytes 196616 | tf_op jit(solution)/shard_map/ppermute | solution.py:239
  67.8 9.3 %copy-start.3 = (s32[16,2,8]{0,2,1:T(8,128)S(1)}, s32[16,2,8]{0,2,1:T(8,128)}, u32[]{:S(2)}) copy-start(s32[16,2,8]{0,2,1:T(8,128)} %param.30) | copy-start | bytes 3076
  67.8 18.0 %copy-start.4 = (s32[256]{0:T(256)S(1)}, s32[256]{0:T(256)}, u32[]{:S(2)}) copy-start(s32[256]{0:T(256)} %eq.51) | copy-start | bytes 3076
  73.5 10.4 %collective-permute-start.10 = (bf16[32,2048]{1,0:T(8,128)(2,1)S(1)}, bf16[32,2048]{1,0:T(8,128)(2,1)S(1)}, u32[]{:S(2)}, u32[]{:S(2)}) collective-permute-start(bf16[32,2048]{1,0:T(8,128)(2,1)S(1)} %get-tuple-element.8), channel_id=1, source_target_pairs={{0,16},{4,20},{8,24},{12,28},{16,0},{20,4},{24,8},{28,12},{1,17},{... | collective-permute-start | bytes 393224 | tf_op jit(solution)/shard_map/ppermute | solution.py:239
  75.0 8.9 %collective-permute-start.11 = (bf16[32,2048]{1,0:T(8,128)(2,1)S(1)}, bf16[32,2048]{1,0:T(8,128)(2,1)S(1)}, u32[]{:S(2)}, u32[]{:S(2)}) collective-permute-start(bf16[32,2048]{1,0:T(8,128)(2,1)S(1)} %get-tuple-element.7), channel_id=1, source_target_pairs={{0,12},{4,16},{8,20},{12,24},{16,28},{20,0},{24,4},{28,8},{1,13},{... | collective-permute-start | bytes 393224 | tf_op jit(solution)/shard_map/ppermute | solution.py:239
  77.1 12.9 %collective-permute-start.12 = (bf16[32,2048]{1,0:T(8,128)(2,1)}, bf16[32,2048]{1,0:T(8,128)(2,1)}, u32[]{:S(2)}, u32[]{:S(2)}) collective-permute-start(bf16[32,2048]{1,0:T(8,128)(2,1)} %get-tuple-element.6), channel_id=1, source_target_pairs={{0,8},{4,12},{8,16},{12,20},{16,24},{20,28},{24,0},{28,4},{1,9},{5... | collective-permute-start | bytes 393224 | tf_op jit(solution)/shard_map/ppermute | solution.py:239
  78.8 11.1 %collective-permute-start.13 = (bf16[32,2048]{1,0:T(8,128)(2,1)}, bf16[32,2048]{1,0:T(8,128)(2,1)}, u32[]{:S(2)}, u32[]{:S(2)}) collective-permute-start(bf16[32,2048]{1,0:T(8,128)(2,1)} %get-tuple-element.5), channel_id=1, source_target_pairs={{0,4},{4,8},{8,12},{12,16},{16,20},{20,24},{24,28},{28,0},{1,5},{5... | collective-permute-start | bytes 393224 | tf_op jit(solution)/shard_map/ppermute | solution.py:239
  80.0 9.9 %collective-permute-start.7 = (bf16[32,2048]{1,0:T(8,128)(2,1)S(1)}, bf16[32,2048]{1,0:T(8,128)(2,1)}, u32[]{:S(2)}, u32[]{:S(2)}) collective-permute-start(bf16[32,2048]{1,0:T(8,128)(2,1)S(1)} %get-tuple-element.4), channel_id=1, source_target_pairs={{0,28},{4,0},{8,4},{12,8},{16,12},{20,16},{24,20},{28,24},{1,29},{... | collective-permute-start | bytes 393224 | tf_op jit(solution)/shard_map/ppermute | solution.py:239
  83.9 1.8 copy-start.1
  83.9 6.0 %collective-permute-start.8 = (bf16[32,2048]{1,0:T(8,128)(2,1)S(1)}, bf16[32,2048]{1,0:T(8,128)(2,1)}, u32[]{:S(2)}, u32[]{:S(2)}) collective-permute-start(bf16[32,2048]{1,0:T(8,128)(2,1)S(1)} %get-tuple-element.10), channel_id=1, source_target_pairs={{0,24},{4,28},{8,0},{12,4},{16,8},{20,12},{24,16},{28,20},{1,25},{... | collective-permute-start | bytes 393224 | tf_op jit(solution)/shard_map/ppermute | solution.py:239
  83.9 1.8 copy-start.2
  83.9 7.8 %collective-permute-start.9 = (bf16[32,2048]{1,0:T(8,128)(2,1)S(1)}, bf16[32,2048]{1,0:T(8,128)(2,1)}, u32[]{:S(2)}, u32[]{:S(2)}) collective-permute-start(bf16[32,2048]{1,0:T(8,128)(2,1)S(1)} %get-tuple-element.9), channel_id=1, source_target_pairs={{0,20},{4,24},{8,28},{12,0},{16,4},{20,8},{24,12},{28,16},{1,21},{... | collective-permute-start | bytes 393224 | tf_op jit(solution)/shard_map/ppermute | solution.py:239
  157.3 7.5 %copy-start.5 = (f32[16,2,8]{0,2,1:T(8,128)S(1)}, f32[16,2,8]{0,2,1:T(8,128)}, u32[]{:S(2)}) copy-start(f32[16,2,8]{0,2,1:T(8,128)} %param.31) | copy-start | bytes 3076
  157.3 35.9 %all-to-all-start.1 = ((bf16[128,4,2048]{2,1,0:T(4,128)(2,1)}), bf16[128,4,2048]{2,1,0:T(4,128)(2,1)}, u32[]{:S(2)}, u32[]{:S(2)}) async-start(bf16[128,4,2048]{2,1,0:T(4,128)(2,1)} %copy.45), calls=%async_computation.1 | async-start | bytes 4194304 | tf_op jit(solution)/shard_map/all_to_all | solution.py:284
Sparse Core Ops, SparseCore 0:
  9.7 55.1 all-gather.1

commit v11 on v9

--- a/solution.py
+++ b/solution.py
@@ -265,11 +265,13 @@
     target = chosen * capacity + rank
     placing = (
         jnp.arange(experts_all * capacity, dtype=jnp.int32)[:, None] == target[None, :]
-    ).reshape(experts_all * capacity, rows, top_k)
-    placing = jnp.any(placing, axis=2).astype(jnp.bfloat16)
-    outgoing = jnp.dot(placing, normed, preferred_element_type=jnp.float32).astype(jnp.bfloat16)
+    ).reshape(experts_all, capacity, rows, top_k)
+    placing = jnp.any(placing, axis=3).astype(jnp.bfloat16)
+    outgoing = jnp.einsum(
+        "ecr,rd->ecd", placing, normed, preferred_element_type=jnp.float32
+    ).astype(jnp.bfloat16)
     arrived = lax.all_to_all(
-        outgoing.reshape(experts_all, capacity, width),
+        outgoing,
         ("dp", "y", "x", "c"),
         split_axis=0,
         concat_axis=0,
@@ -295,10 +297,11 @@
             0.0,
         ),
         axis=1,
-    )
-    blended = jnp.dot(
+    ).reshape(rows, experts_all, capacity)
+    blended = jnp.einsum(
+        "tec,ecd->td",
         gathering,
-        returned.reshape(experts_all * capacity, width).astype(jnp.float32),
+        returned.astype(jnp.float32),
         precision=lax.Precision.HIGHEST,
         preferred_element_type=jnp.float32,
     )

time: 192 us -> 181 us (0.943)
  local copies, waits for them, and re-layouts: 25.6 us -> 19.8 us
  matrix products: 22.5 us -> 18.2 us
    reshape x2 -> x0, local copies, waits for them, and re-layouts: 8.07 us -> none  [the longest x1 4.11 us: shards(): outgoing.reshape(experts_all, capacity, width)]
    dot_general x1, matrix products: 9.14 us -> 4.81 us  [run_experts(): jnp.einsum('sjcd,jdf->sjcf', arriving, expert_gate_up, preferred_element_...]
  transfers between devices with their start and end apart: 8 -> 8, of which waited for: 6 -> 6; matrix products, arithmetic and copies ran while one was open for 8% -> 9% of each run, Pallas kernels for 14% -> 15%
where the time goes in v11:
time: 181 us
  waiting for transfers between devices  46.2 us (26%)
  blocking collectives  36.4 us (20%)
  Pallas kernels  27.2 us (15%)
  local copies, waits for them, and re-layouts  19.8 us (11%)
  matrix products  18.2 us (10%)
  starting transfers between devices  15.1 us (8%)
  between operations  14.2 us (8%)
  other arithmetic  3.55 us (2%)
    all_to_all x1, blocking collectives, shards(): lax.all_to_all(outgoing, ('dp', 'y', 'x', 'c'), split_axis=0, concat_axis...  36.4 us
    all_to_all x1, waiting for transfers between devices, shards(): lax.all_to_all(answer.reshape(sources * experts_local, depth, width), ('d...  27.2 us
    pallas_call x1, Pallas kernels, decode_attention(): pl.pallas_call(kernel, out_shape=jax.ShapeDtypeStruct((requests, steps, h...  27.2 us
    ppermute x6, waiting for transfers between devices, shifted(): lax.ppermute(value, 'y', [(j, (j + shift) % lines) for j in range(lines)])  9.56 us
    ppermute x6, starting transfers between devices, shifted(): lax.ppermute(value, 'y', [(j, (j + shift) % lines) for j in range(lines)])  9.5 us
    all_gather x1, waiting for transfers between devices, shards(): gathered = lax.all_gather(o_weight, ('x', 'c'), axis=0, tiled=True)  8.76 us
    dot_general x1, matrix products, shards(): jnp.dot(jnp.concatenate(pieces, axis=0), gathered, preferred_element_type...  5.95 us
    all_to_all x1, starting transfers between devices, shards(): lax.all_to_all(answer.reshape(sources * experts_local, depth, width), ('d...  5.56 us
  transfers between devices with their start and end apart: 8, of which 6 were waited for; matrix products, arithmetic and copies ran while one was open for 9% of the time, Pallas kernels for 15%

profile of v11, /device:TPU:1, one launch (start us, length us, event | category | flops | bytes accessed | tf_op | source)
XLA Modules:
  0.0 180.7 jit_solution(12879267181117847554)
XLA Ops:
  7.2 0.0 copy-start
  7.2 0.0 copy-start.7
  7.2 0.0 copy-start.8
  7.2 0.0 copy-start.9
  7.2 0.0 all-gather.2.cloned.1.call-start
  7.3 0.7 all-gather.2.cloned.1.call-update
  8.0 2.4 %reshape.107.q_ref = bf16[16,2,64,128]{3,2,1,0:T(8,128)(2,1)} reshape(bf16[16,2,8192]{2,1,0:T(2,128)(2,1)} %param.16) | data formatting | bytes 1048576 | tf_op jit(solution)/shard_map/reshape | solution.py:179
  10.4 0.0 copy-done.7
  10.4 0.1 copy.39
  10.5 0.6 reshape.104.flag_ref
  11.1 0.0 copy-done.8
  11.1 0.1 copy.40
  11.2 0.6 reshape.105.share_ref
  11.8 0.0 copy-done.9
  11.8 0.1 copy.41
  11.9 0.6 reshape.106.weight_ref
  12.5 27.2 %shard_map.167 = bf16[16,2,64,128]{3,2,1,0:T(8,128)(2,1)} custom-call(s32[16]{0:T(128)} %len_ref.1, s32[128]{0:T(128)} %reshape.104.flag_ref, f32[128]{0:T(128)} %reshape.105.share_ref, f32[64]{0:T(128)} %reshape.106.weight_ref, bf16[16,2,64,128]{3,2,1,0:T(8,128)(2,1)} %reshape.107.q_ref, bf16[16,2,512]{2,1,0:T(2,128)(2,1)} %kn_ref.1, ...), custom_call_target="tpu_custom_call" | custom-call | tf_op jit(solution)/shard_map/pallas_call | solution.py:160
  39.7 0.0 copy-start.3
  39.7 2.2 %copy.59 = bf16[4,8,64,128]{3,1,2,0:T(8,128)(2,1)} copy(bf16[4,8,64,128]{3,2,1,0:T(8,128)(2,1)} %bitcast.42) | data formatting | bytes 1048576
  41.9 1.8 constant_dynamic-slice_fusion.3
  43.7 2.2 %collective-permute-start = (bf16[32,2048]{1,0:T(8,128)(2,1)}, bf16[32,2048]{1,0:T(8,128)(2,1)}, u32[]{:S(2)}, u32[]{:S(2)}) collective-permute-start(bf16[32,2048]{1,0:T(8,128)(2,1)} %get-tuple-element.10), channel_id=1, source_target_pairs={{0,8},{8,16},{16,24},{24,0},{1,9},{9,17},{17,25},{25,1},{2,10},{10... | collective-permute-start | bytes 393224 | tf_op jit(solution)/shard_map/ppermute | solution.py:238
  45.9 2.5 %collective-permute-start.1 = (bf16[32,2048]{1,0:T(8,128)(2,1)S(1)}, bf16[32,2048]{1,0:T(8,128)(2,1)}, u32[]{:S(2)}, u32[]{:S(2)}) collective-permute-start(bf16[32,2048]{1,0:T(8,128)(2,1)S(1)} %get-tuple-element.9), channel_id=1, source_target_pairs={{0,16},{8,24},{16,0},{24,8},{1,17},{9,25},{17,1},{25,9},{2,18},{10... | collective-permute-start | bytes 393224 | tf_op jit(solution)/shard_map/ppermute | solution.py:238
  48.4 1.1 collective-permute-start.2
  49.5 0.6 broadcast_multiply_fusion
  50.1 0.8 copy.43
  50.9 0.7 eq.53
  51.6 0.9 convert_reduce_fusion
  52.5 0.0 collective-permute-done
  52.5 1.9 %collective-permute-done.1 = bf16[32,2048]{1,0:T(8,128)(2,1)} collective-permute-done((bf16[32,2048]{1,0:T(8,128)(2,1)S(1)}, bf16[32,2048]{1,0:T(8,128)(2,1)}, u32[]{:S(2)}, u32[]{:S(2)}) %collective-permute-start.1) | collective-permute-done | bytes 131104 | tf_op jit(solution)/shard_map/ppermute | solution.py:238
  54.4 0.0 collective-permute-done.2
  54.4 8.8 %all-gather.2.cloned.1.call-done = bf16[2048,2048]{1,0:T(8,128)(2,1)} async-done(((bf16[256,2048]{1,0:T(8,128)(2,1)}), bf16[2048,2048]{1,0:T(8,128)(2,1)}) %all-gather.2.cloned.1.call-update) | async-done | bytes 8388624 | tf_op jit(solution)/shard_map/all_gather | solution.py:231
  63.1 6.0 %fusion.38 = (bf16[128,2048]{1,0:T(8,128)(2,1)S(1)}, f32[128,2048]{1,0:T(8,128)}) fusion(bf16[2048,2048]{1,0:T(8,128)(2,1)} %all-gather.2.cloned.1.call-done, bf16[32,2048]{1,0:T(8,128)(2,1)} %collective-permute-done.2, bf16[32,2048]{1,0:T(8,128)(2,1)} %collective-permute-done.1, bf16[32,2048]{1,0:T(8,128)(2,1)} %collective-permute-done, ...), kind=kOutput, calls=%fused_computation.50 | convolution fusion | flops 1076101120 | bytes 10485760 | tf_op jit(solution)/shard_map/dot_general | solution.py:244
  69.1 0.7 fusion.37
  69.8 2.5 %collective-permute-start.3 = (bf16[32,2048]{1,0:T(8,128)(2,1)}, bf16[32,2048]{1,0:T(8,128)(2,1)S(1)}, u32[]{:S(2)}, u32[]{:S(2)}) collective-permute-start(bf16[32,2048]{1,0:T(8,128)(2,1)} %get-tuple-element.4), channel_id=1, source_target_pairs={{0,24},{8,0},{16,8},{24,16},{1,25},{9,1},{17,9},{25,17},{2,26},{10... | collective-permute-start | bytes 393224 | tf_op jit(solution)/shard_map/ppermute | solution.py:238
  72.3 0.5 collective-permute-start.4
  72.8 0.7 collective-permute-start.5
  73.5 0.0 copy-done.1
  73.5 0.7 reshape.114
  74.3 0.1 reduce_sum.30
  74.3 0.0 copy-done.4
  74.3 0.1 copy.42
  74.4 0.2 compare_reduce_fusion
  74.7 3.3 %collective-permute-done.3 = bf16[32,2048]{1,0:T(8,128)(2,1)S(1)} collective-permute-done((bf16[32,2048]{1,0:T(8,128)(2,1)}, bf16[32,2048]{1,0:T(8,128)(2,1)S(1)}, u32[]{:S(2)}, u32[]{:S(2)}) %collective-permute-start.3) | collective-permute-done | bytes 131104 | tf_op jit(solution)/shard_map/ppermute | solution.py:238
  78.0 0.7 collective-permute-done.4
  78.7 3.7 %collective-permute-done.5 = bf16[32,2048]{1,0:T(8,128)(2,1)} collective-permute-done((bf16[32,2048]{1,0:T(8,128)(2,1)}, bf16[32,2048]{1,0:T(8,128)(2,1)}, u32[]{:S(2)}, u32[]{:S(2)}) %collective-permute-start.5) | collective-permute-done | bytes 131104 | tf_op jit(solution)/shard_map/ppermute | solution.py:238
  82.4 0.0 copy-done.2
  82.4 1.5 multiply_reduce_fusion
  83.9 0.8 convolution_convert_fusion
  84.7 0.0 slice-start.1
  84.7 1.6 copy.46
  86.3 36.4 %all_to_all.10 = bf16[128,4,2048]{2,1,0:T(4,128)(2,1)S(1)} all-to-all(bf16[128,4,2048]{2,1,0:T(4,128)(2,1)S(1)} %copy.46), channel_id=1, replica_groups=mesh['dp'=4,'y'=4,'x'=4,'c'=2] {'dp','y','x','c'}, dimensions={0} | all-to-all | bytes 4194304 | tf_op jit(solution)/shard_map/all_to_all | solution.py:273
  122.7 0.0 slice-done
  122.8 4.8 %fusion.2 = f32[128,1,4,1536]{3,0,2,1:T(8,128)S(1)} fusion(bf16[1,2048,1536]{2,1,0:T(8,128)(2,1)S(1)} %bitcast.48, bf16[128,4,2048]{2,1,0:T(4,128)(2,1)S(1)} %all_to_all.10), kind=kOutput, calls=%fused_computation.2 | convolution fusion | flops 3221225472 | bytes 11534336 | tf_op jit(solution)/shard_map/sjcd,jdf->sjcf/dot_general | solution.py:190
  127.6 0.0 copy-done
  127.6 1.8 %fusion.7 = bf16[128,4,2048]{2,0,1:T(8,128)(2,1)S(1)} fusion(bf16[1,768,2048]{2,1,0:T(8,128)(2,1)S(1)} %copy-done, f32[128,1,4,1536]{3,0,2,1:T(8,128)S(1)} %fusion.2), kind=kOutput, calls=%fused_computation.5 | convolution fusion | flops 1614020608 | bytes 8388608 | tf_op jit(solution)/shard_map/sjcf,jfd->sjcd/dot_general | solution.py:194
  129.4 2.9 %copy.48 = bf16[128,4,2048]{2,1,0:T(4,128)(2,1)} copy(bf16[128,4,2048]{2,0,1:T(8,128)(2,1)S(1)} %fusion.7) | data formatting | bytes 4194304 | tf_op jit(solution)/shard_map/convert_element_type | solution.py:196
  132.4 5.6 %all-to-all-start.1 = ((bf16[128,4,2048]{2,1,0:T(4,128)(2,1)}), bf16[128,4,2048]{2,1,0:T(4,128)(2,1)}, u32[]{:S(2)}, u32[]{:S(2)}) async-start(bf16[128,4,2048]{2,1,0:T(4,128)(2,1)} %copy.48), calls=%async_computation.1 | async-start | bytes 4194304 | tf_op jit(solution)/shard_map/all_to_all | solution.py:285
  137.9 2.0 %reshape.108 = bf16[16,2,8192]{2,1,0:T(2,128)(2,1)} reshape(bf16[16,2,64,128]{3,2,1,0:T(8,128)(2,1)} %shard_map.167) | data formatting | bytes 1048576 | tf_op jit(solution)/shard_map/reshape | solution.py:185
  139.9 0.1 copy.44
  140.0 0.2 select_reduce_fusion
  140.2 0.8 copy.45
  141.0 27.2 %all-to-all-done.1 = bf16[128,4,2048]{2,1,0:T(4,128)(2,1)} async-done(((bf16[128,4,2048]{2,1,0:T(4,128)(2,1)}), bf16[128,4,2048]{2,1,0:T(4,128)(2,1)}, u32[]{:S(2)}, u32[]{:S(2)}) %all-to-all-start.1) | async-done | bytes 2097184 | tf_op jit(solution)/shard_map/all_to_all | solution.py:285
  168.2 4.8 %fusion.11 = bf16[32,2048]{1,0:T(8,128)(2,1)S(1)} fusion(f32[32,2048]{1,0:T(8,128)S(1)} %get-tuple-element.3, bf16[128,4,2048]{2,1,0:T(4,128)(2,1)} %all-to-all-done.1, f32[32,128,4]{0,2,1:T(4,128)} %bitcast.44), kind=kOutput, calls=%fused_computation.9 | convolution fusion | flops 402784256 | bytes 2555904 | tf_op jit(solution)/shard_map/tec,ecd->td/dot_general | solution.py:301
  173.1 0.8 reshape.113
  (14 shorter events, 0.0 us)
Async XLA Ops:
  7.2 120.4 %copy-start = (bf16[1,768,2048]{2,1,0:T(8,128)(2,1)S(1)}, bf16[1,768,2048]{2,1,0:T(8,128)(2,1)}, u32[]{:S(2)}) copy-start(bf16[1,768,2048]{2,1,0:T(8,128)(2,1)} %param.29) | copy-start | bytes 9437188
  7.2 3.2 %copy-start.7 = (s32[16,2,4]{0,2,1:T(4,128)S(1)}, s32[16,2,4]{0,2,1:T(4,128)}, u32[]{:S(2)}) copy-start(s32[16,2,4]{0,2,1:T(4,128)} %param.20) | copy-start | bytes 1540
  7.2 3.9 %copy-start.8 = (f32[16,2,4]{0,2,1:T(4,128)S(1)}, f32[16,2,4]{0,2,1:T(4,128)}, u32[]{:S(2)}) copy-start(f32[16,2,4]{0,2,1:T(4,128)} %param.19) | copy-start | bytes 1540
  7.2 4.6 %copy-start.9 = (f32[16,4]{0,1:T(4,128)S(1)}, f32[16,4]{0,1:T(4,128)}, u32[]{:S(2)}) copy-start(f32[16,4]{0,1:T(4,128)} %param.23) | copy-start | bytes 772
  7.2 55.9 %all-gather.2.cloned.1.call-start = ((), (), s32[]{:S(2)}) async-start(), calls=%async_computation.2 | async-start | bytes 9437184 | tf_op jit(solution)/shard_map/all_gather | solution.py:231
  39.7 9.9 %copy-start.3 = (s32[16,2,8]{0,2,1:T(8,128)S(1)}, s32[16,2,8]{0,2,1:T(8,128)}, u32[]{:S(2)}) copy-start(s32[16,2,8]{0,2,1:T(8,128)} %param.30) | copy-start | bytes 3076
  43.7 8.8 %collective-permute-start = (bf16[32,2048]{1,0:T(8,128)(2,1)}, bf16[32,2048]{1,0:T(8,128)(2,1)}, u32[]{:S(2)}, u32[]{:S(2)}) collective-permute-start(bf16[32,2048]{1,0:T(8,128)(2,1)} %get-tuple-element.10), channel_id=1, source_target_pairs={{0,8},{8,16},{16,24},{24,0},{1,9},{9,17},{17,25},{25,1},{2,10},{10... | collective-permute-start | bytes 393224 | tf_op jit(solution)/shard_map/ppermute | solution.py:238
  45.9 8.5 %collective-permute-start.1 = (bf16[32,2048]{1,0:T(8,128)(2,1)S(1)}, bf16[32,2048]{1,0:T(8,128)(2,1)}, u32[]{:S(2)}, u32[]{:S(2)}) collective-permute-start(bf16[32,2048]{1,0:T(8,128)(2,1)S(1)} %get-tuple-element.9), channel_id=1, source_target_pairs={{0,16},{8,24},{16,0},{24,8},{1,17},{9,25},{17,1},{25,9},{2,18},{10... | collective-permute-start | bytes 393224 | tf_op jit(solution)/shard_map/ppermute | solution.py:238
  48.4 6.0 %collective-permute-start.2 = (bf16[32,2048]{1,0:T(8,128)(2,1)S(1)}, bf16[32,2048]{1,0:T(8,128)(2,1)}, u32[]{:S(2)}, u32[]{:S(2)}) collective-permute-start(bf16[32,2048]{1,0:T(8,128)(2,1)S(1)} %get-tuple-element.8), channel_id=1, source_target_pairs={{0,24},{8,0},{16,8},{24,16},{1,25},{9,1},{17,9},{25,17},{2,26},{10... | collective-permute-start | bytes 393224 | tf_op jit(solution)/shard_map/ppermute | solution.py:238
  63.1 10.4 %copy-start.1 = (bf16[16,2,2048]{2,1,0:T(2,128)(2,1)S(1)}, bf16[16,2,2048]{2,1,0:T(2,128)(2,1)}, u32[]{:S(2)}) copy-start(bf16[16,2,2048]{2,1,0:T(2,128)(2,1)} %param.25) | copy-start | bytes 393220
  63.1 11.2 %copy-start.4 = (s32[16,2,8]{0,2,1:T(8,128)S(1)}, s32[16,2,8]{0,2,1:T(8,128)}, u32[]{:S(2)}) copy-start(s32[16,2,8]{0,2,1:T(8,128)} %broadcast_multiply_fusion) | copy-start | bytes 3076
  69.1 14.8 %copy-start.5 = (f32[2048]{0:T(1024)S(1)}, f32[2048]{0:T(1024)}, u32[]{:S(2)}) copy-start(f32[2048]{0:T(1024)} %param.27) | copy-start | bytes 24580
  69.8 8.1 %collective-permute-start.3 = (bf16[32,2048]{1,0:T(8,128)(2,1)}, bf16[32,2048]{1,0:T(8,128)(2,1)S(1)}, u32[]{:S(2)}, u32[]{:S(2)}) collective-permute-start(bf16[32,2048]{1,0:T(8,128)(2,1)} %get-tuple-element.4), channel_id=1, source_target_pairs={{0,24},{8,0},{16,8},{24,16},{1,25},{9,1},{17,9},{25,17},{2,26},{10... | collective-permute-start | bytes 393224 | tf_op jit(solution)/shard_map/ppermute | solution.py:238
  72.3 6.4 %collective-permute-start.4 = (bf16[32,2048]{1,0:T(8,128)(2,1)}, bf16[32,2048]{1,0:T(8,128)(2,1)}, u32[]{:S(2)}, u32[]{:S(2)}) collective-permute-start(bf16[32,2048]{1,0:T(8,128)(2,1)} %get-tuple-element.6), channel_id=1, source_target_pairs={{0,16},{8,24},{16,0},{24,8},{1,17},{9,25},{17,1},{25,9},{2,18},{10... | collective-permute-start | bytes 393224 | tf_op jit(solution)/shard_map/ppermute | solution.py:238
  72.8 9.6 %collective-permute-start.5 = (bf16[32,2048]{1,0:T(8,128)(2,1)}, bf16[32,2048]{1,0:T(8,128)(2,1)}, u32[]{:S(2)}, u32[]{:S(2)}) collective-permute-start(bf16[32,2048]{1,0:T(8,128)(2,1)} %get-tuple-element.5), channel_id=1, source_target_pairs={{0,8},{8,16},{16,24},{24,0},{1,9},{9,17},{17,25},{25,1},{2,10},{10... | collective-permute-start | bytes 393224 | tf_op jit(solution)/shard_map/ppermute | solution.py:238
  78.0 4.4 %copy-start.2 = (bf16[32,2048]{1,0:T(8,128)(2,1)}, bf16[32,2048]{1,0:T(8,128)(2,1)S(1)}, u32[]{:S(2)}) copy-start(bf16[32,2048]{1,0:T(8,128)(2,1)S(1)} %collective-permute-done.3) | copy-start | bytes 393220
  82.4 40.4 %slice-start = ((s8[6291456]{0:T(1024)(128)(4,1)}), s8[4194304]{0:T(1024)(128)(4,1)S(1)}, s32[]{:S(2)}) async-start(s8[6291456]{0:T(1024)(128)(4,1)} %bitcast.47), calls=%async_computation.3 | async-start | bytes 8388608
  84.7 38.0 %slice-start.1 = ((s8[6291456]{0:T(1024)(128)(4,1)}), s8[2097152]{0:T(1024)(128)(4,1)S(1)}, s32[]{:S(2)}) async-start(s8[6291456]{0:T(1024)(128)(4,1)} %bitcast.47), calls=%async_computation.4 | async-start | bytes 4194304
  132.4 7.5 %copy-start.6 = (f32[16,2,8]{0,2,1:T(8,128)S(1)}, f32[16,2,8]{0,2,1:T(8,128)}, u32[]{:S(2)}) copy-start(f32[16,2,8]{0,2,1:T(8,128)} %param.31) | copy-start | bytes 3076
  132.4 35.9 %all-to-all-start.1 = ((bf16[128,4,2048]{2,1,0:T(4,128)(2,1)}), bf16[128,4,2048]{2,1,0:T(4,128)(2,1)}, u32[]{:S(2)}, u32[]{:S(2)}) async-start(bf16[128,4,2048]{2,1,0:T(4,128)(2,1)} %copy.48), calls=%async_computation.1 | async-start | bytes 4194304 | tf_op jit(solution)/shard_map/all_to_all | solution.py:285
Sparse Core Ops, SparseCore 0:
  9.8 53.3 all-gather.1

commit v12 on v11

--- a/solution.py
+++ b/solution.py
@@ -228,11 +228,22 @@
     )
     rows = requests * steps
     width = o_weight.shape[1]
-    gathered = lax.all_gather(o_weight, ("x", "c"), axis=0, tiled=True)
+    cols, cores = lax.axis_size("x"), lax.axis_size("c")
+    col, core = lax.axis_index("x"), lax.axis_index("c")
+    part = o_weight.shape[0]
+
+    def along(value, axis, size, shift):
+        return lax.ppermute(value, axis, [(j, (j + shift) % size) for j in range(size)])
+
+    near = jnp.concatenate(
+        [o_weight] + [along(o_weight, "x", cols, shift) for shift in range(1, cols)], axis=0
+    )
+    near, ready = lax.optimization_barrier((near, attended))
+    far = along(near, "c", cores, 1)
     lines = lax.axis_size("y")
     line = lax.axis_index("y")
     block = query_width // lines
-    flat = attended.reshape(rows, query_width)
+    flat = ready.reshape(rows, query_width)
 
     def shifted(value, shift):
         return lax.ppermute(value, "y", [(j, (j + shift) % lines) for j in range(lines)])
@@ -241,8 +252,22 @@
     for shift in range(1, lines):
         piece = lax.dynamic_slice_in_dim(flat, ((line + shift) % lines) * block, block, 1)
         pieces.append(shifted(piece, shift))
-    partials = jnp.dot(
-        jnp.concatenate(pieces, axis=0), gathered, preferred_element_type=jnp.float32
+    stacked = jnp.concatenate(pieces, axis=0)
+
+    def columns(owner):
+        return jnp.concatenate(
+            [
+                lax.dynamic_slice_in_dim(
+                    stacked, (((col - j) % cols) * cores + owner) * part, part, 1
+                )
+                for j in range(cols)
+            ],
+            axis=1,
+        )
+
+    partials = (
+        jnp.dot(columns(core), near, preferred_element_type=jnp.float32)
+        + jnp.dot(columns((core + cores - 1) % cores), far, preferred_element_type=jnp.float32)
     ).reshape(lines, rows, width)
     projected = partials[0]
     for shift in range(1, lines):

time: 181 us -> 185 us (1.022)
  between operations: 14.2 us -> 0.83 us
  starting transfers between devices: 15.1 us -> 20.4 us
  other arithmetic: 3.55 us -> 8.28 us
  blocking collectives: 36.4 us -> 38.4 us
  local copies, waits for them, and re-layouts: 19.8 us -> 21.7 us
    all_gather x1 -> x0, waiting for transfers between devices: 8.76 us -> none  [shards(): gathered = lax.all_gather(o_weight, ('x', 'c'), axis=0, tiled=True)]
    ppermute x0 -> x4, waiting for transfers between devices: none -> 8.63 us  [along(): lax.ppermute(value, axis, [(j, (j + shift) % size) for j in range(size)])]
    ppermute x0 -> x4, starting transfers between devices: none -> 7.26 us  [along(): lax.ppermute(value, axis, [(j, (j + shift) % size) for j in range(size)])]
    concatenate x0 -> x2, other arithmetic: none -> 4.76 us  [the longest x1 3.69 us: shards(): jnp.concatenate([o_weight] + [along(o_weight, 'x', cols, shift) for shift...]
    reshape x0 -> x1, local copies, waits for them, and re-layouts: none -> 2.07 us  [shards(): flat = ready.reshape(rows, query_width)]
    all_to_all x1, blocking collectives: 36.4 us -> 38.4 us  [shards(): lax.all_to_all(outgoing, ('dp', 'y', 'x', 'c'), split_axis=0, concat_axis...]
    all_to_all x1, waiting for transfers between devices: 27.2 us -> 29.1 us  [shards(): lax.all_to_all(answer.reshape(sources * experts_local, depth, width), ('d...]
    ppermute x6, starting transfers between devices: 9.5 us -> 7.6 us  [shifted(): lax.ppermute(value, 'y', [(j, (j + shift) % lines) for j in range(lines)])]
  transfers between devices with their start and end apart: 8 -> 11, of which waited for: 6 -> 6; matrix products, arithmetic and copies ran while one was open for 9% -> 10% of each run, Pallas kernels for 15% -> 15%
where the time goes in v12:
time: 185 us; the launch traced here: 184 us
  waiting for transfers between devices  47.8 us (26%)
  blocking collectives  38.4 us (21%)
  Pallas kernels  27.2 us (15%)
  local copies, waits for them, and re-layouts  21.7 us (12%)
  starting transfers between devices  20.4 us (11%)
  matrix products  19.2 us (10%)
  other arithmetic  8.28 us (4%)
    all_to_all x1, blocking collectives, shards(): lax.all_to_all(outgoing, ('dp', 'y', 'x', 'c'), split_axis=0, concat_axis...  38.4 us
    all_to_all x1, waiting for transfers between devices, shards(): lax.all_to_all(answer.reshape(sources * experts_local, depth, width), ('d...  29.1 us
    pallas_call x1, Pallas kernels, decode_attention(): pl.pallas_call(kernel, out_shape=jax.ShapeDtypeStruct((requests, steps, h...  27.2 us
    ppermute x6, waiting for transfers between devices, shifted(): lax.ppermute(value, 'y', [(j, (j + shift) % lines) for j in range(lines)])  10 us
    ppermute x4, waiting for transfers between devices, along(): lax.ppermute(value, axis, [(j, (j + shift) % size) for j in range(size)])  8.63 us
    ppermute x6, starting transfers between devices, shifted(): lax.ppermute(value, 'y', [(j, (j + shift) % lines) for j in range(lines)])  7.6 us
    ppermute x4, starting transfers between devices, along(): lax.ppermute(value, axis, [(j, (j + shift) % size) for j in range(size)])  7.26 us
    all_to_all x1, starting transfers between devices, shards(): lax.all_to_all(answer.reshape(sources * experts_local, depth, width), ('d...  5.57 us
  transfers between devices with their start and end apart: 11, of which 6 were waited for; matrix products, arithmetic and copies ran while one was open for 10% of the time, Pallas kernels for 15%

profile of v12, /device:TPU:1, one launch (start us, length us, event | category | flops | bytes accessed | tf_op | source)
XLA Modules:
  0.0 183.8 jit_solution(7339712429426089408)
XLA Ops:
  0.6 0.0 copy-start
  0.6 2.1 %collective-permute-start = (bf16[256,2048]{1,0:T(8,128)(2,1)}, bf16[256,2048]{1,0:T(8,128)(2,1)}, u32[]{:S(2)}, u32[]{:S(2)}) collective-permute-start(bf16[256,2048]{1,0:T(8,128)(2,1)} %param.26), channel_id=1, source_target_pairs={{0,2},{2,4},{4,6},{6,0},{1,3},{3,5},{5,7},{7,1},{8,10},{10,12},{12... | collective-permute-start | bytes 3145736 | tf_op jit(solution)/shard_map/ppermute | solution.py:236
  2.8 2.5 %collective-permute-start.1 = (bf16[256,2048]{1,0:T(8,128)(2,1)}, bf16[256,2048]{1,0:T(8,128)(2,1)}, u32[]{:S(2)}, u32[]{:S(2)}) collective-permute-start(bf16[256,2048]{1,0:T(8,128)(2,1)} %param.26), channel_id=1, source_target_pairs={{0,4},{2,6},{4,0},{6,2},{1,5},{3,7},{5,1},{7,3},{8,12},{10,14},{12... | collective-permute-start | bytes 3145736 | tf_op jit(solution)/shard_map/ppermute | solution.py:236
  5.2 1.2 collective-permute-start.2
  6.4 2.2 %reshape.110.q_ref = bf16[16,2,64,128]{3,2,1,0:T(8,128)(2,1)} reshape(bf16[16,2,8192]{2,1,0:T(2,128)(2,1)} %param.16) | data formatting | bytes 1048576 | tf_op jit(solution)/shard_map/reshape | solution.py:179
  8.6 0.8 copy.39
  9.4 0.6 reshape.107.flag_ref
  10.0 0.8 copy.40
  10.8 0.6 reshape.108.share_ref
  11.4 0.8 copy.41
  12.1 0.6 reshape.109.weight_ref
  12.7 27.2 %shard_map.167 = bf16[16,2,64,128]{3,2,1,0:T(8,128)(2,1)} custom-call(s32[16]{0:T(128)} %len_ref.1, s32[128]{0:T(128)} %reshape.107.flag_ref, f32[128]{0:T(128)} %reshape.108.share_ref, f32[64]{0:T(128)} %reshape.109.weight_ref, bf16[16,2,64,128]{3,2,1,0:T(8,128)(2,1)} %reshape.110.q_ref, bf16[16,2,512]{2,1,0:T(2,128)(2,1)} %kn_ref.1, ...), custom_call_target="tpu_custom_call" | custom-call | tf_op jit(solution)/shard_map/pallas_call | solution.py:160
  40.0 2.0 %reshape.111 = bf16[16,2,8192]{2,1,0:T(2,128)(2,1)} reshape(bf16[16,2,64,128]{3,2,1,0:T(8,128)(2,1)} %shard_map.167) | data formatting | bytes 1048576 | tf_op jit(solution)/shard_map/reshape | solution.py:185
  41.9 0.0 collective-permute-done
  41.9 8.6 %collective-permute-done.1 = bf16[256,2048]{1,0:T(8,128)(2,1)} collective-permute-done((bf16[256,2048]{1,0:T(8,128)(2,1)}, bf16[256,2048]{1,0:T(8,128)(2,1)}, u32[]{:S(2)}, u32[]{:S(2)}) %collective-permute-start.1) | collective-permute-done | bytes 1048608 | tf_op jit(solution)/shard_map/ppermute | solution.py:236
  50.6 0.0 collective-permute-done.2
  50.6 3.7 %pad_maximum_fusion = bf16[1024,2048]{1,0:T(8,128)(2,1)} fusion(bf16[256,2048]{1,0:T(8,128)(2,1)} %collective-permute-done.2, bf16[256,2048]{1,0:T(8,128)(2,1)} %collective-permute-done.1, bf16[256,2048]{1,0:T(8,128)(2,1)} %collective-permute-done, bf16[256,2048]{1,0:T(8,128)(2,1)} %param.26), kind=kLoop, calls=%fused_computation.2 | loop fusion | flops 16777216 | bytes 8388608 | tf_op jit(solution)/shard_map/concatenate | solution.py:238
  54.2 1.5 collective-permute-start.6
  55.8 2.1 %reshape.112 = bf16[32,8192]{1,0:T(8,128)(2,1)} reshape(bf16[16,2,8192]{2,1,0:T(2,128)(2,1)} %reshape.111) | data formatting | bytes 1048576 | tf_op jit(solution)/shard_map/reshape | solution.py:246
  57.9 1.8 constant_dynamic-slice_fusion.11
  59.6 1.3 collective-permute-start.3
  60.9 2.6 %collective-permute-start.4 = (bf16[32,2048]{1,0:T(8,128)(2,1)S(1)}, bf16[32,2048]{1,0:T(8,128)(2,1)}, u32[]{:S(2)}, u32[]{:S(2)}) collective-permute-start(bf16[32,2048]{1,0:T(8,128)(2,1)S(1)} %get-tuple-element.21), channel_id=1, source_target_pairs={{0,16},{8,24},{16,0},{24,8},{1,17},{9,25},{17,1},{25,9},{2,18},{10... | collective-permute-start | bytes 393224 | tf_op jit(solution)/shard_map/ppermute | solution.py:249
  63.6 1.1 collective-permute-start.5
  64.6 0.0 copy-done.3
  64.6 0.6 broadcast_multiply_fusion
  65.2 0.8 copy.43
  66.0 0.7 eq.62
  66.7 0.9 convert_reduce_fusion
  67.6 0.0 collective-permute-done.3
  67.6 2.7 %collective-permute-done.4 = bf16[32,2048]{1,0:T(8,128)(2,1)} collective-permute-done((bf16[32,2048]{1,0:T(8,128)(2,1)S(1)}, bf16[32,2048]{1,0:T(8,128)(2,1)}, u32[]{:S(2)}, u32[]{:S(2)}) %collective-permute-start.4) | collective-permute-done | bytes 131104 | tf_op jit(solution)/shard_map/ppermute | solution.py:249
  70.3 0.0 collective-permute-done.5
  70.3 1.1 pad_maximum_fusion.1
  71.4 0.1 constant_dynamic-slice_fusion.7
  71.5 0.0 collective-permute-done.6
  71.5 2.9 %fusion.31 = f32[128,2048]{1,0:T(8,128)S(1)} fusion(bf16[1024,2048]{1,0:T(8,128)(2,1)} %collective-permute-done.6, bf16[128,256]{1,0:T(8,128)(2,1)S(1)} %get-tuple-element.12, bf16[128,256]{1,0:T(8,128)(2,1)S(1)} %get-tuple-element.13, bf16[128,256]{1,0:T(8,128)(2,1)S(1)} %get-tuple-element.14, bf16[128,256]{1,0:T(8,128)(2,1)S(1)} %get-tuple-element.15), kind=kOutput, calls=%fused_computation.33 | convolution fusion | flops 537919488 | bytes 5505024 | tf_op jit(solution)/shard_map/dot_general | solution.py:270
  74.4 0.0 copy-start.1
  74.5 0.0 copy-start.5
  74.5 4.0 %fusion.50 = (bf16[128,2048]{1,0:T(8,128)(2,1)S(1)}, f32[128,2048]{1,0:T(8,128)}) fusion(f32[128,2048]{1,0:T(8,128)S(1)} %fusion.31, bf16[1024,2048]{1,0:T(8,128)(2,1)} %pad_maximum_fusion, bf16[128,256]{1,0:T(8,128)(2,1)S(1)} %get-tuple-element.16, bf16[128,256]{1,0:T(8,128)(2,1)S(1)} %get-tuple-element.17, bf16[128,256]{1,0:T(8,128)(2,1)S(1)} %get-tuple-element.18, ...), kind=kOutput, calls=%fused_computation.69 | convolution fusion | flops 538443776 | bytes 7077888 | tf_op jit(solution)/shard_map/dot_general | solution.py:269
  78.5 0.8 fusion.49
  79.3 1.6 collective-permute-start.7
  80.8 0.4 collective-permute-start.8
  81.2 0.7 collective-permute-start.9
  81.9 0.7 reshape.118
  82.6 0.1 reduce_sum.30
  82.7 0.1 copy.42
  82.8 0.2 compare_reduce_fusion
  83.0 0.7 collective-permute-done.7
  83.7 2.9 %collective-permute-done.8 = bf16[32,2048]{1,0:T(8,128)(2,1)} collective-permute-done((bf16[32,2048]{1,0:T(8,128)(2,1)}, bf16[32,2048]{1,0:T(8,128)(2,1)}, u32[]{:S(2)}, u32[]{:S(2)}) %collective-permute-start.8) | collective-permute-done | bytes 131104 | tf_op jit(solution)/shard_map/ppermute | solution.py:249
  86.6 3.8 %collective-permute-done.9 = bf16[32,2048]{1,0:T(8,128)(2,1)} collective-permute-done((bf16[32,2048]{1,0:T(8,128)(2,1)}, bf16[32,2048]{1,0:T(8,128)(2,1)}, u32[]{:S(2)}, u32[]{:S(2)}) %collective-permute-start.9) | collective-permute-done | bytes 131104 | tf_op jit(solution)/shard_map/ppermute | solution.py:249
  90.3 1.5 multiply_reduce_fusion
  91.9 0.8 convolution_convert_fusion
  92.7 0.0 slice-start.1
  92.7 1.6 copy.46
  94.3 38.4 %all_to_all.10 = bf16[128,4,2048]{2,1,0:T(4,128)(2,1)S(1)} all-to-all(bf16[128,4,2048]{2,1,0:T(4,128)(2,1)S(1)} %copy.46), channel_id=1, replica_groups=mesh['dp'=4,'y'=4,'x'=4,'c'=2] {'dp','y','x','c'}, dimensions={0} | all-to-all | bytes 4194304 | tf_op jit(solution)/shard_map/all_to_all | solution.py:298
  132.8 4.8 %fusion.2 = f32[128,1,4,1536]{3,0,2,1:T(8,128)S(1)} fusion(bf16[1,2048,1536]{2,1,0:T(8,128)(2,1)S(1)} %bitcast.42, bf16[128,4,2048]{2,1,0:T(4,128)(2,1)S(1)} %all_to_all.10), kind=kOutput, calls=%fused_computation.3 | convolution fusion | flops 3221225472 | bytes 11534336 | tf_op jit(solution)/shard_map/sjcd,jdf->sjcf/dot_general | solution.py:190
  137.6 1.8 fusion.7
  139.4 3.0 %copy.48 = bf16[128,4,2048]{2,1,0:T(4,128)(2,1)} copy(bf16[128,4,2048]{2,0,1:T(8,128)(2,1)S(1)} %fusion.7) | data formatting | bytes 4194304 | tf_op jit(solution)/shard_map/convert_element_type | solution.py:196
  142.4 5.6 %all-to-all-start.1 = ((bf16[128,4,2048]{2,1,0:T(4,128)(2,1)}), bf16[128,4,2048]{2,1,0:T(4,128)(2,1)}, u32[]{:S(2)}, u32[]{:S(2)}) async-start(bf16[128,4,2048]{2,1,0:T(4,128)(2,1)} %copy.48), calls=%async_computation.1 | async-start | bytes 4194304 | tf_op jit(solution)/shard_map/all_to_all | solution.py:310
  148.0 0.1 copy.44
  148.0 0.2 select_reduce_fusion
  148.3 0.8 copy.45
  149.1 29.1 %all-to-all-done.1 = bf16[128,4,2048]{2,1,0:T(4,128)(2,1)} async-done(((bf16[128,4,2048]{2,1,0:T(4,128)(2,1)}), bf16[128,4,2048]{2,1,0:T(4,128)(2,1)}, u32[]{:S(2)}, u32[]{:S(2)}) %all-to-all-start.1) | async-done | bytes 2097184 | tf_op jit(solution)/shard_map/all_to_all | solution.py:310
  178.2 4.8 %fusion.11 = bf16[32,2048]{1,0:T(8,128)(2,1)S(1)} fusion(f32[32,2048]{1,0:T(8,128)S(1)} %get-tuple-element.7, bf16[128,4,2048]{2,1,0:T(4,128)(2,1)} %all-to-all-done.1, f32[32,128,4]{0,2,1:T(4,128)} %bitcast.38), kind=kOutput, calls=%fused_computation.10 | convolution fusion | flops 402784256 | bytes 2555904 | tf_op jit(solution)/shard_map/tec,ecd->td/dot_general | solution.py:326
  183.1 0.8 reshape.117
  (17 shorter events, 0.0 us)
Async XLA Ops:
  0.6 136.9 %copy-start = (bf16[1,768,2048]{2,1,0:T(8,128)(2,1)S(1)}, bf16[1,768,2048]{2,1,0:T(8,128)(2,1)}, u32[]{:S(2)}) copy-start(bf16[1,768,2048]{2,1,0:T(8,128)(2,1)} %param.29) | copy-start | bytes 9437188
  0.6 41.3 %collective-permute-start = (bf16[256,2048]{1,0:T(8,128)(2,1)}, bf16[256,2048]{1,0:T(8,128)(2,1)}, u32[]{:S(2)}, u32[]{:S(2)}) collective-permute-start(bf16[256,2048]{1,0:T(8,128)(2,1)} %param.26), channel_id=1, source_target_pairs={{0,2},{2,4},{4,6},{6,0},{1,3},{3,5},{5,7},{7,1},{8,10},{10,12},{12... | collective-permute-start | bytes 3145736 | tf_op jit(solution)/shard_map/ppermute | solution.py:236
  2.8 47.8 %collective-permute-start.1 = (bf16[256,2048]{1,0:T(8,128)(2,1)}, bf16[256,2048]{1,0:T(8,128)(2,1)}, u32[]{:S(2)}, u32[]{:S(2)}) collective-permute-start(bf16[256,2048]{1,0:T(8,128)(2,1)} %param.26), channel_id=1, source_target_pairs={{0,4},{2,6},{4,0},{6,2},{1,5},{3,7},{5,1},{7,3},{8,12},{10,14},{12... | collective-permute-start | bytes 3145736 | tf_op jit(solution)/shard_map/ppermute | solution.py:236
  5.2 45.4 %collective-permute-start.2 = (bf16[256,2048]{1,0:T(8,128)(2,1)}, bf16[256,2048]{1,0:T(8,128)(2,1)}, u32[]{:S(2)}, u32[]{:S(2)}) collective-permute-start(bf16[256,2048]{1,0:T(8,128)(2,1)} %param.26), channel_id=1, source_target_pairs={{0,6},{2,0},{4,2},{6,4},{1,7},{3,1},{5,3},{7,5},{8,14},{10,8},{12,... | collective-permute-start | bytes 3145736 | tf_op jit(solution)/shard_map/ppermute | solution.py:236
  41.9 22.7 %copy-start.3 = (s32[16,2,8]{0,2,1:T(8,128)S(1)}, s32[16,2,8]{0,2,1:T(8,128)}, u32[]{:S(2)}) copy-start(s32[16,2,8]{0,2,1:T(8,128)} %param.30) | copy-start | bytes 3076
  54.2 17.3 %collective-permute-start.6 = (bf16[1024,2048]{1,0:T(8,128)(2,1)}, bf16[1024,2048]{1,0:T(8,128)(2,1)}, u32[]{:S(2)}, u32[]{:S(2)}) collective-permute-start(bf16[1024,2048]{1,0:T(8,128)(2,1)} %pad_maximum_fusion), channel_id=1, source_target_pairs={{0,1},{1,0},{2,3},{3,2},{4,5},{5,4},{6,7},{7,6},{8,9},{9,8},{10,11... | collective-permute-start | bytes 12582920 | tf_op jit(solution)/shard_map/ppermute | solution.py:236
  59.6 7.9 %collective-permute-start.3 = (bf16[32,2048]{1,0:T(8,128)(2,1)}, bf16[32,2048]{1,0:T(8,128)(2,1)}, u32[]{:S(2)}, u32[]{:S(2)}) collective-permute-start(bf16[32,2048]{1,0:T(8,128)(2,1)} %get-tuple-element.22), channel_id=1, source_target_pairs={{0,8},{8,16},{16,24},{24,0},{1,9},{9,17},{17,25},{25,1},{2,10},{10... | collective-permute-start | bytes 393224 | tf_op jit(solution)/shard_map/ppermute | solution.py:249
  60.9 9.4 %collective-permute-start.4 = (bf16[32,2048]{1,0:T(8,128)(2,1)S(1)}, bf16[32,2048]{1,0:T(8,128)(2,1)}, u32[]{:S(2)}, u32[]{:S(2)}) collective-permute-start(bf16[32,2048]{1,0:T(8,128)(2,1)S(1)} %get-tuple-element.21), channel_id=1, source_target_pairs={{0,16},{8,24},{16,0},{24,8},{1,17},{9,25},{17,1},{25,9},{2,18},{10... | collective-permute-start | bytes 393224 | tf_op jit(solution)/shard_map/ppermute | solution.py:249
  63.6 6.8 %collective-permute-start.5 = (bf16[32,2048]{1,0:T(8,128)(2,1)S(1)}, bf16[32,2048]{1,0:T(8,128)(2,1)}, u32[]{:S(2)}, u32[]{:S(2)}) collective-permute-start(bf16[32,2048]{1,0:T(8,128)(2,1)S(1)} %get-tuple-element.20), channel_id=1, source_target_pairs={{0,24},{8,0},{16,8},{24,16},{1,25},{9,1},{17,9},{25,17},{2,26},{10... | collective-permute-start | bytes 393224 | tf_op jit(solution)/shard_map/ppermute | solution.py:249
  74.4 7.4 %copy-start.1 = (bf16[16,2,2048]{2,1,0:T(2,128)(2,1)S(1)}, bf16[16,2,2048]{2,1,0:T(2,128)(2,1)}, u32[]{:S(2)}) copy-start(bf16[16,2,2048]{2,1,0:T(2,128)(2,1)} %param.25) | copy-start | bytes 393220
  74.5 8.2 %copy-start.4 = (s32[16,2,8]{0,2,1:T(8,128)S(1)}, s32[16,2,8]{0,2,1:T(8,128)}, u32[]{:S(2)}) copy-start(s32[16,2,8]{0,2,1:T(8,128)} %broadcast_multiply_fusion) | copy-start | bytes 3076
  74.5 17.4 %copy-start.5 = (f32[2048]{0:T(1024)S(1)}, f32[2048]{0:T(1024)}, u32[]{:S(2)}) copy-start(f32[2048]{0:T(1024)} %param.27) | copy-start | bytes 24580
  79.3 4.5 %collective-permute-start.7 = (bf16[32,2048]{1,0:T(8,128)(2,1)}, bf16[32,2048]{1,0:T(8,128)(2,1)S(1)}, u32[]{:S(2)}, u32[]{:S(2)}) collective-permute-start(bf16[32,2048]{1,0:T(8,128)(2,1)} %get-tuple-element.8), channel_id=1, source_target_pairs={{0,24},{8,0},{16,8},{24,16},{1,25},{9,1},{17,9},{25,17},{2,26},{10... | collective-permute-start | bytes 393224 | tf_op jit(solution)/shard_map/ppermute | solution.py:249
  80.8 5.7 %collective-permute-start.8 = (bf16[32,2048]{1,0:T(8,128)(2,1)}, bf16[32,2048]{1,0:T(8,128)(2,1)}, u32[]{:S(2)}, u32[]{:S(2)}) collective-permute-start(bf16[32,2048]{1,0:T(8,128)(2,1)} %get-tuple-element.10), channel_id=1, source_target_pairs={{0,16},{8,24},{16,0},{24,8},{1,17},{9,25},{17,1},{25,9},{2,18},{10... | collective-permute-start | bytes 393224 | tf_op jit(solution)/shard_map/ppermute | solution.py:249
  81.2 9.1 %collective-permute-start.9 = (bf16[32,2048]{1,0:T(8,128)(2,1)}, bf16[32,2048]{1,0:T(8,128)(2,1)}, u32[]{:S(2)}, u32[]{:S(2)}) collective-permute-start(bf16[32,2048]{1,0:T(8,128)(2,1)} %get-tuple-element.9), channel_id=1, source_target_pairs={{0,8},{8,16},{16,24},{24,0},{1,9},{9,17},{17,25},{25,1},{2,10},{10... | collective-permute-start | bytes 393224 | tf_op jit(solution)/shard_map/ppermute | solution.py:249
  83.7 6.6 %copy-start.2 = (bf16[32,2048]{1,0:T(8,128)(2,1)}, bf16[32,2048]{1,0:T(8,128)(2,1)S(1)}, u32[]{:S(2)}) copy-start(bf16[32,2048]{1,0:T(8,128)(2,1)S(1)} %collective-permute-done.7) | copy-start | bytes 393220
  90.3 42.4 %slice-start = ((s8[6291456]{0:T(1024)(128)(4,1)}), s8[4194304]{0:T(1024)(128)(4,1)S(1)}, s32[]{:S(2)}) async-start(s8[6291456]{0:T(1024)(128)(4,1)} %bitcast.41), calls=%async_computation.2 | async-start | bytes 8388608
  92.7 40.1 %slice-start.1 = ((s8[6291456]{0:T(1024)(128)(4,1)}), s8[2097152]{0:T(1024)(128)(4,1)S(1)}, s32[]{:S(2)}) async-start(s8[6291456]{0:T(1024)(128)(4,1)} %bitcast.41), calls=%async_computation.3 | async-start | bytes 4194304
  142.4 5.6 %copy-start.6 = (f32[16,2,8]{0,2,1:T(8,128)S(1)}, f32[16,2,8]{0,2,1:T(8,128)}, u32[]{:S(2)}) copy-start(f32[16,2,8]{0,2,1:T(8,128)} %param.31) | copy-start | bytes 3076
  142.4 35.9 %all-to-all-start.1 = ((bf16[128,4,2048]{2,1,0:T(4,128)(2,1)}), bf16[128,4,2048]{2,1,0:T(4,128)(2,1)}, u32[]{:S(2)}, u32[]{:S(2)}) async-start(bf16[128,4,2048]{2,1,0:T(4,128)(2,1)} %copy.48), calls=%async_computation.1 | async-start | bytes 4194304 | tf_op jit(solution)/shard_map/all_to_all | solution.py:310

commit v13 on v12

--- a/solution.py
+++ b/solution.py
@@ -235,15 +235,11 @@
     def along(value, axis, size, shift):
         return lax.ppermute(value, axis, [(j, (j + shift) % size) for j in range(size)])
 
-    near = jnp.concatenate(
-        [o_weight] + [along(o_weight, "x", cols, shift) for shift in range(1, cols)], axis=0
-    )
-    near, ready = lax.optimization_barrier((near, attended))
-    far = along(near, "c", cores, 1)
+    fetched = [along(o_weight, "x", cols, shift) for shift in range(1, cols)]
     lines = lax.axis_size("y")
     line = lax.axis_index("y")
     block = query_width // lines
-    flat = ready.reshape(rows, query_width)
+    flat = attended.reshape(rows, query_width)
 
     def shifted(value, shift):
         return lax.ppermute(value, "y", [(j, (j + shift) % lines) for j in range(lines)])
@@ -252,6 +248,9 @@
     for shift in range(1, lines):
         piece = lax.dynamic_slice_in_dim(flat, ((line + shift) % lines) * block, block, 1)
         pieces.append(shifted(piece, shift))
+    fetched, pieces = lax.optimization_barrier((fetched, pieces))
+    near = jnp.concatenate([o_weight] + fetched, axis=0)
+    far = along(near, "c", cores, 1)
     stacked = jnp.concatenate(pieces, axis=0)
 
     def columns(owner):

time: 185 us -> 184 us (level)
  local copies, waits for them, and re-layouts: 21.7 us -> 31.5 us
  waiting for transfers between devices: 47.8 us -> 39.8 us
  other arithmetic: 8.28 us -> 3.65 us
  starting transfers between devices: 20.4 us -> 24 us
    unnamed x23 -> x28, local copies, waits for them, and re-layouts: 3.21 us -> 12.4 us
    ppermute x4, waiting for transfers between devices: 8.63 us -> 2.99 us  [along(): lax.ppermute(value, axis, [(j, (j + shift) % size) for j in range(size)])]
    concatenate x2 -> x0, other arithmetic: 4.76 us -> none  [the longest x1 3.69 us: shards(): jnp.concatenate([o_weight] + [along(o_weight, 'x', cols, shift) for shift...]
    concatenate x0 -> x2, local copies, waits for them, and re-layouts: none -> 3.25 us  [the longest x1 2.33 us: shards(): near = jnp.concatenate([o_weight] + fetched, axis=0)]
    ppermute x4, starting transfers between devices: 7.26 us -> 9.89 us  [along(): lax.ppermute(value, axis, [(j, (j + shift) % size) for j in range(size)])]
    reshape x1 -> x0, local copies, waits for them, and re-layouts: 2.07 us -> none  [shards(): flat = ready.reshape(rows, query_width)]
    all_to_all x1, waiting for transfers between devices: 29.1 us -> 27.2 us  [shards(): lax.all_to_all(answer.reshape(sources * experts_local, depth, width), ('d...]
  transfers between devices with their start and end apart: 11 -> 11, of which waited for: 6 -> 7; matrix products, arithmetic and copies ran while one was open for 10% -> 11% of each run, Pallas kernels for 15% -> 15%
where the time goes in v13:
time: 184 us; the launch traced here: 183 us
  waiting for transfers between devices  39.8 us (22%)
  blocking collectives  37 us (20%)
  local copies, waits for them, and re-layouts  31.5 us (17%)
  Pallas kernels  27.2 us (15%)
  starting transfers between devices  24 us (13%)
  matrix products  19.1 us (10%)
  other arithmetic  3.65 us (2%)
    all_to_all x1, blocking collectives, shards(): lax.all_to_all(outgoing, ('dp', 'y', 'x', 'c'), split_axis=0, concat_axis...  37 us
    pallas_call x1, Pallas kernels, decode_attention(): pl.pallas_call(kernel, out_shape=jax.ShapeDtypeStruct((requests, steps, h...  27.2 us
    all_to_all x1, waiting for transfers between devices, shards(): lax.all_to_all(answer.reshape(sources * experts_local, depth, width), ('d...  27.2 us
    unnamed x28, local copies, waits for them, and re-layouts  12.4 us
    ppermute x4, starting transfers between devices, along(): lax.ppermute(value, axis, [(j, (j + shift) % size) for j in range(size)])  9.89 us
    ppermute x6, waiting for transfers between devices, shifted(): lax.ppermute(value, 'y', [(j, (j + shift) % lines) for j in range(lines)])  9.62 us
    ppermute x6, starting transfers between devices, shifted(): lax.ppermute(value, 'y', [(j, (j + shift) % lines) for j in range(lines)])  8.57 us
    all_to_all x1, starting transfers between devices, shards(): lax.all_to_all(answer.reshape(sources * experts_local, depth, width), ('d...  5.56 us
  transfers between devices with their start and end apart: 11, of which 7 were waited for; matrix products, arithmetic and copies ran while one was open for 11% of the time, Pallas kernels for 15%

profile of v13, /device:TPU:1, one launch (start us, length us, event | category | flops | bytes accessed | tf_op | source)
XLA Modules:
  0.0 183.1 jit_solution(14977024350699910159)
XLA Ops:
  0.6 0.0 copy-start
  0.6 2.1 %collective-permute-start = (bf16[256,2048]{1,0:T(8,128)(2,1)}, bf16[256,2048]{1,0:T(8,128)(2,1)}, u32[]{:S(2)}, u32[]{:S(2)}) collective-permute-start(bf16[256,2048]{1,0:T(8,128)(2,1)} %param.26), channel_id=1, source_target_pairs={{0,2},{2,4},{4,6},{6,0},{1,3},{3,5},{5,7},{7,1},{8,10},{10,12},{12... | collective-permute-start | bytes 3145736 | tf_op jit(solution)/shard_map/ppermute | solution.py:236
  2.8 2.5 %collective-permute-start.1 = (bf16[256,2048]{1,0:T(8,128)(2,1)}, bf16[256,2048]{1,0:T(8,128)(2,1)}, u32[]{:S(2)}, u32[]{:S(2)}) collective-permute-start(bf16[256,2048]{1,0:T(8,128)(2,1)} %param.26), channel_id=1, source_target_pairs={{0,4},{2,6},{4,0},{6,2},{1,5},{3,7},{5,1},{7,3},{8,12},{10,14},{12... | collective-permute-start | bytes 3145736 | tf_op jit(solution)/shard_map/ppermute | solution.py:236
  5.2 1.2 collective-permute-start.2
  6.4 2.2 %reshape.107.q_ref = bf16[16,2,64,128]{3,2,1,0:T(8,128)(2,1)} reshape(bf16[16,2,8192]{2,1,0:T(2,128)(2,1)} %param.16) | data formatting | bytes 1048576 | tf_op jit(solution)/shard_map/reshape | solution.py:179
  8.6 0.8 copy.39
  9.4 0.6 reshape.104.flag_ref
  10.0 0.8 copy.40
  10.8 0.7 reshape.105.share_ref
  11.5 0.8 copy.41
  12.2 0.7 reshape.106.weight_ref
  12.9 27.2 %shard_map.167 = bf16[16,2,64,128]{3,2,1,0:T(8,128)(2,1)} custom-call(s32[16]{0:T(128)} %len_ref.1, s32[128]{0:T(128)} %reshape.104.flag_ref, f32[128]{0:T(128)} %reshape.105.share_ref, f32[64]{0:T(128)} %reshape.106.weight_ref, bf16[16,2,64,128]{3,2,1,0:T(8,128)(2,1)} %reshape.107.q_ref, bf16[16,2,512]{2,1,0:T(2,128)(2,1)} %kn_ref.1, ...), custom_call_target="tpu_custom_call" | custom-call | tf_op jit(solution)/shard_map/pallas_call | solution.py:160
  40.1 2.2 %copy.59 = bf16[4,8,64,128]{3,1,2,0:T(8,128)(2,1)} copy(bf16[4,8,64,128]{3,2,1,0:T(8,128)(2,1)} %bitcast.43) | data formatting | bytes 1048576
  42.3 1.1 constant_dynamic-slice_fusion.8
  43.4 1.3 collective-permute-start.3
  44.7 2.8 %collective-permute-start.4 = (bf16[32,2048]{1,0:T(8,128)(2,1)S(1)}, bf16[32,2048]{1,0:T(8,128)(2,1)S(1)}, u32[]{:S(2)}, u32[]{:S(2)}) collective-permute-start(bf16[32,2048]{1,0:T(8,128)(2,1)S(1)} %get-tuple-element.30), channel_id=1, source_target_pairs={{0,16},{8,24},{16,0},{24,8},{1,17},{9,25},{17,1},{25,9},{2,18},{10... | collective-permute-start | bytes 393224 | tf_op jit(solution)/shard_map/ppermute | solution.py:245
  47.5 1.6 collective-permute-done.3
  49.1 1.5 collective-permute-start.5
  50.5 2.3 %constant_dynamic-update-slice_fusion.7 = bf16[1024,2048]{1,0:T(8,128)(2,1)} fusion(bf16[256,2048]{1,0:T(8,128)(2,1)} %param.26), kind=kLoop, calls=%fused_computation.55 | loop fusion | bytes 2097152
  52.8 0.0 collective-permute-done.4
  52.8 0.3 collective-permute-done.5
  53.2 0.0 collective-permute-done.2
  53.2 2.4 %constant_dynamic-update-slice_fusion.6 = bf16[1024,2048]{1,0:T(8,128)(2,1)} fusion(bf16[1024,2048]{1,0:T(8,128)(2,1)} %constant_dynamic-update-slice_fusion.7, bf16[256,2048]{1,0:T(8,128)(2,1)} %collective-permute-done), kind=kLoop, calls=%fused_computation.54 | loop fusion | bytes 2097152
  55.6 2.3 %constant_dynamic-update-slice_fusion.5 = bf16[1024,2048]{1,0:T(8,128)(2,1)} fusion(bf16[1024,2048]{1,0:T(8,128)(2,1)} %constant_dynamic-update-slice_fusion.6, bf16[256,2048]{1,0:T(8,128)(2,1)} %collective-permute-done.1), kind=kLoop, calls=%fused_computation.53 | loop fusion | bytes 2097152
  57.9 2.3 %constant_dynamic-update-slice_fusion.4 = bf16[1024,2048]{1,0:T(8,128)(2,1)} fusion(bf16[1024,2048]{1,0:T(8,128)(2,1)} %constant_dynamic-update-slice_fusion.5, bf16[256,2048]{1,0:T(8,128)(2,1)} %collective-permute-done.2), kind=kLoop, calls=%fused_computation.52 | loop fusion | bytes 2097152 | tf_op jit(solution)/shard_map/concatenate | solution.py:252
  60.2 4.2 %collective-permute-start.6 = (bf16[1024,2048]{1,0:T(8,128)(2,1)}, bf16[1024,2048]{1,0:T(8,128)(2,1)}, u32[]{:S(2)}, u32[]{:S(2)}) collective-permute-start(bf16[1024,2048]{1,0:T(8,128)(2,1)} %constant_dynamic-update-slice_fusion.4), channel_id=1, source_target_pairs={{0,1},{1,0},{2,3},{3,2},{4,5},{5,4},{6,7},{7,6},{8,9},{9,8},{10,11... | collective-permute-start | bytes 12582920 | tf_op jit(solution)/shard_map/ppermute | solution.py:236
  64.4 0.8 copy.43
  65.2 0.7 eq.62
  65.8 0.9 convert_reduce_fusion
  66.8 0.7 broadcast_multiply_fusion
  67.5 0.9 constant_dynamic-update-slice_fusion
  68.4 0.1 constant_dynamic-slice_fusion.7
  68.5 3.0 %collective-permute-done.6 = bf16[1024,2048]{1,0:T(8,128)(2,1)} collective-permute-done((bf16[1024,2048]{1,0:T(8,128)(2,1)}, bf16[1024,2048]{1,0:T(8,128)(2,1)}, u32[]{:S(2)}, u32[]{:S(2)}) %collective-permute-start.6) | collective-permute-done | bytes 4194336 | tf_op jit(solution)/shard_map/ppermute | solution.py:236
  71.5 2.9 %fusion.27 = f32[128,2048]{1,0:T(8,128)S(1)} fusion(bf16[1024,2048]{1,0:T(8,128)(2,1)} %collective-permute-done.6, bf16[128,256]{1,0:T(8,128)(2,1)S(1)} %get-tuple-element.22, bf16[128,256]{1,0:T(8,128)(2,1)S(1)} %get-tuple-element.23, bf16[128,256]{1,0:T(8,128)(2,1)S(1)} %get-tuple-element.24, bf16[128,256]{1,0:T(8,128)(2,1)S(1)} %get-tuple-element.25), kind=kOutput, calls=%fused_computation.31 | convolution fusion | flops 537919488 | bytes 5505024 | tf_op jit(solution)/shard_map/dot_general | solution.py:269
  74.4 0.0 copy-start.1
  74.4 0.0 copy-start.4
  74.4 4.0 %fusion.46 = (bf16[128,2048]{1,0:T(8,128)(2,1)S(1)}, f32[128,2048]{1,0:T(8,128)}) fusion(f32[128,2048]{1,0:T(8,128)S(1)} %fusion.27, bf16[1024,2048]{1,0:T(8,128)(2,1)} %constant_dynamic-update-slice_fusion.4, bf16[128,256]{1,0:T(8,128)(2,1)S(1)} %get-tuple-element.26, bf16[128,256]{1,0:T(8,128)(2,1)S(1)} %get-tuple-element.27, ...), kind=kOutput, calls=%fused_computation.75 | convolution fusion | flops 538443776 | bytes 7077888 | tf_op jit(solution)/shard_map/dot_general | solution.py:268
  78.4 0.7 fusion.45
  79.2 2.5 %collective-permute-start.7 = (bf16[32,2048]{1,0:T(8,128)(2,1)}, bf16[32,2048]{1,0:T(8,128)(2,1)S(1)}, u32[]{:S(2)}, u32[]{:S(2)}) collective-permute-start(bf16[32,2048]{1,0:T(8,128)(2,1)} %get-tuple-element.18), channel_id=1, source_target_pairs={{0,24},{8,0},{16,8},{24,16},{1,25},{9,1},{17,9},{25,17},{2,26},{10... | collective-permute-start | bytes 393224 | tf_op jit(solution)/shard_map/ppermute | solution.py:245
  81.6 0.0 collective-permute-start.8
  81.6 0.6 collective-permute-start.9
  82.2 0.7 reshape.114
  83.0 0.1 reduce_sum.30
  83.0 0.1 copy.42
  83.1 0.2 compare_reduce_fusion
  83.4 3.8 %collective-permute-done.7 = bf16[32,2048]{1,0:T(8,128)(2,1)S(1)} collective-permute-done((bf16[32,2048]{1,0:T(8,128)(2,1)}, bf16[32,2048]{1,0:T(8,128)(2,1)S(1)}, u32[]{:S(2)}, u32[]{:S(2)}) %collective-permute-start.7) | collective-permute-done | bytes 131104 | tf_op jit(solution)/shard_map/ppermute | solution.py:245
  87.2 0.8 collective-permute-done.8
  87.9 3.2 %collective-permute-done.9 = bf16[32,2048]{1,0:T(8,128)(2,1)} collective-permute-done((bf16[32,2048]{1,0:T(8,128)(2,1)}, bf16[32,2048]{1,0:T(8,128)(2,1)}, u32[]{:S(2)}, u32[]{:S(2)}) %collective-permute-start.9) | collective-permute-done | bytes 131104 | tf_op jit(solution)/shard_map/ppermute | solution.py:245
  91.1 1.5 multiply_reduce_fusion
  92.6 0.8 convolution_convert_fusion
  93.4 0.0 slice-start.1
  93.4 1.6 copy.46
  95.1 37.0 %all_to_all.10 = bf16[128,4,2048]{2,1,0:T(4,128)(2,1)S(1)} all-to-all(bf16[128,4,2048]{2,1,0:T(4,128)(2,1)S(1)} %copy.46), channel_id=1, replica_groups=mesh['dp'=4,'y'=4,'x'=4,'c'=2] {'dp','y','x','c'}, dimensions={0} | all-to-all | bytes 4194304 | tf_op jit(solution)/shard_map/all_to_all | solution.py:297
  132.1 4.8 %fusion.2 = f32[128,1,4,1536]{3,0,2,1:T(8,128)S(1)} fusion(bf16[1,2048,1536]{2,1,0:T(8,128)(2,1)S(1)} %bitcast.49, bf16[128,4,2048]{2,1,0:T(4,128)(2,1)S(1)} %all_to_all.10), kind=kOutput, calls=%fused_computation.2 | convolution fusion | flops 3221225472 | bytes 11534336 | tf_op jit(solution)/shard_map/sjcd,jdf->sjcf/dot_general | solution.py:190
  136.9 1.8 fusion.7
  138.7 2.9 %copy.48 = bf16[128,4,2048]{2,1,0:T(4,128)(2,1)} copy(bf16[128,4,2048]{2,0,1:T(8,128)(2,1)S(1)} %fusion.7) | data formatting | bytes 4194304 | tf_op jit(solution)/shard_map/convert_element_type | solution.py:196
  141.7 5.6 %all-to-all-start.1 = ((bf16[128,4,2048]{2,1,0:T(4,128)(2,1)}), bf16[128,4,2048]{2,1,0:T(4,128)(2,1)}, u32[]{:S(2)}, u32[]{:S(2)}) async-start(bf16[128,4,2048]{2,1,0:T(4,128)(2,1)} %copy.48), calls=%async_computation.1 | async-start | bytes 4194304 | tf_op jit(solution)/shard_map/all_to_all | solution.py:309
  147.2 2.0 %reshape.108 = bf16[16,2,8192]{2,1,0:T(2,128)(2,1)} reshape(bf16[16,2,64,128]{3,2,1,0:T(8,128)(2,1)} %shard_map.167) | data formatting | bytes 1048576 | tf_op jit(solution)/shard_map/reshape | solution.py:185
  149.2 0.1 copy.44
  149.3 0.2 select_reduce_fusion
  149.5 0.8 copy.45
  150.3 27.2 %all-to-all-done.1 = bf16[128,4,2048]{2,1,0:T(4,128)(2,1)} async-done(((bf16[128,4,2048]{2,1,0:T(4,128)(2,1)}), bf16[128,4,2048]{2,1,0:T(4,128)(2,1)}, u32[]{:S(2)}, u32[]{:S(2)}) %all-to-all-start.1) | async-done | bytes 2097184 | tf_op jit(solution)/shard_map/all_to_all | solution.py:309
  177.5 4.8 %fusion.11 = bf16[32,2048]{1,0:T(8,128)(2,1)S(1)} fusion(f32[32,2048]{1,0:T(8,128)S(1)} %get-tuple-element.17, bf16[128,4,2048]{2,1,0:T(4,128)(2,1)} %all-to-all-done.1, f32[32,128,4]{0,2,1:T(4,128)} %bitcast.45), kind=kOutput, calls=%fused_computation.10 | convolution fusion | flops 402784256 | bytes 2555904 | tf_op jit(solution)/shard_map/tec,ecd->td/dot_general | solution.py:325
  182.4 0.8 reshape.113
  (21 shorter events, 0.1 us)
Async XLA Ops:
  0.6 136.2 %copy-start = (bf16[1,768,2048]{2,1,0:T(8,128)(2,1)S(1)}, bf16[1,768,2048]{2,1,0:T(8,128)(2,1)}, u32[]{:S(2)}) copy-start(bf16[1,768,2048]{2,1,0:T(8,128)(2,1)} %param.29) | copy-start | bytes 9437188
  0.6 52.5 %collective-permute-start = (bf16[256,2048]{1,0:T(8,128)(2,1)}, bf16[256,2048]{1,0:T(8,128)(2,1)}, u32[]{:S(2)}, u32[]{:S(2)}) collective-permute-start(bf16[256,2048]{1,0:T(8,128)(2,1)} %param.26), channel_id=1, source_target_pairs={{0,2},{2,4},{4,6},{6,0},{1,3},{3,5},{5,7},{7,1},{8,10},{10,12},{12... | collective-permute-start | bytes 3145736 | tf_op jit(solution)/shard_map/ppermute | solution.py:236
  2.8 50.4 %collective-permute-start.1 = (bf16[256,2048]{1,0:T(8,128)(2,1)}, bf16[256,2048]{1,0:T(8,128)(2,1)}, u32[]{:S(2)}, u32[]{:S(2)}) collective-permute-start(bf16[256,2048]{1,0:T(8,128)(2,1)} %param.26), channel_id=1, source_target_pairs={{0,4},{2,6},{4,0},{6,2},{1,5},{3,7},{5,1},{7,3},{8,12},{10,14},{12... | collective-permute-start | bytes 3145736 | tf_op jit(solution)/shard_map/ppermute | solution.py:236
  5.2 48.0 %collective-permute-start.2 = (bf16[256,2048]{1,0:T(8,128)(2,1)}, bf16[256,2048]{1,0:T(8,128)(2,1)}, u32[]{:S(2)}, u32[]{:S(2)}) collective-permute-start(bf16[256,2048]{1,0:T(8,128)(2,1)} %param.26), channel_id=1, source_target_pairs={{0,6},{2,0},{4,2},{6,4},{1,7},{3,1},{5,3},{7,5},{8,14},{10,8},{12,... | collective-permute-start | bytes 3145736 | tf_op jit(solution)/shard_map/ppermute | solution.py:236
  43.4 5.7 %collective-permute-start.3 = (bf16[32,2048]{1,0:T(8,128)(2,1)S(1)}, bf16[32,2048]{1,0:T(8,128)(2,1)S(1)}, u32[]{:S(2)}, u32[]{:S(2)}) collective-permute-start(bf16[32,2048]{1,0:T(8,128)(2,1)S(1)} %get-tuple-element.31), channel_id=1, source_target_pairs={{0,8},{8,16},{16,24},{24,0},{1,9},{9,17},{17,25},{25,1},{2,10},{10... | collective-permute-start | bytes 393224 | tf_op jit(solution)/shard_map/ppermute | solution.py:245
  44.7 8.2 %collective-permute-start.4 = (bf16[32,2048]{1,0:T(8,128)(2,1)S(1)}, bf16[32,2048]{1,0:T(8,128)(2,1)S(1)}, u32[]{:S(2)}, u32[]{:S(2)}) collective-permute-start(bf16[32,2048]{1,0:T(8,128)(2,1)S(1)} %get-tuple-element.30), channel_id=1, source_target_pairs={{0,16},{8,24},{16,0},{24,8},{1,17},{9,25},{17,1},{25,9},{2,18},{10... | collective-permute-start | bytes 393224 | tf_op jit(solution)/shard_map/ppermute | solution.py:245
  49.1 4.1 %collective-permute-start.5 = (bf16[32,2048]{1,0:T(8,128)(2,1)S(1)}, bf16[32,2048]{1,0:T(8,128)(2,1)S(1)}, u32[]{:S(2)}, u32[]{:S(2)}) collective-permute-start(bf16[32,2048]{1,0:T(8,128)(2,1)S(1)} %get-tuple-element.29), channel_id=1, source_target_pairs={{0,24},{8,0},{16,8},{24,16},{1,25},{9,1},{17,9},{25,17},{2,26},{10... | collective-permute-start | bytes 393224 | tf_op jit(solution)/shard_map/ppermute | solution.py:245
  53.2 7.0 %copy-start.3 = (bf16[32,2048]{1,0:T(8,128)(2,1)}, bf16[32,2048]{1,0:T(8,128)(2,1)S(1)}, u32[]{:S(2)}) copy-start(bf16[32,2048]{1,0:T(8,128)(2,1)S(1)} %collective-permute-done.5) | copy-start | bytes 393220
  60.2 11.3 %collective-permute-start.6 = (bf16[1024,2048]{1,0:T(8,128)(2,1)}, bf16[1024,2048]{1,0:T(8,128)(2,1)}, u32[]{:S(2)}, u32[]{:S(2)}) collective-permute-start(bf16[1024,2048]{1,0:T(8,128)(2,1)} %constant_dynamic-update-slice_fusion.4), channel_id=1, source_target_pairs={{0,1},{1,0},{2,3},{3,2},{4,5},{5,4},{6,7},{7,6},{8,9},{9,8},{10,11... | collective-permute-start | bytes 12582920 | tf_op jit(solution)/shard_map/ppermute | solution.py:236
  74.4 7.8 %copy-start.1 = (bf16[16,2,2048]{2,1,0:T(2,128)(2,1)S(1)}, bf16[16,2,2048]{2,1,0:T(2,128)(2,1)}, u32[]{:S(2)}) copy-start(bf16[16,2,2048]{2,1,0:T(2,128)(2,1)} %param.25) | copy-start | bytes 393220
  74.4 18.2 %copy-start.4 = (f32[2048]{0:T(1024)S(1)}, f32[2048]{0:T(1024)}, u32[]{:S(2)}) copy-start(f32[2048]{0:T(1024)} %param.27) | copy-start | bytes 24580
  79.2 8.0 %collective-permute-start.7 = (bf16[32,2048]{1,0:T(8,128)(2,1)}, bf16[32,2048]{1,0:T(8,128)(2,1)S(1)}, u32[]{:S(2)}, u32[]{:S(2)}) collective-permute-start(bf16[32,2048]{1,0:T(8,128)(2,1)} %get-tuple-element.18), channel_id=1, source_target_pairs={{0,24},{8,0},{16,8},{24,16},{1,25},{9,1},{17,9},{25,17},{2,26},{10... | collective-permute-start | bytes 393224 | tf_op jit(solution)/shard_map/ppermute | solution.py:245
  81.6 6.3 %collective-permute-start.8 = (bf16[32,2048]{1,0:T(8,128)(2,1)}, bf16[32,2048]{1,0:T(8,128)(2,1)}, u32[]{:S(2)}, u32[]{:S(2)}) collective-permute-start(bf16[32,2048]{1,0:T(8,128)(2,1)} %get-tuple-element.20), channel_id=1, source_target_pairs={{0,16},{8,24},{16,0},{24,8},{1,17},{9,25},{17,1},{25,9},{2,18},{10... | collective-permute-start | bytes 393224 | tf_op jit(solution)/shard_map/ppermute | solution.py:245
  81.6 9.5 %collective-permute-start.9 = (bf16[32,2048]{1,0:T(8,128)(2,1)}, bf16[32,2048]{1,0:T(8,128)(2,1)}, u32[]{:S(2)}, u32[]{:S(2)}) collective-permute-start(bf16[32,2048]{1,0:T(8,128)(2,1)} %get-tuple-element.19), channel_id=1, source_target_pairs={{0,8},{8,16},{16,24},{24,0},{1,9},{9,17},{17,25},{25,1},{2,10},{10... | collective-permute-start | bytes 393224 | tf_op jit(solution)/shard_map/ppermute | solution.py:245
  87.2 3.9 %copy-start.2 = (bf16[32,2048]{1,0:T(8,128)(2,1)}, bf16[32,2048]{1,0:T(8,128)(2,1)S(1)}, u32[]{:S(2)}) copy-start(bf16[32,2048]{1,0:T(8,128)(2,1)S(1)} %collective-permute-done.7) | copy-start | bytes 393220
  91.1 41.0 %slice-start = ((s8[6291456]{0:T(1024)(128)(4,1)}), s8[4194304]{0:T(1024)(128)(4,1)S(1)}, s32[]{:S(2)}) async-start(s8[6291456]{0:T(1024)(128)(4,1)} %bitcast.48), calls=%async_computation.2 | async-start | bytes 8388608
  93.4 38.7 %slice-start.1 = ((s8[6291456]{0:T(1024)(128)(4,1)}), s8[2097152]{0:T(1024)(128)(4,1)S(1)}, s32[]{:S(2)}) async-start(s8[6291456]{0:T(1024)(128)(4,1)} %bitcast.48), calls=%async_computation.3 | async-start | bytes 4194304
  141.7 7.5 %copy-start.5 = (f32[16,2,8]{0,2,1:T(8,128)S(1)}, f32[16,2,8]{0,2,1:T(8,128)}, u32[]{:S(2)}) copy-start(f32[16,2,8]{0,2,1:T(8,128)} %param.31) | copy-start | bytes 3076
  141.7 35.9 %all-to-all-start.1 = ((bf16[128,4,2048]{2,1,0:T(4,128)(2,1)}), bf16[128,4,2048]{2,1,0:T(4,128)(2,1)}, u32[]{:S(2)}, u32[]{:S(2)}) async-start(bf16[128,4,2048]{2,1,0:T(4,128)(2,1)} %copy.48), calls=%async_computation.1 | async-start | bytes 4194304 | tf_op jit(solution)/shard_map/all_to_all | solution.py:309

commit v14 on v11

--- a/solution.py
+++ b/solution.py
@@ -298,13 +298,11 @@
         ),
         axis=1,
     ).reshape(rows, experts_all, capacity)
+    high = gathering.astype(jnp.bfloat16)
+    low = (gathering - high.astype(jnp.float32)).astype(jnp.bfloat16)
     blended = jnp.einsum(
-        "tec,ecd->td",
-        gathering,
-        returned.astype(jnp.float32),
-        precision=lax.Precision.HIGHEST,
-        preferred_element_type=jnp.float32,
-    )
+        "tec,ecd->td", high, returned, preferred_element_type=jnp.float32
+    ) + jnp.einsum("tec,ecd->td", low, returned, preferred_element_type=jnp.float32)
     layer_out = (mixed + blended).astype(jnp.bfloat16).reshape(requests, steps, width)
     return (attended, layer_out)
 

time: 181 us -> 186 us (1.028)
  matrix products: 18.2 us -> 21.9 us
  local copies, waits for them, and re-layouts: 19.8 us -> 21.8 us
    dot_general x1 -> x2, matrix products: 4.82 us -> 8.52 us  [the longest x1 4.6 us: shards(): jnp.einsum('tec,ecd->td', low, returned, preferred_element_type=jnp.float32)]
where the time goes in v14:
time: 186 us; the launch traced here: 185 us
  waiting for transfers between devices  45.2 us (24%)
  blocking collectives  36.4 us (20%)
  Pallas kernels  27.3 us (15%)
  matrix products  21.9 us (12%)
  local copies, waits for them, and re-layouts  21.8 us (12%)
  starting transfers between devices  15 us (8%)
  between operations  14.2 us (8%)
  other arithmetic  3.55 us (2%)
    all_to_all x1, blocking collectives, shards(): lax.all_to_all(outgoing, ('dp', 'y', 'x', 'c'), split_axis=0, concat_axis...  36.4 us
    pallas_call x1, Pallas kernels, decode_attention(): pl.pallas_call(kernel, out_shape=jax.ShapeDtypeStruct((requests, steps, h...  27.3 us
    all_to_all x1, waiting for transfers between devices, shards(): lax.all_to_all(answer.reshape(sources * experts_local, depth, width), ('d...  26.2 us
    all_gather x1, waiting for transfers between devices, shards(): gathered = lax.all_gather(o_weight, ('x', 'c'), axis=0, tiled=True)  9.38 us
    ppermute x6, starting transfers between devices, shifted(): lax.ppermute(value, 'y', [(j, (j + shift) % lines) for j in range(lines)])  9.36 us
    ppermute x6, waiting for transfers between devices, shifted(): lax.ppermute(value, 'y', [(j, (j + shift) % lines) for j in range(lines)])  8.94 us
    dot_general x1, matrix products, shards(): jnp.dot(jnp.concatenate(pieces, axis=0), gathered, preferred_element_type...  5.95 us
    all_to_all x1, starting transfers between devices, shards(): lax.all_to_all(answer.reshape(sources * experts_local, depth, width), ('d...  5.59 us
  transfers between devices with their start and end apart: 8, of which 6 were waited for; matrix products, arithmetic and copies ran while one was open for 9% of the time, Pallas kernels for 15%

profile of v14, /device:TPU:1, one launch (start us, length us, event | category | flops | bytes accessed | tf_op | source)
XLA Modules:
  0.0 185.2 jit_solution(17150244173077086958)
XLA Ops:
  7.2 0.0 copy-start
  7.2 0.0 copy-start.7
  7.2 0.0 copy-start.8
  7.2 0.0 copy-start.9
  7.2 0.0 all-gather.2.cloned.1.call-start
  7.3 0.7 all-gather.2.cloned.1.call-update
  8.0 2.4 %reshape.107.q_ref = bf16[16,2,64,128]{3,2,1,0:T(8,128)(2,1)} reshape(bf16[16,2,8192]{2,1,0:T(2,128)(2,1)} %param.16) | data formatting | bytes 1048576 | tf_op jit(solution)/shard_map/reshape | solution.py:179
  10.4 0.0 copy-done.7
  10.4 0.1 copy.56
  10.5 0.6 reshape.104.flag_ref
  11.1 0.0 copy-done.8
  11.1 0.1 copy.57
  11.2 0.6 reshape.105.share_ref
  11.8 0.0 copy-done.9
  11.8 0.1 copy.58
  11.9 0.6 reshape.106.weight_ref
  12.5 27.3 %shard_map.167 = bf16[16,2,64,128]{3,2,1,0:T(8,128)(2,1)} custom-call(s32[16]{0:T(128)} %len_ref.1, s32[128]{0:T(128)} %reshape.104.flag_ref, f32[128]{0:T(128)} %reshape.105.share_ref, f32[64]{0:T(128)} %reshape.106.weight_ref, bf16[16,2,64,128]{3,2,1,0:T(8,128)(2,1)} %reshape.107.q_ref, bf16[16,2,512]{2,1,0:T(2,128)(2,1)} %kn_ref.1, ...), custom_call_target="tpu_custom_call" | custom-call | tf_op jit(solution)/shard_map/pallas_call | solution.py:160
  39.8 0.0 copy-start.3
  39.8 2.2 %copy.78 = bf16[4,8,64,128]{3,1,2,0:T(8,128)(2,1)} copy(bf16[4,8,64,128]{3,2,1,0:T(8,128)(2,1)} %bitcast.46) | data formatting | bytes 1048576
  42.0 1.8 constant_dynamic-slice_fusion.3
  43.8 2.0 %collective-permute-start = (bf16[32,2048]{1,0:T(8,128)(2,1)}, bf16[32,2048]{1,0:T(8,128)(2,1)}, u32[]{:S(2)}, u32[]{:S(2)}) collective-permute-start(bf16[32,2048]{1,0:T(8,128)(2,1)} %get-tuple-element.10), channel_id=1, source_target_pairs={{0,8},{8,16},{16,24},{24,0},{1,9},{9,17},{17,25},{25,1},{2,10},{10... | collective-permute-start | bytes 393224 | tf_op jit(solution)/shard_map/ppermute | solution.py:238
  45.8 2.6 %collective-permute-start.1 = (bf16[32,2048]{1,0:T(8,128)(2,1)S(1)}, bf16[32,2048]{1,0:T(8,128)(2,1)}, u32[]{:S(2)}, u32[]{:S(2)}) collective-permute-start(bf16[32,2048]{1,0:T(8,128)(2,1)S(1)} %get-tuple-element.9), channel_id=1, source_target_pairs={{0,16},{8,24},{16,0},{24,8},{1,17},{9,25},{17,1},{25,9},{2,18},{10... | collective-permute-start | bytes 393224 | tf_op jit(solution)/shard_map/ppermute | solution.py:238
  48.4 1.1 collective-permute-start.2
  49.5 0.6 broadcast_multiply_fusion
  50.1 0.8 copy.60
  50.9 0.7 eq.53
  51.6 0.9 convert_reduce_fusion
  52.5 0.0 collective-permute-done
  52.5 1.2 collective-permute-done.1
  53.8 0.0 collective-permute-done.2
  53.8 9.4 %all-gather.2.cloned.1.call-done = bf16[2048,2048]{1,0:T(8,128)(2,1)} async-done(((bf16[256,2048]{1,0:T(8,128)(2,1)}), bf16[2048,2048]{1,0:T(8,128)(2,1)}) %all-gather.2.cloned.1.call-update) | async-done | bytes 8388624 | tf_op jit(solution)/shard_map/all_gather | solution.py:231
  63.2 6.0 %fusion.41 = (bf16[128,2048]{1,0:T(8,128)(2,1)S(1)}, f32[128,2048]{1,0:T(8,128)}) fusion(bf16[2048,2048]{1,0:T(8,128)(2,1)} %all-gather.2.cloned.1.call-done, bf16[32,2048]{1,0:T(8,128)(2,1)} %collective-permute-done.2, bf16[32,2048]{1,0:T(8,128)(2,1)} %collective-permute-done.1, bf16[32,2048]{1,0:T(8,128)(2,1)} %collective-permute-done, ...), kind=kOutput, calls=%fused_computation.55 | convolution fusion | flops 1076101120 | bytes 10485760 | tf_op jit(solution)/shard_map/dot_general | solution.py:244
  69.1 0.7 fusion.40
  69.9 2.4 %collective-permute-start.3 = (bf16[32,2048]{1,0:T(8,128)(2,1)}, bf16[32,2048]{1,0:T(8,128)(2,1)S(1)}, u32[]{:S(2)}, u32[]{:S(2)}) collective-permute-start(bf16[32,2048]{1,0:T(8,128)(2,1)} %get-tuple-element.4), channel_id=1, source_target_pairs={{0,24},{8,0},{16,8},{24,16},{1,25},{9,1},{17,9},{25,17},{2,26},{10... | collective-permute-start | bytes 393224 | tf_op jit(solution)/shard_map/ppermute | solution.py:238
  72.3 0.5 collective-permute-start.4
  72.8 0.7 collective-permute-start.5
  73.5 0.7 reshape.114
  74.2 0.1 reduce_sum.30
  74.3 0.0 copy-done.4
  74.3 0.1 copy.59
  74.4 0.2 compare_reduce_fusion
  74.7 3.3 %collective-permute-done.3 = bf16[32,2048]{1,0:T(8,128)(2,1)S(1)} collective-permute-done((bf16[32,2048]{1,0:T(8,128)(2,1)}, bf16[32,2048]{1,0:T(8,128)(2,1)S(1)}, u32[]{:S(2)}, u32[]{:S(2)}) %collective-permute-start.3) | collective-permute-done | bytes 131104 | tf_op jit(solution)/shard_map/ppermute | solution.py:238
  77.9 0.7 collective-permute-done.4
  78.7 3.7 %collective-permute-done.5 = bf16[32,2048]{1,0:T(8,128)(2,1)} collective-permute-done((bf16[32,2048]{1,0:T(8,128)(2,1)}, bf16[32,2048]{1,0:T(8,128)(2,1)}, u32[]{:S(2)}, u32[]{:S(2)}) %collective-permute-start.5) | collective-permute-done | bytes 131104 | tf_op jit(solution)/shard_map/ppermute | solution.py:238
  82.4 0.0 copy-done.2
  82.4 1.5 multiply_reduce_fusion
  83.9 0.8 convolution_convert_fusion
  84.7 0.0 slice-start.1
  84.7 1.6 copy.64
  86.3 36.4 %all_to_all.10 = bf16[128,4,2048]{2,1,0:T(4,128)(2,1)S(1)} all-to-all(bf16[128,4,2048]{2,1,0:T(4,128)(2,1)S(1)} %copy.64), channel_id=1, replica_groups=mesh['dp'=4,'y'=4,'x'=4,'c'=2] {'dp','y','x','c'}, dimensions={0} | all-to-all | bytes 4194304 | tf_op jit(solution)/shard_map/all_to_all | solution.py:273
  122.7 0.0 slice-done.1
  122.7 4.8 %fusion.2 = f32[128,1,4,1536]{3,0,2,1:T(8,128)S(1)} fusion(bf16[1,2048,1536]{2,1,0:T(8,128)(2,1)S(1)} %bitcast.52, bf16[128,4,2048]{2,1,0:T(4,128)(2,1)S(1)} %all_to_all.10), kind=kOutput, calls=%fused_computation.2 | convolution fusion | flops 3221225472 | bytes 11534336 | tf_op jit(solution)/shard_map/sjcd,jdf->sjcf/dot_general | solution.py:190
  127.5 1.8 fusion.7
  129.4 2.9 %copy.66 = bf16[128,4,2048]{2,1,0:T(4,128)(2,1)} copy(bf16[128,4,2048]{2,0,1:T(8,128)(2,1)S(1)} %fusion.7) | data formatting | bytes 4194304 | tf_op jit(solution)/shard_map/convert_element_type | solution.py:196
  132.3 5.6 %all-to-all-start.1 = ((bf16[128,4,2048]{2,1,0:T(4,128)(2,1)}), bf16[128,4,2048]{2,1,0:T(4,128)(2,1)}, u32[]{:S(2)}, u32[]{:S(2)}) async-start(bf16[128,4,2048]{2,1,0:T(4,128)(2,1)} %copy.66), calls=%async_computation.1 | async-start | bytes 4194304 | tf_op jit(solution)/shard_map/all_to_all | solution.py:285
  137.9 2.0 %reshape.108 = bf16[16,2,8192]{2,1,0:T(2,128)(2,1)} reshape(bf16[16,2,64,128]{3,2,1,0:T(8,128)(2,1)} %shard_map.167) | data formatting | bytes 1048576 | tf_op jit(solution)/shard_map/reshape | solution.py:185
  139.9 0.1 copy.61
  140.0 0.2 select_reduce_fusion
  140.2 0.8 copy.62
  141.0 1.0 copy.63
  142.1 26.2 %all-to-all-done.1 = bf16[128,4,2048]{2,1,0:T(4,128)(2,1)} async-done(((bf16[128,4,2048]{2,1,0:T(4,128)(2,1)}), bf16[128,4,2048]{2,1,0:T(4,128)(2,1)}, u32[]{:S(2)}, u32[]{:S(2)}) %all-to-all-start.1) | async-done | bytes 2097184 | tf_op jit(solution)/shard_map/all_to_all | solution.py:285
  168.2 3.9 %convolution_bitcast_fusion.1 = f32[32,2048]{1,0:T(8,128)S(1)} fusion(bf16[128,4,2048]{2,1,0:T(4,128)(2,1)} %all-to-all-done.1, f32[32,128,4]{1,0,2:T(8,128)S(1)} %copy.63), kind=kOutput, calls=%fused_computation.10 | convolution fusion | flops 67125248 | bytes 2424832 | tf_op jit(solution)/shard_map/tec,ecd->td/dot_general | solution.py:303
  172.1 4.6 %fusion.12 = bf16[32,2048]{1,0:T(8,128)(2,1)} fusion(f32[32,2048]{1,0:T(8,128)S(1)} %get-tuple-element.3, f32[32,2048]{1,0:T(8,128)S(1)} %convolution_bitcast_fusion.1, bf16[128,4,2048]{2,1,0:T(4,128)(2,1)} %all-to-all-done.1, f32[32,128,4]{1,0,2:T(8,128)S(1)} %copy.63), kind=kOutput, calls=%fused_computation.11 | convolution fusion | flops 67371008 | bytes 2818048 | tf_op jit(solution)/shard_map/tec,ecd->td/dot_general | solution.py:305
  176.7 1.7 reshape.113
  (16 shorter events, 0.0 us)
Async XLA Ops:
  7.2 120.4 %copy-start = (bf16[1,768,2048]{2,1,0:T(8,128)(2,1)S(1)}, bf16[1,768,2048]{2,1,0:T(8,128)(2,1)}, u32[]{:S(2)}) copy-start(bf16[1,768,2048]{2,1,0:T(8,128)(2,1)} %param.29) | copy-start | bytes 9437188
  7.2 3.2 %copy-start.7 = (s32[16,2,4]{0,2,1:T(4,128)S(1)}, s32[16,2,4]{0,2,1:T(4,128)}, u32[]{:S(2)}) copy-start(s32[16,2,4]{0,2,1:T(4,128)} %param.20) | copy-start | bytes 1540
  7.2 3.9 %copy-start.8 = (f32[16,2,4]{0,2,1:T(4,128)S(1)}, f32[16,2,4]{0,2,1:T(4,128)}, u32[]{:S(2)}) copy-start(f32[16,2,4]{0,2,1:T(4,128)} %param.19) | copy-start | bytes 1540
  7.2 4.6 %copy-start.9 = (f32[16,4]{0,1:T(4,128)S(1)}, f32[16,4]{0,1:T(4,128)}, u32[]{:S(2)}) copy-start(f32[16,4]{0,1:T(4,128)} %param.23) | copy-start | bytes 772
  7.2 56.0 %all-gather.2.cloned.1.call-start = ((), (), s32[]{:S(2)}) async-start(), calls=%async_computation.2 | async-start | bytes 9437184 | tf_op jit(solution)/shard_map/all_gather | solution.py:231
  39.8 9.7 %copy-start.3 = (s32[16,2,8]{0,2,1:T(8,128)S(1)}, s32[16,2,8]{0,2,1:T(8,128)}, u32[]{:S(2)}) copy-start(s32[16,2,8]{0,2,1:T(8,128)} %param.30) | copy-start | bytes 3076
  43.8 8.7 %collective-permute-start = (bf16[32,2048]{1,0:T(8,128)(2,1)}, bf16[32,2048]{1,0:T(8,128)(2,1)}, u32[]{:S(2)}, u32[]{:S(2)}) collective-permute-start(bf16[32,2048]{1,0:T(8,128)(2,1)} %get-tuple-element.10), channel_id=1, source_target_pairs={{0,8},{8,16},{16,24},{24,0},{1,9},{9,17},{17,25},{25,1},{2,10},{10... | collective-permute-start | bytes 393224 | tf_op jit(solution)/shard_map/ppermute | solution.py:238
  45.8 8.0 %collective-permute-start.1 = (bf16[32,2048]{1,0:T(8,128)(2,1)S(1)}, bf16[32,2048]{1,0:T(8,128)(2,1)}, u32[]{:S(2)}, u32[]{:S(2)}) collective-permute-start(bf16[32,2048]{1,0:T(8,128)(2,1)S(1)} %get-tuple-element.9), channel_id=1, source_target_pairs={{0,16},{8,24},{16,0},{24,8},{1,17},{9,25},{17,1},{25,9},{2,18},{10... | collective-permute-start | bytes 393224 | tf_op jit(solution)/shard_map/ppermute | solution.py:238
  48.4 5.4 %collective-permute-start.2 = (bf16[32,2048]{1,0:T(8,128)(2,1)S(1)}, bf16[32,2048]{1,0:T(8,128)(2,1)}, u32[]{:S(2)}, u32[]{:S(2)}) collective-permute-start(bf16[32,2048]{1,0:T(8,128)(2,1)S(1)} %get-tuple-element.8), channel_id=1, source_target_pairs={{0,24},{8,0},{16,8},{24,16},{1,25},{9,1},{17,9},{25,17},{2,26},{10... | collective-permute-start | bytes 393224 | tf_op jit(solution)/shard_map/ppermute | solution.py:238
  63.2 10.3 %copy-start.1 = (bf16[16,2,2048]{2,1,0:T(2,128)(2,1)S(1)}, bf16[16,2,2048]{2,1,0:T(2,128)(2,1)}, u32[]{:S(2)}) copy-start(bf16[16,2,2048]{2,1,0:T(2,128)(2,1)} %param.25) | copy-start | bytes 393220
  63.2 11.2 %copy-start.4 = (s32[16,2,8]{0,2,1:T(8,128)S(1)}, s32[16,2,8]{0,2,1:T(8,128)}, u32[]{:S(2)}) copy-start(s32[16,2,8]{0,2,1:T(8,128)} %broadcast_multiply_fusion) | copy-start | bytes 3076
  69.1 14.8 %copy-start.5 = (f32[2048]{0:T(1024)S(1)}, f32[2048]{0:T(1024)}, u32[]{:S(2)}) copy-start(f32[2048]{0:T(1024)} %param.27) | copy-start | bytes 24580
  69.9 8.1 %collective-permute-start.3 = (bf16[32,2048]{1,0:T(8,128)(2,1)}, bf16[32,2048]{1,0:T(8,128)(2,1)S(1)}, u32[]{:S(2)}, u32[]{:S(2)}) collective-permute-start(bf16[32,2048]{1,0:T(8,128)(2,1)} %get-tuple-element.4), channel_id=1, source_target_pairs={{0,24},{8,0},{16,8},{24,16},{1,25},{9,1},{17,9},{25,17},{2,26},{10... | collective-permute-start | bytes 393224 | tf_op jit(solution)/shard_map/ppermute | solution.py:238
  72.3 6.4 %collective-permute-start.4 = (bf16[32,2048]{1,0:T(8,128)(2,1)}, bf16[32,2048]{1,0:T(8,128)(2,1)}, u32[]{:S(2)}, u32[]{:S(2)}) collective-permute-start(bf16[32,2048]{1,0:T(8,128)(2,1)} %get-tuple-element.6), channel_id=1, source_target_pairs={{0,16},{8,24},{16,0},{24,8},{1,17},{9,25},{17,1},{25,9},{2,18},{10... | collective-permute-start | bytes 393224 | tf_op jit(solution)/shard_map/ppermute | solution.py:238
  72.8 9.5 %collective-permute-start.5 = (bf16[32,2048]{1,0:T(8,128)(2,1)}, bf16[32,2048]{1,0:T(8,128)(2,1)}, u32[]{:S(2)}, u32[]{:S(2)}) collective-permute-start(bf16[32,2048]{1,0:T(8,128)(2,1)} %get-tuple-element.5), channel_id=1, source_target_pairs={{0,8},{8,16},{16,24},{24,0},{1,9},{9,17},{17,25},{25,1},{2,10},{10... | collective-permute-start | bytes 393224 | tf_op jit(solution)/shard_map/ppermute | solution.py:238
  77.9 4.4 %copy-start.2 = (bf16[32,2048]{1,0:T(8,128)(2,1)}, bf16[32,2048]{1,0:T(8,128)(2,1)S(1)}, u32[]{:S(2)}) copy-start(bf16[32,2048]{1,0:T(8,128)(2,1)S(1)} %collective-permute-done.3) | copy-start | bytes 393220
  82.4 40.4 %slice-start = ((s8[6291456]{0:T(1024)(128)(4,1)}), s8[4194304]{0:T(1024)(128)(4,1)S(1)}, s32[]{:S(2)}) async-start(s8[6291456]{0:T(1024)(128)(4,1)} %bitcast.51), calls=%async_computation.3 | async-start | bytes 8388608
  84.7 38.0 %slice-start.1 = ((s8[6291456]{0:T(1024)(128)(4,1)}), s8[2097152]{0:T(1024)(128)(4,1)S(1)}, s32[]{:S(2)}) async-start(s8[6291456]{0:T(1024)(128)(4,1)} %bitcast.51), calls=%async_computation.4 | async-start | bytes 4194304
  132.3 7.6 %copy-start.6 = (f32[16,2,8]{0,2,1:T(8,128)S(1)}, f32[16,2,8]{0,2,1:T(8,128)}, u32[]{:S(2)}) copy-start(f32[16,2,8]{0,2,1:T(8,128)} %param.31) | copy-start | bytes 3076
  132.3 35.9 %all-to-all-start.1 = ((bf16[128,4,2048]{2,1,0:T(4,128)(2,1)}), bf16[128,4,2048]{2,1,0:T(4,128)(2,1)}, u32[]{:S(2)}, u32[]{:S(2)}) async-start(bf16[128,4,2048]{2,1,0:T(4,128)(2,1)} %copy.66), calls=%async_computation.1 | async-start | bytes 4194304 | tf_op jit(solution)/shard_map/all_to_all | solution.py:285
Sparse Core Ops, SparseCore 0:
  9.8 53.3 all-gather.1
